TPU v7x, 256 devices: a whole 4x4x8 slice. The times are simulated.
256 devices in a mesh: coil: 4 (over x_hi, core), slab: 64 (over z, y, x_lo).
Axes of the slice: x: 4 (x_hi: 2, x_lo: 2; x = x_hi * 2 + x_lo), y: 4, z: 8, core: 2. Of those that a mesh axis runs over, the one named last changes fastest.
Arguments:
- partial_time: bfloat16 [4, 4, 128, 512, 1024], P('coil', None, 'slab'), may hold values from -6 to 6
- brain_mask: int32 [512], P(('coil', 'slab')), may hold values from 0 to 1, as said below
- rank_limit: int32 [512], P(('coil', 'slab')), may hold values from 2 to 16
- start_basis: float32 [16, 1024], replicated, may hold values from -6 to 6
Outputs:
- denoised: bfloat16 [512, 512, 1024], P(('coil', 'slab'))
Inputs may be any that keep to these rules, and one draw needn't show every extreme that they name: `brain_mask`: A patch p can be 1 only if its slab position (p // 2) mod 64 lies in the middle half, from 16 up to 47.
All inputs are finite; a program needn't handle non-finite values.
Results may differ from a plain program's by a relative error of at most 0.023.
Values may be sent and summed in bfloat16 or wider, within the bound.
No kernel may reach another device: no remote copies, remote signals or barrier semaphores. Data moves between devices by JAX's collectives and lax.ppermute only.
A program may use at most 128 MiB of HBM per device.

v0:
```python
import math

import jax
import jax.numpy as jnp
from jax import lax
from jax.sharding import PartitionSpec as P

ITERS = 4


def spectral_table(length):
    points = jnp.arange(length, dtype=jnp.int32)
    phase_index = points[:, None] * points[None, :] % length
    angles = phase_index.astype(jnp.float32) * (2.0 * math.pi / length)
    cosine = jnp.cos(angles) / math.sqrt(length)
    sine_part = jnp.sin(angles) / math.sqrt(length)
    upper_rows = jnp.concatenate([cosine, -sine_part], axis=1)
    lower_rows = jnp.concatenate([sine_part, cosine], axis=1)
    return jnp.concatenate([upper_rows, lower_rows], axis=0).astype(jnp.bfloat16)


def denoise_patch(patch_block, rank_cap, transform, start_basis):
    spectra = jnp.dot(patch_block, transform, preferred_element_type=jnp.float32)
    spectral_gram = lax.dot_general(
        spectra, spectra, (((0,), (0,)), ((), ())), precision=lax.Precision.HIGHEST
    )
    subspace = start_basis
    for sweep_index in range(ITERS):
        product_rows = jnp.dot(subspace, spectral_gram, precision=lax.Precision.HIGHEST)
        inner_gram = jnp.dot(product_rows, product_rows.T, precision=lax.Precision.HIGHEST)
        factor = jnp.linalg.cholesky(inner_gram)
        subspace = jax.scipy.linalg.solve_triangular(factor, product_rows, lower=True)
    keep_rows = jnp.arange(subspace.shape[0], dtype=jnp.int32) < rank_cap
    truncated = jnp.where(keep_rows[:, None], subspace, jnp.zeros_like(subspace))
    coefficients = lax.dot_general(
        truncated, spectra, (((1,), (1,)), ((), ())), precision=lax.Precision.HIGHEST
    )
    result = lax.dot_general(
        coefficients, truncated, (((0,), (0,)), ((), ())), precision=lax.Precision.HIGHEST
    )
    return result.astype(jnp.bfloat16)


def run_patches(patches, flags, ranks, transform, start_basis):
    work_count = jnp.sum(flags.astype(jnp.int32))
    work_order = jnp.argsort(1 - flags.astype(jnp.int32), stable=True)
    results = jnp.zeros(patches.shape, jnp.bfloat16)

    def process(position, current):
        slot_index = work_order[position]
        patch_block = lax.dynamic_index_in_dim(patches, slot_index, 0, keepdims=False)
        rank_cap = lax.dynamic_index_in_dim(ranks, slot_index, 0, keepdims=False)
        cleaned = denoise_patch(patch_block, rank_cap, transform, start_basis)
        return lax.dynamic_update_index_in_dim(current, cleaned, slot_index, 0)

    return lax.fori_loop(0, work_count, process, results)


def body(partial_time, brain_mask, rank_limit, start_basis):
    summed = lax.psum_scatter(
        partial_time.astype(jnp.float32).astype(jnp.bfloat16),
        "coil",
        scatter_dimension=1,
        tiled=True,
    )
    patches = summed.reshape((-1, summed.shape[-2], summed.shape[-1]))
    transform = spectral_table(patches.shape[-1] // 2)
    denoised = run_patches(patches, brain_mask > 0, rank_limit, transform, start_basis)
    return denoised


def solution(mesh):
    return jax.shard_map(
        body,
        mesh=mesh,
        in_specs=(
            P("coil", None, "slab", None, None),
            P(("coil", "slab")),
            P(("coil", "slab")),
            P(),
        ),
        out_specs=P(("coil", "slab"), None, None),
        check_vma=False,
    )
```

profile of v0, /device:TPU:64, one launch (start us, length us, event | category | flops | bytes accessed | tf_op | source)
XLA Modules:
  0.0 211.4 jit_solution(12678545297770424111)
XLA Ops:
  6.5 0.7 reduce-scatter.2.cloned.1.call-update
  8.5 4.0 %fusion.34 = bf16[512,512]{1,0:T(8,128)(2,1)S(1)} fusion(), kind=kLoop, calls=%fused_computation.59 | loop fusion | flops 4194304 | bytes 524288 | tf_op jit(solution)/shard_map/convert.2
  12.5 4.4 %negate_convert_fusion = (bf16[512,512]{1,0:T(8,128)(2,1)S(1)}, bf16[512,512]{1,0:T(8,128)(2,1)S(1)}) fusion(), kind=kLoop, calls=%fused_computation.53 | loop fusion | flops 4980736 | bytes 1048576 | tf_op jit(solution)/shard_map/convert.5
  16.9 1.7 maximum_maximum_fusion
  18.6 77.3 %reduce-scatter.2.cloned.1.call-done = bf16[1,1,2,512,1024]{4,3,2,1,0:T(8,128)(2,1)} async-done(((bf16[1,4,2,512,1024]{4,3,2,1,0:T(8,128)(2,1)}), bf16[1,1,2,512,1024]{4,3,2,1,0:T(8,128)(2,1)}) %reduce-scatter.2.cloned.1.call-update) | async-done | bytes 2097168 | tf_op jit(solution)/shard_map/reduce_scatter | solution.py:60
  95.9 1.6 broadcast_in_dim.19
  97.5 107.1 %while.10 = (s32[]{:T(128)}, bf16[2,512,1024]{2,1,0:T(8,128)(2,1)}, s32[]{:T(128)}, s32[2]{0:T(128)S(1)}, s32[2]{0:T(128)S(1)}, /*index=5*/bf16[2,512,1024]{2,1,...) while((s32[]{:T(128)}, bf16[2,512,1024]{2,1,0:T(8,128)(2,1)}, ...), condition=%wide.region_6.9_spmd, body=%wide.region_3.8_spmd.sunk | while | flops 8548540416 | bytes 49783572 | solution.py:56
  98.1 0.7 dynamic_slice.19
  100.8 3.2 %fusion.163 = f32[512,1024]{1,0:T(8,128)S(1)} fusion(bf16[1024,1024]{1,0:T(8,128)(2,1)} %get-tuple-element.151, bf16[2,512,1024]{2,1,0:T(8,128)(2,1)} %get-tuple-element.150, s32[]{:T(128)S(6)} %select_n.76), kind=kOutput, calls=%fused_computation.4.clone.1 | convolution fusion | flops 1073741824 | bytes 5242884 | tf_op jit(solution)/shard_map/while/body/dot_general | solution.py:23
  104.0 7.3 %fusion.164 = f32[1024,1024]{1,0:T(8,128)S(1)} fusion(f32[512,1024]{1,0:T(8,128)S(1)} %fusion.163), kind=kOutput, calls=%fused_computation.63.clone.1 | convolution fusion | flops 6442450944 | bytes 6291456 | tf_op jit(solution)/shard_map/while/body/dot_general | solution.py:24
  111.3 2.3 %fusion.165 = f32[1024,16]{0,1:T(8,128)S(1)} fusion(f32[1024,1024]{1,0:T(8,128)S(1)} %fusion.164, f32[16,1024]{1,0:T(8,128)S(1)} %get-tuple-element.152), kind=kOutput, calls=%fused_computation.64.clone.1 | convolution fusion | flops 201326592 | bytes 4325376 | tf_op jit(solution)/shard_map/while/body/dot_general | solution.py:29
  113.8 1.5 cholesky.280
  116.6 1.2 custom-call.16
  118.1 4.3 %fusion.171 = f32[16,1024]{1,0:T(8,128)S(1)} fusion(f32[16,1024]{1,0:T(8,128)S(1)} %fusion.170, f32[1024,1024]{1,0:T(8,128)} %copy-done), kind=kOutput, calls=%fused_computation.66.clone.1 | convolution fusion | flops 201326592 | bytes 4325376 | tf_op jit(solution)/shard_map/while/body/dot_general | solution.py:29
  122.6 1.5 cholesky.281
  125.4 1.2 custom-call.17
  126.9 4.3 %fusion.177 = f32[16,1024]{1,0:T(8,128)S(1)} fusion(f32[16,1024]{1,0:T(8,128)S(1)} %fusion.176, f32[1024,1024]{1,0:T(8,128)} %copy-done), kind=kOutput, calls=%fused_computation.68.clone.1 | convolution fusion | flops 201326592 | bytes 4325376 | tf_op jit(solution)/shard_map/while/body/dot_general | solution.py:29
  131.4 1.5 cholesky.282
  134.2 1.2 custom-call.18
  135.7 4.3 %fusion.183 = f32[16,1024]{1,0:T(8,128)S(1)} fusion(f32[16,1024]{1,0:T(8,128)S(1)} %fusion.182, f32[1024,1024]{1,0:T(8,128)} %copy-done), kind=kOutput, calls=%fused_computation.70.clone.1 | convolution fusion | flops 201326592 | bytes 4325376 | tf_op jit(solution)/shard_map/while/body/dot_general | solution.py:29
  140.2 1.5 cholesky.283
  141.8 0.7 compare_reduce_fusion.11
  142.5 0.7 fusion.186
  143.2 1.2 custom-call.19
  144.4 0.7 dynamic_slice.20
  145.1 0.7 iota_compare_fusion.4
  146.1 1.8 fusion.187
  147.9 2.8 %fusion.188 = bf16[2,512,1024]{2,1,0:T(8,128)(2,1)} fusion(bf16[2,512,1024]{2,1,0:T(8,128)(2,1)} %get-tuple-element.135, s32[]{:T(128)S(6)} %select_n.76, f32[16,512]{1,0:T(8,128)S(1)} %fusion.187, f32[16,1024]{1,0:T(8,128)S(1)} %convolution_select_fusion.2), kind=kOutput, calls=%fused_computation.2.clone.1 | convolution fusion | flops 101187584 | bytes 1146884 | tf_op jit(solution)/shard_map/while/body/dot_general | solution.py:38
  154.0 3.2 %fusion.163 = f32[512,1024]{1,0:T(8,128)S(1)} fusion(bf16[1024,1024]{1,0:T(8,128)(2,1)} %get-tuple-element.151, bf16[2,512,1024]{2,1,0:T(8,128)(2,1)} %get-tuple-element.150, s32[]{:T(128)S(6)} %select_n.76), kind=kOutput, calls=%fused_computation.4.clone.1 | convolution fusion | flops 1073741824 | bytes 5242884 | tf_op jit(solution)/shard_map/while/body/dot_general | solution.py:23
  157.2 7.3 %fusion.164 = f32[1024,1024]{1,0:T(8,128)S(1)} fusion(f32[512,1024]{1,0:T(8,128)S(1)} %fusion.163), kind=kOutput, calls=%fused_computation.63.clone.1 | convolution fusion | flops 6442450944 | bytes 6291456 | tf_op jit(solution)/shard_map/while/body/dot_general | solution.py:24
  164.5 2.3 %fusion.165 = f32[1024,16]{0,1:T(8,128)S(1)} fusion(f32[1024,1024]{1,0:T(8,128)S(1)} %fusion.164, f32[16,1024]{1,0:T(8,128)S(1)} %get-tuple-element.152), kind=kOutput, calls=%fused_computation.64.clone.1 | convolution fusion | flops 201326592 | bytes 4325376 | tf_op jit(solution)/shard_map/while/body/dot_general | solution.py:29
  167.1 1.5 cholesky.280
  169.8 1.2 custom-call.16
  171.4 4.3 %fusion.171 = f32[16,1024]{1,0:T(8,128)S(1)} fusion(f32[16,1024]{1,0:T(8,128)S(1)} %fusion.170, f32[1024,1024]{1,0:T(8,128)} %copy-done), kind=kOutput, calls=%fused_computation.66.clone.1 | convolution fusion | flops 201326592 | bytes 4325376 | tf_op jit(solution)/shard_map/while/body/dot_general | solution.py:29
  175.9 1.5 cholesky.281
  178.7 1.2 custom-call.17
  180.2 4.3 %fusion.177 = f32[16,1024]{1,0:T(8,128)S(1)} fusion(f32[16,1024]{1,0:T(8,128)S(1)} %fusion.176, f32[1024,1024]{1,0:T(8,128)} %copy-done), kind=kOutput, calls=%fused_computation.68.clone.1 | convolution fusion | flops 201326592 | bytes 4325376 | tf_op jit(solution)/shard_map/while/body/dot_general | solution.py:29
  184.7 1.5 cholesky.282
  187.5 1.2 custom-call.18
  189.0 4.3 %fusion.183 = f32[16,1024]{1,0:T(8,128)S(1)} fusion(f32[16,1024]{1,0:T(8,128)S(1)} %fusion.182, f32[1024,1024]{1,0:T(8,128)} %copy-done), kind=kOutput, calls=%fused_computation.70.clone.1 | convolution fusion | flops 201326592 | bytes 4325376 | tf_op jit(solution)/shard_map/while/body/dot_general | solution.py:29
  193.5 1.5 cholesky.283
  195.0 0.7 compare_reduce_fusion.11
  195.8 0.7 fusion.186
  196.5 1.2 custom-call.19
  197.7 0.7 dynamic_slice.20
  198.4 0.7 iota_compare_fusion.4
  199.3 1.8 fusion.187
  201.1 2.8 %fusion.188 = bf16[2,512,1024]{2,1,0:T(8,128)(2,1)} fusion(bf16[2,512,1024]{2,1,0:T(8,128)(2,1)} %get-tuple-element.135, s32[]{:T(128)S(6)} %select_n.76, f32[16,512]{1,0:T(8,128)S(1)} %fusion.187, f32[16,1024]{1,0:T(8,128)S(1)} %convolution_select_fusion.2), kind=kOutput, calls=%fused_computation.2.clone.1 | convolution fusion | flops 101187584 | bytes 1146884 | tf_op jit(solution)/shard_map/while/body/dot_general | solution.py:38
  (67 shorter events, 13.7 us)
Async XLA Ops:
  6.5 0.7 copy-start.2
  6.5 89.3 %reduce-scatter.2.cloned.1.call-start = ((), (), s32[]{:S(2)}) async-start(), calls=%async_computation.1 | async-start | bytes 10485760 | tf_op jit(solution)/shard_map/reduce_scatter | solution.py:60
  16.9 80.6 %copy-start.1 = (f32[16,1024]{1,0:T(8,128)S(1)}, f32[16,1024]{1,0:T(8,128)}, u32[]{:S(2)}) copy-start(f32[16,1024]{1,0:T(8,128)} %param.12) | copy-start | bytes 196612
  16.9 80.6 %copy-start.3 = (s32[2]{0:T(128)S(1)}, s32[2]{0:T(128)}, u32[]{:S(2)}) copy-start(s32[2]{0:T(128)} %param.11) | copy-start | bytes 28
  111.3 2.3 %copy-start = (f32[1024,1024]{1,0:T(8,128)}, f32[1024,1024]{1,0:T(8,128)S(1)}, u32[]{:S(2)}) copy-start(f32[1024,1024]{1,0:T(8,128)S(1)} %fusion.164) | copy-start | bytes 12582916 | tf_op jit(solution)/shard_map/while
  164.5 2.3 %copy-start = (f32[1024,1024]{1,0:T(8,128)}, f32[1024,1024]{1,0:T(8,128)S(1)}, u32[]{:S(2)}) copy-start(f32[1024,1024]{1,0:T(8,128)S(1)} %fusion.164) | copy-start | bytes 12582916 | tf_op jit(solution)/shard_map/while
Sparse Core Ops, SparseCore 0:
  10.2 85.6 reduce-scatter.1
where the time goes:
time: 212 us; the launch traced here: 211 us
  waiting for transfers between devices  78 us (37%)
  matrix products  63.9 us (30%)
  other arithmetic  44.9 us (21%)
  between operations  13.5 us (6%)
  loops' own time  6.14 us (3%)
  local copies, waits for them, and re-layouts  4.98 us (2%)
    reduce_scatter x1, waiting for transfers between devices, body(): lax.psum_scatter(partial_time.astype(jnp.float32).astype(jnp.bfloat16), '...  77.3 us
    dot_general x8, matrix products, denoise_patch(): jnp.dot(subspace, spectral_gram, precision=lax.Precision.HIGHEST)  30.3 us
    another operation x24, other arithmetic, denoise_patch(): factor = jnp.linalg.cholesky(inner_gram)  17.5 us
    another operation x16, other arithmetic, denoise_patch(): jax.scipy.linalg.solve_triangular(factor, product_rows, lower=True)  14.7 us
    dot_general x2, matrix products, denoise_patch(): lax.dot_general(spectra, spectra, (((0,), (0,)), ((), ())), precision=lax...  14.6 us
    another operation x2, other arithmetic  8.38 us
    dot_general x2, matrix products, denoise_patch(): jnp.dot(patch_block, transform, preferred_element_type=jnp.float32)  6.35 us
    another operation x1, loops' own time, run_patches(): return lax.fori_loop(0, work_count, process, results)  6.14 us
  transfers between devices with their start and end apart: 1, of which 1 were waited for; matrix products, arithmetic and copies ran while one was open for 5% of the time, Pallas kernels for 0%

commit v1 on v0

v1 whole, which is shorter than its diff:
```python
import math

import jax
import jax.numpy as jnp
from jax import lax
from jax.sharding import PartitionSpec as P

ITERS = 4
HI = lax.Precision.HIGHEST


def spectral_table(length):
    points = jnp.arange(length, dtype=jnp.int32)
    phase_index = points[:, None] * points[None, :] % length
    angles = phase_index.astype(jnp.float32) * (2.0 * math.pi / length)
    cosine = jnp.cos(angles) / math.sqrt(length)
    sine_part = jnp.sin(angles) / math.sqrt(length)
    upper_rows = jnp.concatenate([cosine, -sine_part], axis=1)
    lower_rows = jnp.concatenate([sine_part, cosine], axis=1)
    return jnp.concatenate([upper_rows, lower_rows], axis=0).astype(jnp.bfloat16)


def denoise_batch(patches, flags, ranks, transform, start_basis):
    spectra = jnp.einsum("bvt,tf->bvf", patches, transform, preferred_element_type=jnp.float32)
    kernel = jnp.einsum("bvf,bwf->bvw", spectra, spectra, precision=HI)
    coeff = jnp.einsum("kf,bvf->bkv", start_basis, spectra, precision=HI)
    for sweep_index in range(ITERS):
        pushed = jnp.einsum("bkv,bvw->bkw", coeff, kernel, precision=HI)
        inner_gram = jnp.einsum("bkw,bjw->bkj", pushed, coeff, precision=HI)
        factor = jnp.linalg.cholesky(inner_gram)
        if sweep_index < ITERS - 1:
            coeff = jax.scipy.linalg.solve_triangular(factor, pushed, lower=True)
        else:
            image = jnp.einsum("bkv,bvf->bkf", coeff, spectra, precision=HI)
            both = jax.scipy.linalg.solve_triangular(
                factor, jnp.concatenate([pushed, image], axis=-1), lower=True
            )
            coeff = both[..., : pushed.shape[-1]]
            subspace = both[..., pushed.shape[-1]:]
    keep_rows = jnp.arange(subspace.shape[1], dtype=jnp.int32)[None, :, None] < ranks[:, None, None]
    truncated = jnp.where(keep_rows, subspace, 0.0)
    coefficients = jnp.where(keep_rows, coeff, 0.0)
    result = jnp.einsum("bkv,bkf->bvf", coefficients, truncated, precision=HI)
    result = result.astype(jnp.bfloat16)
    return jnp.where(flags[:, None, None], result, jnp.zeros_like(result))


def body(partial_time, brain_mask, rank_limit, start_basis):
    summed = lax.psum_scatter(partial_time, "coil", scatter_dimension=1, tiled=True)
    patches = summed.reshape((-1, summed.shape[-2], summed.shape[-1]))
    transform = spectral_table(patches.shape[-1] // 2)
    return denoise_batch(patches, brain_mask > 0, rank_limit, transform, start_basis)


def solution(mesh):
    return jax.shard_map(
        body,
        mesh=mesh,
        in_specs=(
            P("coil", None, "slab", None, None),
            P(("coil", "slab")),
            P(("coil", "slab")),
            P(),
        ),
        out_specs=P(("coil", "slab"), None, None),
        check_vma=False,
    )
```

time: 212 us -> 158 us (0.75)
  matrix products: 63.9 us -> 30.6 us
  other arithmetic: 44.9 us -> 31 us
  loops' own time: 6.14 us -> 0 us
  local copies, waits for them, and re-layouts: 4.98 us -> 0.31 us
  waiting for transfers between devices: 78 us -> 80.8 us
    dot_general x24 -> x13, matrix products: 61.8 us -> 29.3 us  [the longest x1 7.08 us: denoise_batch(): kernel = jnp.einsum('bvf,bwf->bvw', spectra, spectra, precision=HI)]
    another operation x42 -> x24, other arithmetic: 40.6 us -> 30.9 us  [the longest x13 12.3 us: denoise_batch(): factor = jnp.linalg.cholesky(inner_gram)]
    another operation x1 -> x0, loops' own time: 6.14 us -> none  [run_patches(): return lax.fori_loop(0, work_count, process, results)]
    reduce_scatter x1, waiting for transfers between devices: 77.3 us -> 80.1 us  [body(): lax.psum_scatter(partial_time, 'coil', scatter_dimension=1, tiled=True)]
    dynamic_slice x4 -> x0, local copies, waits for them, and re-layouts: 2.68 us -> none  [the longest x2 1.35 us: process(): rank_cap = lax.dynamic_index_in_dim(ranks, slot_index, 0, keepdims=False)]
where the time goes in v1:
time: 158 us; the launch traced here: 156 us
  waiting for transfers between devices  80.8 us (51%)
  other arithmetic  31 us (20%)
  matrix products  30.6 us (19%)
  between operations  13.6 us (9%)
    reduce_scatter x1, waiting for transfers between devices, body(): lax.psum_scatter(partial_time, 'coil', scatter_dimension=1, tiled=True)  80.1 us
    another operation x13, other arithmetic, denoise_batch(): factor = jnp.linalg.cholesky(inner_gram)  12.3 us
    another operation x2, other arithmetic  8.39 us
    another operation x6, other arithmetic, denoise_batch(): coeff = jax.scipy.linalg.solve_triangular(factor, pushed, lower=True)  7.61 us
    dot_general x1, matrix products, denoise_batch(): kernel = jnp.einsum('bvf,bwf->bvw', spectra, spectra, precision=HI)  7.08 us
    dot_general x1, matrix products, denoise_batch(): image = jnp.einsum('bkv,bvf->bkf', coeff, spectra, precision=HI)  5.66 us
    dot_general x1, matrix products, denoise_batch(): result = jnp.einsum('bkv,bkf->bvf', coefficients, truncated, precision=HI)  4.83 us
    dot_general x4, matrix products, denoise_batch(): pushed = jnp.einsum('bkv,bvw->bkw', coeff, kernel, precision=HI)  4.62 us
  transfers between devices with their start and end apart: 1, of which 1 were waited for; matrix products, arithmetic and copies ran while one was open for 5% of the time, Pallas kernels for 0%

profile of v1, /device:TPU:64, one launch (start us, length us, event | category | flops | bytes accessed | tf_op | source)
XLA Modules:
  0.0 156.2 jit_solution(9718098215484486392)
XLA Ops:
  6.5 0.0 copy-start
  6.5 0.0 reduce-scatter.2.cloned.1.call-start
  6.5 0.7 reduce-scatter.2.cloned.1.call-update
  7.3 4.0 %fusion.20 = bf16[512,512]{0,1:T(8,128)(2,1)S(1)} fusion(), kind=kLoop, calls=%fused_computation.28 | loop fusion | flops 4194304 | bytes 524288 | tf_op jit(solution)/shard_map/convert.2
  11.3 4.4 %negate_convert_fusion = (bf16[512,512]{0,1:T(8,128)(2,1)S(1)}, bf16[512,512]{0,1:T(8,128)(2,1)S(1)}) fusion(), kind=kLoop, calls=%fused_computation.22 | loop fusion | flops 4980736 | bytes 1048576 | tf_op jit(solution)/shard_map/convert.5
  15.7 0.0 copy-done.2
  15.7 0.0 copy-done.3
  15.7 0.1 iota_compare_fusion.2
  15.8 80.1 %reduce-scatter.2.cloned.1.call-done = bf16[1,1,2,512,1024]{4,3,2,1,0:T(8,128)(2,1)} async-done(((bf16[1,4,2,512,1024]{4,3,2,1,0:T(8,128)(2,1)}), bf16[1,1,2,512,1024]{4,3,2,1,0:T(8,128)(2,1)}) %reduce-scatter.2.cloned.1.call-update) | async-done | bytes 2097168 | tf_op jit(solution)/shard_map/reduce_scatter | solution.py:49
  95.9 4.0 %fusion.6 = f32[1024,2,512]{2,0,1:T(8,128)S(1)} fusion(bf16[512,512]{0,1:T(8,128)(2,1)S(1)} %get-tuple-element.8, bf16[512,512]{0,1:T(8,128)(2,1)S(1)} %fusion.20, bf16[512,512]{0,1:T(8,128)(2,1)S(1)} %get-tuple-element.6, bf16[1,1,2,512,1024]{4,3,2,1,0:T(8,128)(2,1)} %reduce-scatter.2.cloned.1.call-done), kind=kOutput, calls=%fused_computation.7 | convolution fusion | flops 2155872256 | bytes 7864320 | tf_op jit(solution)/shard_map/bvt,tf->bvf/dot_general | solution.py:24
  99.8 0.0 copy-start.1
  99.9 7.1 %fusion.2 = f32[2,512,512]{2,1,0:T(8,128)S(1)} fusion(f32[1024,2,512]{2,0,1:T(8,128)S(1)} %fusion.6), kind=kOutput, calls=%fused_computation.2 | convolution fusion | flops 6442450944 | bytes 6291456 | tf_op jit(solution)/shard_map/bvf,bwf->bvw/dot_general | solution.py:25
  106.9 0.0 copy-done.1
  107.0 2.3 %fusion.4 = f32[2,512,16]{1,2,0:T(8,128)S(1)} fusion(f32[1024,2,512]{2,0,1:T(8,128)S(1)} %fusion.6, f32[16,1024]{1,0:T(8,128)S(1)} %copy-done), kind=kOutput, calls=%fused_computation.4 | convolution fusion | flops 201326592 | bytes 4325376 | tf_op jit(solution)/shard_map/kf,bvf->bkv/dot_general | solution.py:26
  109.3 1.3 fusion.45
  110.6 0.2 fusion.46
  110.8 0.1 copy.19
  110.8 2.9 %custom-call.16 = f32[2,16,16]{2,1,0:T(8,128)S(1)} custom-call(f32[2,16,16]{2,1,0:T(8,128)S(1)} %fusion.40), custom_call_target="Cholesky" | custom-call | tf_op jit(solution)/shard_map/jit(cholesky)/cholesky | solution.py:30
  113.8 0.1 compare_reduce_fusion.3
  113.9 0.1 select_bitcast_fusion.2
  114.0 2.5 %custom-call.17 = f32[2,1,16,16]{2,3,1,0:T(8,128)S(1)} custom-call(f32[2,1,16,16]{3,2,1,0:T(8,128)S(1)} %select_bitcast_fusion.2), custom_call_target="InvertDiagBlocksLowerTriangular" | custom-call | tf_op jit(solution)/shard_map/jit(_solve_triangular)/vmap()/triangular_solve | solution.py:32
  116.5 0.3 fusion.38
  116.8 1.1 fusion.47
  117.9 0.2 fusion.48
  118.1 0.1 copy.21
  118.2 2.9 %custom-call.18 = f32[2,16,16]{2,1,0:T(8,128)S(1)} custom-call(f32[2,16,16]{2,1,0:T(8,128)S(1)} %fusion.37), custom_call_target="Cholesky" | custom-call | tf_op jit(solution)/shard_map/jit(cholesky)/cholesky | solution.py:30
  121.1 0.1 compare_reduce_fusion.2
  121.3 0.1 select_bitcast_fusion.1
  121.3 2.5 %custom-call.19 = f32[2,1,16,16]{2,3,1,0:T(8,128)S(1)} custom-call(f32[2,1,16,16]{3,2,1,0:T(8,128)S(1)} %select_bitcast_fusion.1), custom_call_target="InvertDiagBlocksLowerTriangular" | custom-call | tf_op jit(solution)/shard_map/jit(_solve_triangular)/vmap()/triangular_solve | solution.py:32
  123.8 0.3 fusion.35
  124.1 1.1 fusion.49
  125.2 0.2 fusion.50
  125.4 0.1 copy.23
  125.5 2.9 %custom-call.20 = f32[2,16,16]{2,1,0:T(8,128)S(1)} custom-call(f32[2,16,16]{2,1,0:T(8,128)S(1)} %fusion.34), custom_call_target="Cholesky" | custom-call | tf_op jit(solution)/shard_map/jit(cholesky)/cholesky | solution.py:30
  128.5 0.1 compare_reduce_fusion.1
  128.6 0.1 select_bitcast_fusion
  128.7 2.5 %custom-call.21 = f32[2,1,16,16]{2,3,1,0:T(8,128)S(1)} custom-call(f32[2,1,16,16]{3,2,1,0:T(8,128)S(1)} %select_bitcast_fusion), custom_call_target="InvertDiagBlocksLowerTriangular" | custom-call | tf_op jit(solution)/shard_map/jit(_solve_triangular)/vmap()/triangular_solve | solution.py:32
  131.1 0.3 fusion.32
  131.4 1.1 fusion.51
  132.5 5.7 %fusion = f32[2,16,1024]{2,1,0:T(8,128)S(1)} fusion(f32[2,16,512]{2,1,0:T(8,128)S(1)} %fusion.32, f32[1024,2,512]{2,0,1:T(8,128)} %copy-done.1), kind=kOutput, calls=%fused_computation | convolution fusion | flops 201326592 | bytes 4390912 | tf_op jit(solution)/shard_map/bkv,bvf->bkf/dot_general | solution.py:34
  138.2 0.2 fusion.52
  138.4 0.1 copy.25
  138.5 2.9 %custom-call.22 = f32[2,16,16]{2,1,0:T(8,128)S(1)} custom-call(f32[2,16,16]{2,1,0:T(8,128)S(1)} %fusion.31), custom_call_target="Cholesky" | custom-call | tf_op jit(solution)/shard_map/jit(cholesky)/cholesky | solution.py:30
  141.5 0.1 compare_reduce_fusion
  141.6 0.1 fusion.41
  141.7 2.5 %custom-call.10 = f32[2,1,16,16]{2,3,1,0:T(8,128)S(1)} custom-call(f32[2,1,16,16]{3,2,1,0:T(8,128)S(1)} %fusion.41), custom_call_target="InvertDiagBlocksLowerTriangular" | custom-call | tf_op jit(solution)/shard_map/jit(_solve_triangular)/vmap()/triangular_solve | solution.py:35
  144.1 0.4 fusion.21
  144.5 4.8 %convert_select_fusion = bf16[2,512,1024]{2,1,0:T(8,128)(2,1)} fusion(pred[2]{0:T(512)(128)(4,1)S(1)} %broadcast_compare_fusion, f32[2,16,1536]{2,1,0:T(8,128)S(1)} %fusion.21, pred[2,16]{1,0:T(4,128)(4,1)S(1)} %iota_compare_fusion.2), kind=kOutput, calls=%fused_computation.15 | convolution fusion | flops 203472896 | bytes 2295296 | tf_op jit(solution)/shard_map/bkv,bkf->bvf/dot_general | solution.py:43
  (14 shorter events, 0.2 us)
Async XLA Ops:
  6.5 100.4 %copy-start = (f32[16,1024]{1,0:T(8,128)S(1)}, f32[16,1024]{1,0:T(8,128)}, u32[]{:S(2)}) copy-start(f32[16,1024]{1,0:T(8,128)} %param.10) | copy-start | bytes 196612
  6.5 9.2 %copy-start.2 = (s32[2]{0:T(128)S(1)}, s32[2]{0:T(128)}, u32[]{:S(2)}) copy-start(s32[2]{0:T(128)} %param.8) | copy-start | bytes 28
  6.5 9.2 %copy-start.3 = (s32[2]{0:T(128)S(1)}, s32[2]{0:T(128)}, u32[]{:S(2)}) copy-start(s32[2]{0:T(128)} %param.9) | copy-start | bytes 28
  6.5 89.3 %reduce-scatter.2.cloned.1.call-start = ((), (), s32[]{:S(2)}) async-start(), calls=%async_computation.1 | async-start | bytes 10485760 | tf_op jit(solution)/shard_map/reduce_scatter | solution.py:49
  99.8 7.1 %copy-start.1 = (f32[1024,2,512]{2,0,1:T(8,128)}, f32[1024,2,512]{2,0,1:T(8,128)S(1)}, u32[]{:S(2)}) copy-start(f32[1024,2,512]{2,0,1:T(8,128)S(1)} %fusion.6) | copy-start | bytes 12582916
Sparse Core Ops, SparseCore 0:
  10.2 85.6 reduce-scatter.1

commit v2 on v1

--- a/solution.py
+++ b/solution.py
@@ -45,16 +45,51 @@
     return jnp.where(flags[:, None, None], result, jnp.zeros_like(result))
 
 
-def body(partial_time, brain_mask, rank_limit, start_basis):
-    summed = lax.psum_scatter(partial_time, "coil", scatter_dimension=1, tiled=True)
-    patches = summed.reshape((-1, summed.shape[-2], summed.shape[-1]))
-    transform = spectral_table(patches.shape[-1] // 2)
-    return denoise_batch(patches, brain_mask > 0, rank_limit, transform, start_basis)
+def ring_pairs(n_coil, n_slab):
+    pairs = []
+    for coil in range(n_coil):
+        x_hi, core = divmod(coil, 2)
+        for slab in range(n_slab):
+            x_lo = slab % 2
+            x = 2 * x_hi + x_lo
+            step = 1 if core == 0 else -1
+            x_to = (x + step) % 4
+            coil_to = 2 * (x_to // 2) + core
+            slab_to = slab - x_lo + x_to % 2
+            pairs.append((coil * n_slab + slab, coil_to * n_slab + slab_to))
+    return pairs
+
+
+def coil_sum(partial_time, n_coil, n_slab):
+    parts = partial_time[0]
+    coil = lax.axis_index("coil")
+    chip_pair = [(i, i ^ 1) for i in range(n_coil)]
+
+    def pick(o):
+        return lax.dynamic_index_in_dim(parts, o, 0, keepdims=False)
+
+    got_forward = lax.ppermute(pick(coil ^ 3), "coil", chip_pair)
+    forward = (pick(coil ^ 2).astype(jnp.float32) + got_forward.astype(jnp.float32)).astype(jnp.bfloat16)
+    got_own = lax.ppermute(pick(coil ^ 1), "coil", chip_pair)
+    own = pick(coil).astype(jnp.float32) + got_own.astype(jnp.float32)
+    pairs = ring_pairs(n_coil, n_slab)
+    hop = lax.ppermute(forward, ("coil", "slab"), pairs)
+    hop = lax.ppermute(hop, ("coil", "slab"), pairs)
+    return (own + hop.astype(jnp.float32)).astype(jnp.bfloat16)
+
+
+def make_body(n_coil, n_slab):
+    def body(partial_time, brain_mask, rank_limit, start_basis):
+        patches = coil_sum(partial_time, n_coil, n_slab)
+        transform = spectral_table(patches.shape[-1] // 2)
+        return denoise_batch(patches, brain_mask > 0, rank_limit, transform, start_basis)
+
+    return body
 
 
 def solution(mesh):
     return jax.shard_map(
-        body,
+        make_body(mesh.shape["coil"], mesh.shape["slab"]),
         mesh=mesh,
         in_specs=(
             P("coil", None, "slab", None, None),

time: 158 us -> 122 us (0.77)
  waiting for transfers between devices: 80.8 us -> 47.8 us
  between operations: 13.6 us -> 0.16 us
  local copies, waits for them, and re-layouts: 0.31 us -> 4.54 us
  other arithmetic: 31 us -> 34.4 us
  starting transfers between devices: 0.01 us -> 2.98 us
    reduce_scatter x1 -> x0, waiting for transfers between devices: 80.1 us -> none  [body(): lax.psum_scatter(partial_time, 'coil', scatter_dimension=1, tiled=True)]
    ppermute x0 -> x4, waiting for transfers between devices: none -> 47.8 us  [the longest x1 24.7 us: coil_sum(): hop = lax.ppermute(forward, ('coil', 'slab'), pairs)]
    squeeze x0 -> x1, local copies, waits for them, and re-layouts: none -> 4.23 us  [pick(): return lax.dynamic_index_in_dim(parts, o, 0, keepdims=False)]
    convert_element_type x0 -> x1, other arithmetic: none -> 3.19 us  [coil_sum(): (pick(coil ^ 2).astype(jnp.float32) + got_forward.astype(jnp.float32)).as...]
    ppermute x0 -> x4, starting transfers between devices: none -> 2.98 us  [the longest x1 1.57 us: coil_sum(): hop = lax.ppermute(forward, ('coil', 'slab'), pairs)]
  transfers between devices with their start and end apart: 1 -> 4, of which waited for: 1 -> 3; matrix products, arithmetic and copies ran while one was open for 5% -> 7% of each run, Pallas kernels for 0% -> 0%
where the time goes in v2:
time: 122 us; the launch traced here: 121 us
  waiting for transfers between devices  47.8 us (39%)
  other arithmetic  34.4 us (28%)
  matrix products  31.6 us (26%)
  local copies, waits for them, and re-layouts  4.54 us (4%)
  starting transfers between devices  2.98 us (2%)
    ppermute x1, waiting for transfers between devices, coil_sum(): hop = lax.ppermute(forward, ('coil', 'slab'), pairs)  24.7 us
    ppermute x1, waiting for transfers between devices, coil_sum(): hop = lax.ppermute(hop, ('coil', 'slab'), pairs)  18.6 us
    another operation x13, other arithmetic, denoise_batch(): factor = jnp.linalg.cholesky(inner_gram)  12.3 us
    another operation x2, other arithmetic  8.57 us
    another operation x6, other arithmetic, denoise_batch(): coeff = jax.scipy.linalg.solve_triangular(factor, pushed, lower=True)  7.61 us
    dot_general x1, matrix products, denoise_batch(): kernel = jnp.einsum('bvf,bwf->bvw', spectra, spectra, precision=HI)  6.91 us
    dot_general x1, matrix products, denoise_batch(): jnp.einsum('bvt,tf->bvf', patches, transform, preferred_element_type=jnp....  5.24 us
    dot_general x1, matrix products, denoise_batch(): result = jnp.einsum('bkv,bkf->bvf', coefficients, truncated, precision=HI)  4.83 us
  transfers between devices with their start and end apart: 4, of which 3 were waited for; matrix products, arithmetic and copies ran while one was open for 7% of the time, Pallas kernels for 0%

profile of v2, /device:TPU:64, one launch (start us, length us, event | category | flops | bytes accessed | tf_op | source)
XLA Modules:
  0.0 121.5 jit_solution(5560992582318634085)
XLA Ops:
  0.0 4.2 %dynamic-slice_bitcast_fusion.1 = (bf16[2,512,1024]{2,1,0:T(8,128)(2,1)S(1)}, bf16[2,512,1024]{2,1,0:T(8,128)(2,1)}) fusion(bf16[1,4,2,512,1024]{4,3,2,1,0:T(8,128)(2,1)} %param.7, s32[]{:T(128)S(6)} %select_n.42, s32[]{:T(128)S(6)} %select_n.44), kind=kLoop, calls=%fused_computation.16 | loop fusion | bytes 8388616 | tf_op jit(solution)/shard_map/jit(dynamic_index_in_dim)/squeeze | solution.py:69
  4.2 4.5 %collective-permute-done.1 = bf16[2,512,1024]{2,1,0:T(8,128)(2,1)} collective-permute-done((bf16[2,512,1024]{2,1,0:T(8,128)(2,1)}, bf16[2,512,1024]{2,1,0:T(8,128)(2,1)}, u32[]{:S(2)}, u32[]{:S(2)}) %collective-permute-start.1) | collective-permute-done | bytes 2097184 | tf_op jit(solution)/shard_map/ppermute | solution.py:71
  8.7 3.2 %fusion = bf16[2,512,1024]{2,1,0:T(8,128)(2,1)S(1)} fusion(bf16[2,512,1024]{2,1,0:T(8,128)(2,1)} %collective-permute-done.1, bf16[1,4,2,512,1024]{4,3,2,1,0:T(8,128)(2,1)} %param.7, s32[]{:T(128)S(6)} %select_n.43), kind=kLoop, calls=%fused_computation.1 | loop fusion | flops 4194304 | bytes 6291460 | tf_op jit(solution)/shard_map/convert_element_type | solution.py:72
  11.9 1.6 %collective-permute-start.2 = (bf16[2,512,1024]{2,1,0:T(8,128)(2,1)S(1)}, bf16[2,512,1024]{2,1,0:T(8,128)(2,1)}, u32[]{:S(2)}, u32[]{:S(2)}) collective-permute-start(bf16[2,512,1024]{2,1,0:T(8,128)(2,1)S(1)} %fusion), channel_id=1, source_target_pairs={{0,1},{1,128},{2,3},{3,130},{4,5},{5,132},{6,7},{7,134},{8,9},{9,1... | collective-permute-start | bytes 6291464 | tf_op jit(solution)/shard_map/ppermute | solution.py:76
  13.5 1.1 collective-permute-start
  14.6 24.7 %collective-permute-done.2 = bf16[2,512,1024]{2,1,0:T(8,128)(2,1)} collective-permute-done((bf16[2,512,1024]{2,1,0:T(8,128)(2,1)S(1)}, bf16[2,512,1024]{2,1,0:T(8,128)(2,1)}, u32[]{:S(2)}, u32[]{:S(2)}) %collective-permute-start.2) | collective-permute-done | bytes 2097184 | tf_op jit(solution)/shard_map/ppermute | solution.py:76
  39.4 0.3 collective-permute-start.3
  39.7 4.0 %fusion.19 = bf16[512,512]{1,0:T(8,128)(2,1)S(1)} fusion(), kind=kLoop, calls=%fused_computation.30 | loop fusion | flops 4194304 | bytes 524288 | tf_op jit(solution)/shard_map/convert.4
  43.7 4.6 %negate_convert_fusion = (bf16[512,512]{1,0:T(8,128)(2,1)S(1)}, bf16[512,512]{1,0:T(8,128)(2,1)S(1)}) fusion(), kind=kLoop, calls=%fused_computation.24 | loop fusion | flops 4980736 | bytes 1048576 | tf_op jit(solution)/shard_map/convert.7
  48.3 0.1 iota_compare_fusion.2
  48.4 18.6 %collective-permute-done.3 = bf16[2,512,1024]{2,1,0:T(8,128)(2,1)} collective-permute-done((bf16[2,512,1024]{2,1,0:T(8,128)(2,1)}, bf16[2,512,1024]{2,1,0:T(8,128)(2,1)}, u32[]{:S(2)}, u32[]{:S(2)}) %collective-permute-start.3) | collective-permute-done | bytes 2097184 | tf_op jit(solution)/shard_map/ppermute | solution.py:77
  66.9 5.2 %fusion.3 = f32[2,512,1024]{2,1,0:T(8,128)S(1)} fusion(bf16[2,512,1024]{2,1,0:T(8,128)(2,1)} %collective-permute-done.3, bf16[2,512,1024]{2,1,0:T(8,128)(2,1)} %collective-permute-done, bf16[512,512]{1,0:T(8,128)(2,1)S(1)} %get-tuple-element.10, bf16[512,512]{1,0:T(8,128)(2,1)S(1)} %fusion.19, bf16[512,512]{1,0:T(8,128)(2,1)S(1)} %get-tuple-element.9, ...), kind=kOutput, calls=%fused_computation.5 | convolution fusion | flops 2162163712 | bytes 12058628 | tf_op jit(solution)/shard_map/bvt,tf->bvf/dot_general | solution.py:24
  72.2 6.9 %fusion.46 = f32[2,512,512]{2,1,0:T(8,128)S(1)} fusion(f32[2,512,1024]{2,1,0:T(8,128)S(1)} %fusion.3), kind=kOutput, calls=%fused_computation.79 | convolution fusion | flops 6442450944 | bytes 6291456 | tf_op jit(solution)/shard_map/bvf,bwf->bvw/dot_general | solution.py:25
  79.1 3.6 %fusion.24 = f32[2,512,16]{1,2,0:T(8,128)S(1)} fusion(f32[2,512,1024]{2,1,0:T(8,128)S(1)} %fusion.3, f32[16,1024]{1,0:T(8,128)S(1)} %copy-done), kind=kOutput, calls=%fused_computation.37 | convolution fusion | flops 201326592 | bytes 4325376 | tf_op jit(solution)/shard_map/kf,bvf->bkv/dot_general | solution.py:26
  82.7 1.3 %fusion.47 = f32[2,16,512]{2,1,0:T(8,128)S(1)} fusion(f32[2,512,16]{1,2,0:T(8,128)S(1)} %fusion.24, f32[2,512,512]{2,1,0:T(8,128)S(1)} %fusion.46), kind=kOutput, calls=%fused_computation.80 | convolution fusion | flops 100663296 | bytes 2228224 | tf_op jit(solution)/shard_map/bkv,bvw->bkw/dot_general | solution.py:28
  84.1 0.2 fusion.48
  84.3 0.1 copy.13
  84.4 2.9 %custom-call.16 = f32[2,16,16]{2,1,0:T(8,128)S(1)} custom-call(f32[2,16,16]{2,1,0:T(8,128)S(1)} %fusion.40), custom_call_target="Cholesky" | custom-call | tf_op jit(solution)/shard_map/jit(cholesky)/cholesky | solution.py:30
  87.3 0.1 compare_reduce_fusion.3
  87.5 0.1 select_bitcast_fusion.2
  87.5 2.5 %custom-call.17 = f32[2,1,16,16]{2,3,1,0:T(8,128)S(1)} custom-call(f32[2,1,16,16]{3,2,1,0:T(8,128)S(1)} %select_bitcast_fusion.2), custom_call_target="InvertDiagBlocksLowerTriangular" | custom-call | tf_op jit(solution)/shard_map/jit(_solve_triangular)/vmap()/triangular_solve | solution.py:32
  90.0 0.3 fusion.38
  90.3 1.1 fusion.49
  91.4 0.2 fusion.50
  91.6 0.1 copy.15
  91.7 2.9 %custom-call.18 = f32[2,16,16]{2,1,0:T(8,128)S(1)} custom-call(f32[2,16,16]{2,1,0:T(8,128)S(1)} %fusion.37), custom_call_target="Cholesky" | custom-call | tf_op jit(solution)/shard_map/jit(cholesky)/cholesky | solution.py:30
  94.7 0.1 compare_reduce_fusion.2
  94.8 0.1 select_bitcast_fusion.1
  94.9 2.5 %custom-call.19 = f32[2,1,16,16]{2,3,1,0:T(8,128)S(1)} custom-call(f32[2,1,16,16]{3,2,1,0:T(8,128)S(1)} %select_bitcast_fusion.1), custom_call_target="InvertDiagBlocksLowerTriangular" | custom-call | tf_op jit(solution)/shard_map/jit(_solve_triangular)/vmap()/triangular_solve | solution.py:32
  97.3 0.3 fusion.35
  97.6 1.1 fusion.51
  98.7 0.2 fusion.52
  98.9 0.1 copy.17
  99.0 2.9 %custom-call.20 = f32[2,16,16]{2,1,0:T(8,128)S(1)} custom-call(f32[2,16,16]{2,1,0:T(8,128)S(1)} %fusion.34), custom_call_target="Cholesky" | custom-call | tf_op jit(solution)/shard_map/jit(cholesky)/cholesky | solution.py:30
  102.0 0.1 compare_reduce_fusion.1
  102.1 0.1 select_bitcast_fusion
  102.2 2.5 %custom-call.21 = f32[2,1,16,16]{2,3,1,0:T(8,128)S(1)} custom-call(f32[2,1,16,16]{3,2,1,0:T(8,128)S(1)} %select_bitcast_fusion), custom_call_target="InvertDiagBlocksLowerTriangular" | custom-call | tf_op jit(solution)/shard_map/jit(_solve_triangular)/vmap()/triangular_solve | solution.py:32
  104.6 0.3 fusion.32
  104.9 1.1 fusion.53
  106.1 4.3 %fusion.55 = f32[2,16,1024]{2,1,0:T(8,128)S(1)} fusion(f32[2,16,512]{2,1,0:T(8,128)S(1)} %fusion.32, f32[2,512,1024]{2,1,0:T(8,128)} %copy-done.1), kind=kOutput, calls=%fused_computation.88 | convolution fusion | flops 201326592 | bytes 4390912 | tf_op jit(solution)/shard_map/bkv,bvf->bkf/dot_general | solution.py:34
  110.3 0.2 fusion.54
  110.5 0.1 copy.19
  110.6 2.9 %custom-call.22 = f32[2,16,16]{2,1,0:T(8,128)S(1)} custom-call(f32[2,16,16]{2,1,0:T(8,128)S(1)} %fusion.31), custom_call_target="Cholesky" | custom-call | tf_op jit(solution)/shard_map/jit(cholesky)/cholesky | solution.py:30
  113.6 0.1 compare_reduce_fusion
  113.7 0.1 fusion.41
  113.8 2.5 %custom-call.10 = f32[2,1,16,16]{2,3,1,0:T(8,128)S(1)} custom-call(f32[2,1,16,16]{3,2,1,0:T(8,128)S(1)} %fusion.41), custom_call_target="InvertDiagBlocksLowerTriangular" | custom-call | tf_op jit(solution)/shard_map/jit(_solve_triangular)/vmap()/triangular_solve | solution.py:35
  116.2 0.4 fusion.20
  116.7 4.8 %convert_select_fusion = bf16[2,512,1024]{2,1,0:T(8,128)(2,1)} fusion(pred[2]{0:T(512)(128)(4,1)S(1)} %broadcast_compare_fusion, f32[2,16,1536]{2,1,0:T(8,128)S(1)} %fusion.20, pred[2,16]{1,0:T(4,128)(4,1)S(1)} %iota_compare_fusion.2), kind=kOutput, calls=%fused_computation.14 | convolution fusion | flops 203472896 | bytes 2295296 | tf_op jit(solution)/shard_map/bkv,bkf->bvf/dot_general | solution.py:43
  (21 shorter events, 0.2 us)
Async XLA Ops:
  0.0 79.1 %copy-start = (f32[16,1024]{1,0:T(8,128)S(1)}, f32[16,1024]{1,0:T(8,128)}, u32[]{:S(2)}) copy-start(f32[16,1024]{1,0:T(8,128)} %param.10) | copy-start | bytes 196612
  4.2 4.5 %collective-permute-start.1 = (bf16[2,512,1024]{2,1,0:T(8,128)(2,1)}, bf16[2,512,1024]{2,1,0:T(8,128)(2,1)}, u32[]{:S(2)}, u32[]{:S(2)}) collective-permute-start(bf16[2,512,1024]{2,1,0:T(8,128)(2,1)} %get-tuple-element.8), channel_id=1, source_target_pairs={{0,64},{64,0},{128,192},{192,128},{1,65},{65,1},{129,193},{193,129... | collective-permute-start | bytes 6291464 | tf_op jit(solution)/shard_map/ppermute | solution.py:71
  4.2 44.0 %copy-start.2 = (s32[2]{0:T(128)S(1)}, s32[2]{0:T(128)}, u32[]{:S(2)}) copy-start(s32[2]{0:T(128)} %param.8) | copy-start | bytes 28
  4.2 44.0 %copy-start.3 = (s32[2]{0:T(128)S(1)}, s32[2]{0:T(128)}, u32[]{:S(2)}) copy-start(s32[2]{0:T(128)} %param.9) | copy-start | bytes 28
  11.9 27.4 %collective-permute-start.2 = (bf16[2,512,1024]{2,1,0:T(8,128)(2,1)S(1)}, bf16[2,512,1024]{2,1,0:T(8,128)(2,1)}, u32[]{:S(2)}, u32[]{:S(2)}) collective-permute-start(bf16[2,512,1024]{2,1,0:T(8,128)(2,1)S(1)} %fusion), channel_id=1, source_target_pairs={{0,1},{1,128},{2,3},{3,130},{4,5},{5,132},{6,7},{7,134},{8,9},{9,1... | collective-permute-start | bytes 6291464 | tf_op jit(solution)/shard_map/ppermute | solution.py:76
  13.5 34.8 %collective-permute-start = (bf16[2,512,1024]{2,1,0:T(8,128)(2,1)S(1)}, bf16[2,512,1024]{2,1,0:T(8,128)(2,1)}, u32[]{:S(2)}, u32[]{:S(2)}) collective-permute-start(bf16[2,512,1024]{2,1,0:T(8,128)(2,1)S(1)} %get-tuple-element.6), channel_id=1, source_target_pairs={{0,64},{64,0},{128,192},{192,128},{1,65},{65,1},{129,193},{193,129... | collective-permute-start | bytes 6291464 | tf_op jit(solution)/shard_map/ppermute | solution.py:73
  39.4 27.6 %collective-permute-start.3 = (bf16[2,512,1024]{2,1,0:T(8,128)(2,1)}, bf16[2,512,1024]{2,1,0:T(8,128)(2,1)}, u32[]{:S(2)}, u32[]{:S(2)}) collective-permute-start(bf16[2,512,1024]{2,1,0:T(8,128)(2,1)} %collective-permute-done.2), channel_id=1, source_target_pairs={{0,1},{1,128},{2,3},{3,130},{4,5},{5,132},{6,7},{7,134},{8,9},{9,1... | collective-permute-start | bytes 6291464 | tf_op jit(solution)/shard_map/ppermute | solution.py:77
  72.2 6.9 %copy-start.1 = (f32[2,512,1024]{2,1,0:T(8,128)}, f32[2,512,1024]{2,1,0:T(8,128)S(1)}, u32[]{:S(2)}) copy-start(f32[2,512,1024]{2,1,0:T(8,128)S(1)} %fusion.3) | copy-start | bytes 12582916

commit v3 on v2

--- a/solution.py
+++ b/solution.py
@@ -3,6 +3,7 @@
 import jax
 import jax.numpy as jnp
 from jax import lax
+from jax.experimental import pallas as pl
 from jax.sharding import PartitionSpec as P
 
 ITERS = 4
@@ -20,6 +21,28 @@
     return jnp.concatenate([upper_rows, lower_rows], axis=0).astype(jnp.bfloat16)
 
 
+def factor_solve_kernel(gram_ref, rhs_ref, out_ref):
+    for item in range(gram_ref.shape[0]):
+        gram = gram_ref[item]
+        work = rhs_ref[item]
+        for col in range(gram.shape[0]):
+            scale = 1.0 / jnp.sqrt(gram[col:col + 1, col:col + 1])
+            column = gram[:, col:col + 1] * scale
+            row = gram[col:col + 1, :] * scale
+            solved = work[col:col + 1, :] * scale
+            out_ref[item, col:col + 1, :] = solved
+            gram = gram - column * row
+            work = work - column * solved
+
+
+def factor_solve(inner_gram, rhs):
+    sym = 0.5 * (inner_gram + jnp.swapaxes(inner_gram, -1, -2))
+    return pl.pallas_call(
+        factor_solve_kernel,
+        out_shape=jax.ShapeDtypeStruct(rhs.shape, jnp.float32),
+    )(sym, rhs)
+
+
 def denoise_batch(patches, flags, ranks, transform, start_basis):
     spectra = jnp.einsum("bvt,tf->bvf", patches, transform, preferred_element_type=jnp.float32)
     kernel = jnp.einsum("bvf,bwf->bvw", spectra, spectra, precision=HI)
@@ -27,14 +50,11 @@
     for sweep_index in range(ITERS):
         pushed = jnp.einsum("bkv,bvw->bkw", coeff, kernel, precision=HI)
         inner_gram = jnp.einsum("bkw,bjw->bkj", pushed, coeff, precision=HI)
-        factor = jnp.linalg.cholesky(inner_gram)
         if sweep_index < ITERS - 1:
-            coeff = jax.scipy.linalg.solve_triangular(factor, pushed, lower=True)
+            coeff = factor_solve(inner_gram, pushed)
         else:
             image = jnp.einsum("bkv,bvf->bkf", coeff, spectra, precision=HI)
-            both = jax.scipy.linalg.solve_triangular(
-                factor, jnp.concatenate([pushed, image], axis=-1), lower=True
-            )
+            both = factor_solve(inner_gram, jnp.concatenate([pushed, image], axis=-1))
             coeff = both[..., : pushed.shape[-1]]
             subspace = both[..., pushed.shape[-1]:]
     keep_rows = jnp.arange(subspace.shape[1], dtype=jnp.int32)[None, :, None] < ranks[:, None, None]

time: 122 us -> 116 us (0.951)
  other arithmetic: 34.4 us -> 15 us
  Pallas kernels: 0 us -> 11.8 us
  matrix products: 31.6 us -> 33.2 us
    another operation x24 -> x2, other arithmetic: 31.1 us -> 8.56 us  [the longest x13 12.3 us: denoise_batch(): factor = jnp.linalg.cholesky(inner_gram)]
    pallas_call x0 -> x4, Pallas kernels: none -> 11.8 us  [factor_solve(): pl.pallas_call(factor_solve_kernel, out_shape=jax.ShapeDtypeStruct(rhs.sh...]
    mul x0 -> x4, other arithmetic: none -> 2.48 us  [factor_solve(): sym = 0.5 * (inner_gram + jnp.swapaxes(inner_gram, -1, -2))]
    dot_general x4, matrix products: 4.68 us -> 6.5 us  [denoise_batch(): pushed = jnp.einsum('bkv,bvw->bkw', coeff, kernel, precision=HI)]
    another operation x4 -> x0, matrix products: 1.27 us -> none  [the longest x3 0.87 us: denoise_batch(): coeff = jax.scipy.linalg.solve_triangular(factor, pushed, lower=True)]
where the time goes in v3:
time: 116 us; the launch traced here: 115 us
  waiting for transfers between devices  47.8 us (41%)
  matrix products  33.2 us (29%)
  other arithmetic  15 us (13%)
  Pallas kernels  11.8 us (10%)
  local copies, waits for them, and re-layouts  4.56 us (4%)
  starting transfers between devices  2.98 us (3%)
    ppermute x1, waiting for transfers between devices, coil_sum(): hop = lax.ppermute(forward, ('coil', 'slab'), pairs)  24.7 us
    ppermute x1, waiting for transfers between devices, coil_sum(): hop = lax.ppermute(hop, ('coil', 'slab'), pairs)  18.6 us
    pallas_call x4, Pallas kernels, factor_solve(): pl.pallas_call(factor_solve_kernel, out_shape=jax.ShapeDtypeStruct(rhs.sh...  11.8 us
    another operation x2, other arithmetic  8.56 us
    dot_general x1, matrix products, denoise_batch(): kernel = jnp.einsum('bvf,bwf->bvw', spectra, spectra, precision=HI)  6.91 us
    dot_general x4, matrix products, denoise_batch(): pushed = jnp.einsum('bkv,bvw->bkw', coeff, kernel, precision=HI)  6.5 us
    dot_general x1, matrix products, denoise_batch(): result = jnp.einsum('bkv,bkf->bvf', coefficients, truncated, precision=HI)  5.8 us
    dot_general x1, matrix products, denoise_batch(): jnp.einsum('bvt,tf->bvf', patches, transform, preferred_element_type=jnp....  5.24 us
  transfers between devices with their start and end apart: 4, of which 3 were waited for; matrix products, arithmetic and copies ran while one was open for 7% of the time, Pallas kernels for 0%

profile of v3, /device:TPU:64, one launch (start us, length us, event | category | flops | bytes accessed | tf_op | source)
XLA Modules:
  0.0 115.5 jit_solution(17744775493655018933)
XLA Ops:
  0.0 0.0 copy-start
  0.0 4.2 %dynamic-slice_bitcast_fusion.1 = (bf16[2,512,1024]{2,1,0:T(8,128)(2,1)S(1)}, bf16[2,512,1024]{2,1,0:T(8,128)(2,1)}) fusion(bf16[1,4,2,512,1024]{4,3,2,1,0:T(8,128)(2,1)} %param.4, s32[]{:T(128)S(6)} %select_n.39, s32[]{:T(128)S(6)} %select_n.41), kind=kLoop, calls=%fused_computation.16 | loop fusion | bytes 8388616 | tf_op jit(solution)/shard_map/jit(dynamic_index_in_dim)/squeeze | solution.py:89
  4.2 0.0 collective-permute-start.1
  4.2 4.5 %collective-permute-done.1 = bf16[2,512,1024]{2,1,0:T(8,128)(2,1)} collective-permute-done((bf16[2,512,1024]{2,1,0:T(8,128)(2,1)}, bf16[2,512,1024]{2,1,0:T(8,128)(2,1)}, u32[]{:S(2)}, u32[]{:S(2)}) %collective-permute-start.1) | collective-permute-done | bytes 2097184 | tf_op jit(solution)/shard_map/ppermute | solution.py:91
  8.7 3.2 %fusion = bf16[2,512,1024]{2,1,0:T(8,128)(2,1)S(1)} fusion(bf16[2,512,1024]{2,1,0:T(8,128)(2,1)} %collective-permute-done.1, bf16[1,4,2,512,1024]{4,3,2,1,0:T(8,128)(2,1)} %param.4, s32[]{:T(128)S(6)} %select_n.40), kind=kLoop, calls=%fused_computation.1 | loop fusion | flops 4194304 | bytes 6291460 | tf_op jit(solution)/shard_map/convert_element_type | solution.py:92
  11.9 1.6 %collective-permute-start.2 = (bf16[2,512,1024]{2,1,0:T(8,128)(2,1)S(1)}, bf16[2,512,1024]{2,1,0:T(8,128)(2,1)}, u32[]{:S(2)}, u32[]{:S(2)}) collective-permute-start(bf16[2,512,1024]{2,1,0:T(8,128)(2,1)S(1)} %fusion), channel_id=1, source_target_pairs={{0,1},{1,128},{2,3},{3,130},{4,5},{5,132},{6,7},{7,134},{8,9},{9,1... | collective-permute-start | bytes 6291464 | tf_op jit(solution)/shard_map/ppermute | solution.py:96
  13.5 1.1 collective-permute-start
  14.6 24.7 %collective-permute-done.2 = bf16[2,512,1024]{2,1,0:T(8,128)(2,1)} collective-permute-done((bf16[2,512,1024]{2,1,0:T(8,128)(2,1)S(1)}, bf16[2,512,1024]{2,1,0:T(8,128)(2,1)}, u32[]{:S(2)}, u32[]{:S(2)}) %collective-permute-start.2) | collective-permute-done | bytes 2097184 | tf_op jit(solution)/shard_map/ppermute | solution.py:96
  39.4 0.3 collective-permute-start.3
  39.6 4.0 %fusion.19 = bf16[512,512]{1,0:T(8,128)(2,1)S(1)} fusion(), kind=kLoop, calls=%fused_computation.30 | loop fusion | flops 4194304 | bytes 524288 | tf_op jit(solution)/shard_map/convert.4
  43.6 4.6 %negate_convert_fusion = (bf16[512,512]{1,0:T(8,128)(2,1)S(1)}, bf16[512,512]{1,0:T(8,128)(2,1)S(1)}) fusion(), kind=kLoop, calls=%fused_computation.24 | loop fusion | flops 4980736 | bytes 1048576 | tf_op jit(solution)/shard_map/convert.7
  48.2 0.0 copy-done.8
  48.2 0.0 copy-done.9
  48.3 0.1 iota_compare_fusion
  48.3 0.0 collective-permute-done
  48.3 18.6 %collective-permute-done.3 = bf16[2,512,1024]{2,1,0:T(8,128)(2,1)} collective-permute-done((bf16[2,512,1024]{2,1,0:T(8,128)(2,1)}, bf16[2,512,1024]{2,1,0:T(8,128)(2,1)}, u32[]{:S(2)}, u32[]{:S(2)}) %collective-permute-start.3) | collective-permute-done | bytes 2097184 | tf_op jit(solution)/shard_map/ppermute | solution.py:97
  66.9 5.2 %fusion.3 = f32[2,512,1024]{2,1,0:T(8,128)S(1)} fusion(bf16[2,512,1024]{2,1,0:T(8,128)(2,1)} %collective-permute-done.3, bf16[2,512,1024]{2,1,0:T(8,128)(2,1)} %collective-permute-done, bf16[512,512]{1,0:T(8,128)(2,1)S(1)} %get-tuple-element.8, bf16[512,512]{1,0:T(8,128)(2,1)S(1)} %fusion.19, bf16[512,512]{1,0:T(8,128)(2,1)S(1)} %get-tuple-element.7, ...), kind=kOutput, calls=%fused_computation.5 | convolution fusion | flops 2162163712 | bytes 12058628 | tf_op jit(solution)/shard_map/bvt,tf->bvf/dot_general | solution.py:47
  72.2 0.0 copy-start.1
  72.2 6.9 %fusion.33 = f32[2,512,512]{2,1,0:T(8,128)S(1)} fusion(f32[2,512,1024]{2,1,0:T(8,128)S(1)} %fusion.3), kind=kOutput, calls=%fused_computation.53 | convolution fusion | flops 6442450944 | bytes 6291456 | tf_op jit(solution)/shard_map/bvf,bwf->bvw/dot_general | solution.py:48
  79.1 0.0 copy-done.1
  79.1 0.0 copy-done
  79.1 3.6 %fusion.20 = f32[2,512,16]{1,2,0:T(8,128)S(1)} fusion(f32[2,512,1024]{2,1,0:T(8,128)S(1)} %fusion.3, f32[16,1024]{1,0:T(8,128)S(1)} %copy-done), kind=kOutput, calls=%fused_computation.34 | convolution fusion | flops 201326592 | bytes 4325376 | tf_op jit(solution)/shard_map/kf,bvf->bkv/dot_general | solution.py:49
  82.7 1.3 %fusion.34.rhs_ref = f32[2,16,512]{2,1,0:T(8,128)S(1)} fusion(f32[2,512,16]{1,2,0:T(8,128)S(1)} %fusion.20, f32[2,512,512]{2,1,0:T(8,128)S(1)} %fusion.33), kind=kOutput, calls=%fused_computation.54 | convolution fusion | flops 100663296 | bytes 2228224 | tf_op jit(solution)/shard_map/bkv,bvw->bkw/dot_general | solution.py:51
  84.1 0.2 fusion.35
  84.3 0.1 copy.5
  84.4 0.6 fusion.29.gram_ref
  85.0 0.0 copy-done.3
  85.0 2.9 %shard_map.46 = f32[2,16,512]{2,1,0:T(8,128)} custom-call(f32[2,16,16]{2,1,0:T(8,128)} %fusion.29.gram_ref, f32[2,16,512]{2,1,0:T(8,128)} %copy-done.3), custom_call_target="tpu_custom_call" | custom-call | tf_op jit(solution)/shard_map/pallas_call | solution.py:40
  87.9 2.0 %fusion.36.rhs_ref = f32[2,16,512]{2,1,0:T(8,128)S(1)} fusion(f32[2,16,512]{2,1,0:T(8,128)} %shard_map.46, f32[2,512,512]{2,1,0:T(8,128)S(1)} %fusion.33), kind=kOutput, calls=%fused_computation.56 | convolution fusion | flops 100663296 | bytes 2228224 | tf_op jit(solution)/shard_map/bkv,bvw->bkw/dot_general | solution.py:51
  89.9 0.2 fusion.37
  90.1 0.1 copy.6
  90.2 0.6 fusion.28.gram_ref
  90.8 2.9 %shard_map.47 = f32[2,16,512]{2,1,0:T(8,128)} custom-call(f32[2,16,16]{2,1,0:T(8,128)} %fusion.28.gram_ref, f32[2,16,512]{2,1,0:T(8,128)} %copy-done.4), custom_call_target="tpu_custom_call" | custom-call | tf_op jit(solution)/shard_map/pallas_call | solution.py:40
  93.7 2.0 %fusion.38.rhs_ref = f32[2,16,512]{2,1,0:T(8,128)S(1)} fusion(f32[2,16,512]{2,1,0:T(8,128)} %shard_map.47, f32[2,512,512]{2,1,0:T(8,128)S(1)} %fusion.33), kind=kOutput, calls=%fused_computation.58 | convolution fusion | flops 100663296 | bytes 2228224 | tf_op jit(solution)/shard_map/bkv,bvw->bkw/dot_general | solution.py:51
  95.7 0.2 fusion.39
  95.9 0.1 copy.7
  96.0 0.6 fusion.27.gram_ref
  96.6 0.0 copy-done.5
  96.6 2.9 %shard_map.48 = f32[2,16,512]{2,1,0:T(8,128)} custom-call(f32[2,16,16]{2,1,0:T(8,128)} %fusion.27.gram_ref, f32[2,16,512]{2,1,0:T(8,128)} %copy-done.5), custom_call_target="tpu_custom_call" | custom-call | tf_op jit(solution)/shard_map/pallas_call | solution.py:40
  99.5 4.3 %fusion.42 = f32[2,16,1024]{2,1,0:T(8,128)S(1)} fusion(f32[2,16,512]{2,1,0:T(8,128)} %shard_map.48, f32[2,512,1024]{2,1,0:T(8,128)} %copy-done.1), kind=kOutput, calls=%fused_computation.62 | convolution fusion | flops 201326592 | bytes 4390912 | tf_op jit(solution)/shard_map/bkv,bvf->bkf/dot_general | solution.py:56
  103.9 0.0 copy-done.2
  103.9 1.1 fusion.40
  105.0 0.2 fusion.41
  105.2 0.7 pad_maximum_fusion.rhs_ref
  105.9 0.1 copy.8
  106.0 0.6 fusion.26.gram_ref
  106.6 3.1 %shard_map.49 = f32[2,16,1536]{2,1,0:T(8,128)} custom-call(f32[2,16,16]{2,1,0:T(8,128)} %fusion.26.gram_ref, f32[2,16,1536]{2,1,0:T(8,128)} %pad_maximum_fusion.rhs_ref), custom_call_target="tpu_custom_call" | custom-call | tf_op jit(solution)/shard_map/pallas_call | solution.py:40
  109.7 5.8 %convert_select_fusion = bf16[2,512,1024]{2,1,0:T(8,128)(2,1)} fusion(pred[2]{0:T(512)(128)(4,1)S(1)} %broadcast_compare_fusion, f32[2,16,1536]{2,1,0:T(8,128)} %shard_map.49, pred[2,16]{1,0:T(4,128)(4,1)S(1)} %iota_compare_fusion), kind=kOutput, calls=%fused_computation.14 | convolution fusion | flops 203472896 | bytes 2295296 | tf_op jit(solution)/shard_map/bkv,bkf->bvf/dot_general | solution.py:63
  (12 shorter events, 0.0 us)
Async XLA Ops:
  0.0 79.1 %copy-start = (f32[16,1024]{1,0:T(8,128)S(1)}, f32[16,1024]{1,0:T(8,128)}, u32[]{:S(2)}) copy-start(f32[16,1024]{1,0:T(8,128)} %param.7) | copy-start | bytes 196612
  4.2 4.5 %collective-permute-start.1 = (bf16[2,512,1024]{2,1,0:T(8,128)(2,1)}, bf16[2,512,1024]{2,1,0:T(8,128)(2,1)}, u32[]{:S(2)}, u32[]{:S(2)}) collective-permute-start(bf16[2,512,1024]{2,1,0:T(8,128)(2,1)} %get-tuple-element.6), channel_id=1, source_target_pairs={{0,64},{64,0},{128,192},{192,128},{1,65},{65,1},{129,193},{193,129... | collective-permute-start | bytes 6291464 | tf_op jit(solution)/shard_map/ppermute | solution.py:91
  4.2 44.0 %copy-start.8 = (s32[2]{0:T(128)S(1)}, s32[2]{0:T(128)}, u32[]{:S(2)}) copy-start(s32[2]{0:T(128)} %param.5) | copy-start | bytes 28
  4.2 44.0 %copy-start.9 = (s32[2]{0:T(128)S(1)}, s32[2]{0:T(128)}, u32[]{:S(2)}) copy-start(s32[2]{0:T(128)} %param.6) | copy-start | bytes 28
  11.9 27.4 %collective-permute-start.2 = (bf16[2,512,1024]{2,1,0:T(8,128)(2,1)S(1)}, bf16[2,512,1024]{2,1,0:T(8,128)(2,1)}, u32[]{:S(2)}, u32[]{:S(2)}) collective-permute-start(bf16[2,512,1024]{2,1,0:T(8,128)(2,1)S(1)} %fusion), channel_id=1, source_target_pairs={{0,1},{1,128},{2,3},{3,130},{4,5},{5,132},{6,7},{7,134},{8,9},{9,1... | collective-permute-start | bytes 6291464 | tf_op jit(solution)/shard_map/ppermute | solution.py:96
  13.5 34.8 %collective-permute-start = (bf16[2,512,1024]{2,1,0:T(8,128)(2,1)S(1)}, bf16[2,512,1024]{2,1,0:T(8,128)(2,1)}, u32[]{:S(2)}, u32[]{:S(2)}) collective-permute-start(bf16[2,512,1024]{2,1,0:T(8,128)(2,1)S(1)} %get-tuple-element.5), channel_id=1, source_target_pairs={{0,64},{64,0},{128,192},{192,128},{1,65},{65,1},{129,193},{193,129... | collective-permute-start | bytes 6291464 | tf_op jit(solution)/shard_map/ppermute | solution.py:93
  39.4 27.6 %collective-permute-start.3 = (bf16[2,512,1024]{2,1,0:T(8,128)(2,1)}, bf16[2,512,1024]{2,1,0:T(8,128)(2,1)}, u32[]{:S(2)}, u32[]{:S(2)}) collective-permute-start(bf16[2,512,1024]{2,1,0:T(8,128)(2,1)} %collective-permute-done.2), channel_id=1, source_target_pairs={{0,1},{1,128},{2,3},{3,130},{4,5},{5,132},{6,7},{7,134},{8,9},{9,1... | collective-permute-start | bytes 6291464 | tf_op jit(solution)/shard_map/ppermute | solution.py:97
  72.2 6.9 %copy-start.1 = (f32[2,512,1024]{2,1,0:T(8,128)}, f32[2,512,1024]{2,1,0:T(8,128)S(1)}, u32[]{:S(2)}) copy-start(f32[2,512,1024]{2,1,0:T(8,128)S(1)} %fusion.3) | copy-start | bytes 12582916
  84.1 0.9 copy-start.3
  87.9 2.0 %copy-start.6 = (f32[2,16,512]{2,1,0:T(8,128)S(1)}, f32[2,16,512]{2,1,0:T(8,128)}, u32[]{:S(2)}) copy-start(f32[2,16,512]{2,1,0:T(8,128)} %shard_map.46) | copy-start | bytes 196612
  89.9 0.9 copy-start.4
  93.7 2.0 %copy-start.7 = (f32[2,16,512]{2,1,0:T(8,128)S(1)}, f32[2,16,512]{2,1,0:T(8,128)}, u32[]{:S(2)}) copy-start(f32[2,16,512]{2,1,0:T(8,128)} %shard_map.47) | copy-start | bytes 196612
  95.7 0.9 copy-start.5
  99.5 4.3 %copy-start.2 = (f32[2,16,512]{2,1,0:T(8,128)S(1)}, f32[2,16,512]{2,1,0:T(8,128)}, u32[]{:S(2)}) copy-start(f32[2,16,512]{2,1,0:T(8,128)} %shard_map.48) | copy-start | bytes 196612

commit v4 on v3

--- a/solution.py
+++ b/solution.py
@@ -7,7 +7,7 @@
 from jax.sharding import PartitionSpec as P
 
 ITERS = 4
-HI = lax.Precision.HIGHEST
+HI = lax.Precision.HIGH
 
 
 def spectral_table(length):
@@ -22,17 +22,19 @@
 
 
 def factor_solve_kernel(gram_ref, rhs_ref, out_ref):
-    for item in range(gram_ref.shape[0]):
-        gram = gram_ref[item]
-        work = rhs_ref[item]
-        for col in range(gram.shape[0]):
+    items = range(gram_ref.shape[0])
+    grams = [gram_ref[item] for item in items]
+    works = [rhs_ref[item] for item in items]
+    for col in range(grams[0].shape[0]):
+        for item in items:
+            gram, work = grams[item], works[item]
             scale = 1.0 / jnp.sqrt(gram[col:col + 1, col:col + 1])
             column = gram[:, col:col + 1] * scale
             row = gram[col:col + 1, :] * scale
             solved = work[col:col + 1, :] * scale
             out_ref[item, col:col + 1, :] = solved
-            gram = gram - column * row
-            work = work - column * solved
+            grams[item] = gram - column * row
+            works[item] = work - column * solved
 
 
 def factor_solve(inner_gram, rhs):

time: 116 us -> 106 us (0.914)
  matrix products: 33.2 us -> 23.1 us
    dot_general x1, matrix products: 6.91 us -> 3.65 us  [denoise_batch(): kernel = jnp.einsum('bvf,bwf->bvw', spectra, spectra, precision=HI)]
    dot_general x4, matrix products: 6.5 us -> 4.28 us  [denoise_batch(): pushed = jnp.einsum('bkv,bvw->bkw', coeff, kernel, precision=HI)]
    dot_general x1, matrix products: 3.61 us -> 1.73 us  [denoise_batch(): coeff = jnp.einsum('kf,bvf->bkv', start_basis, spectra, precision=HI)]
    dot_general x1, matrix products: 5.8 us -> 4.18 us  [denoise_batch(): result = jnp.einsum('bkv,bkf->bvf', coefficients, truncated, precision=HI)]
  transfers between devices with their start and end apart: 4 -> 4, of which waited for: 3 -> 3; matrix products, arithmetic and copies ran while one was open for 7% -> 8% of each run, Pallas kernels for 0% -> 0%
where the time goes in v4:
time: 106 us; the launch traced here: 105 us
  waiting for transfers between devices  47.8 us (45%)
  matrix products  23.1 us (22%)
  other arithmetic  15 us (14%)
  Pallas kernels  11.8 us (11%)
  local copies, waits for them, and re-layouts  4.58 us (4%)
  starting transfers between devices  2.98 us (3%)
    ppermute x1, waiting for transfers between devices, coil_sum(): hop = lax.ppermute(forward, ('coil', 'slab'), pairs)  24.7 us
    ppermute x1, waiting for transfers between devices, coil_sum(): hop = lax.ppermute(hop, ('coil', 'slab'), pairs)  18.6 us
    pallas_call x4, Pallas kernels, factor_solve(): pl.pallas_call(factor_solve_kernel, out_shape=jax.ShapeDtypeStruct(rhs.sh...  11.8 us
    another operation x2, other arithmetic  8.56 us
    dot_general x1, matrix products, denoise_batch(): jnp.einsum('bvt,tf->bvf', patches, transform, preferred_element_type=jnp....  5.24 us
    ppermute x1, waiting for transfers between devices, coil_sum(): got_forward = lax.ppermute(pick(coil ^ 3), 'coil', chip_pair)  4.49 us
    dot_general x4, matrix products, denoise_batch(): pushed = jnp.einsum('bkv,bvw->bkw', coeff, kernel, precision=HI)  4.28 us
    squeeze x1, local copies, waits for them, and re-layouts, pick(): return lax.dynamic_index_in_dim(parts, o, 0, keepdims=False)  4.23 us
  transfers between devices with their start and end apart: 4, of which 3 were waited for; matrix products, arithmetic and copies ran while one was open for 8% of the time, Pallas kernels for 0%

profile of v4, /device:TPU:64, one launch (start us, length us, event | category | flops | bytes accessed | tf_op | source)
XLA Modules:
  0.0 105.4 jit_solution(15603044399555557868)
XLA Ops:
  0.0 0.0 copy-start
  0.0 4.2 %dynamic-slice_bitcast_fusion.1 = (bf16[2,512,1024]{2,1,0:T(8,128)(2,1)S(1)}, bf16[2,512,1024]{2,1,0:T(8,128)(2,1)}) fusion(bf16[1,4,2,512,1024]{4,3,2,1,0:T(8,128)(2,1)} %param.4, s32[]{:T(128)S(6)} %select_n.39, s32[]{:T(128)S(6)} %select_n.41), kind=kLoop, calls=%fused_computation.16 | loop fusion | bytes 8388616 | tf_op jit(solution)/shard_map/jit(dynamic_index_in_dim)/squeeze | solution.py:91
  4.2 0.0 collective-permute-start.1
  4.2 4.5 %collective-permute-done.1 = bf16[2,512,1024]{2,1,0:T(8,128)(2,1)} collective-permute-done((bf16[2,512,1024]{2,1,0:T(8,128)(2,1)}, bf16[2,512,1024]{2,1,0:T(8,128)(2,1)}, u32[]{:S(2)}, u32[]{:S(2)}) %collective-permute-start.1) | collective-permute-done | bytes 2097184 | tf_op jit(solution)/shard_map/ppermute | solution.py:93
  8.7 3.2 %fusion = bf16[2,512,1024]{2,1,0:T(8,128)(2,1)S(1)} fusion(bf16[2,512,1024]{2,1,0:T(8,128)(2,1)} %collective-permute-done.1, bf16[1,4,2,512,1024]{4,3,2,1,0:T(8,128)(2,1)} %param.4, s32[]{:T(128)S(6)} %select_n.40), kind=kLoop, calls=%fused_computation.1 | loop fusion | flops 4194304 | bytes 6291460 | tf_op jit(solution)/shard_map/convert_element_type | solution.py:94
  11.9 1.6 %collective-permute-start.2 = (bf16[2,512,1024]{2,1,0:T(8,128)(2,1)S(1)}, bf16[2,512,1024]{2,1,0:T(8,128)(2,1)}, u32[]{:S(2)}, u32[]{:S(2)}) collective-permute-start(bf16[2,512,1024]{2,1,0:T(8,128)(2,1)S(1)} %fusion), channel_id=1, source_target_pairs={{0,1},{1,128},{2,3},{3,130},{4,5},{5,132},{6,7},{7,134},{8,9},{9,1... | collective-permute-start | bytes 6291464 | tf_op jit(solution)/shard_map/ppermute | solution.py:98
  13.5 1.1 %collective-permute-start = (bf16[2,512,1024]{2,1,0:T(8,128)(2,1)S(1)}, bf16[2,512,1024]{2,1,0:T(8,128)(2,1)}, u32[]{:S(2)}, u32[]{:S(2)}) collective-permute-start(bf16[2,512,1024]{2,1,0:T(8,128)(2,1)S(1)} %get-tuple-element.5), channel_id=1, source_target_pairs={{0,64},{64,0},{128,192},{192,128},{1,65},{65,1},{129,193},{193,129... | collective-permute-start | bytes 6291464 | tf_op jit(solution)/shard_map/ppermute | solution.py:95
  14.6 24.7 %collective-permute-done.2 = bf16[2,512,1024]{2,1,0:T(8,128)(2,1)} collective-permute-done((bf16[2,512,1024]{2,1,0:T(8,128)(2,1)S(1)}, bf16[2,512,1024]{2,1,0:T(8,128)(2,1)}, u32[]{:S(2)}, u32[]{:S(2)}) %collective-permute-start.2) | collective-permute-done | bytes 2097184 | tf_op jit(solution)/shard_map/ppermute | solution.py:98
  39.4 0.3 collective-permute-start.3
  39.6 4.0 %fusion.19 = bf16[512,512]{1,0:T(8,128)(2,1)S(1)} fusion(), kind=kLoop, calls=%fused_computation.30 | loop fusion | flops 4194304 | bytes 524288 | tf_op jit(solution)/shard_map/convert.4
  43.6 4.6 %negate_convert_fusion = (bf16[512,512]{1,0:T(8,128)(2,1)S(1)}, bf16[512,512]{1,0:T(8,128)(2,1)S(1)}) fusion(), kind=kLoop, calls=%fused_computation.24 | loop fusion | flops 4980736 | bytes 1048576 | tf_op jit(solution)/shard_map/convert.7
  48.2 0.0 copy-done.8
  48.2 0.0 copy-done.9
  48.3 0.1 iota_compare_fusion
  48.3 0.0 collective-permute-done
  48.3 18.6 %collective-permute-done.3 = bf16[2,512,1024]{2,1,0:T(8,128)(2,1)} collective-permute-done((bf16[2,512,1024]{2,1,0:T(8,128)(2,1)}, bf16[2,512,1024]{2,1,0:T(8,128)(2,1)}, u32[]{:S(2)}, u32[]{:S(2)}) %collective-permute-start.3) | collective-permute-done | bytes 2097184 | tf_op jit(solution)/shard_map/ppermute | solution.py:99
  66.9 5.2 %fusion.3 = f32[2,512,1024]{2,1,0:T(8,128)S(1)} fusion(bf16[2,512,1024]{2,1,0:T(8,128)(2,1)} %collective-permute-done.3, bf16[2,512,1024]{2,1,0:T(8,128)(2,1)} %collective-permute-done, bf16[512,512]{1,0:T(8,128)(2,1)S(1)} %get-tuple-element.8, bf16[512,512]{1,0:T(8,128)(2,1)S(1)} %fusion.19, bf16[512,512]{1,0:T(8,128)(2,1)S(1)} %get-tuple-element.7, ...), kind=kOutput, calls=%fused_computation.5 | convolution fusion | flops 2162163712 | bytes 12058628 | tf_op jit(solution)/shard_map/bvt,tf->bvf/dot_general | solution.py:49
  72.2 0.0 copy-start.1
  72.2 3.7 %fusion.33 = f32[2,512,512]{2,1,0:T(8,128)S(1)} fusion(f32[2,512,1024]{2,1,0:T(8,128)S(1)} %fusion.3), kind=kOutput, calls=%fused_computation.53 | convolution fusion | flops 3221225472 | bytes 6291456 | tf_op jit(solution)/shard_map/bvf,bwf->bvw/dot_general | solution.py:50
  75.8 0.0 copy-done.1
  75.9 0.0 copy-done
  75.9 1.7 %fusion.20 = f32[2,512,16]{1,2,0:T(8,128)S(1)} fusion(f32[2,512,1024]{2,1,0:T(8,128)S(1)} %fusion.3, f32[16,1024]{1,0:T(8,128)S(1)} %copy-done), kind=kOutput, calls=%fused_computation.34 | convolution fusion | flops 100663296 | bytes 4325376 | tf_op jit(solution)/shard_map/kf,bvf->bkv/dot_general | solution.py:51
  77.6 0.6 fusion.34.rhs_ref
  78.2 0.2 fusion.35
  78.4 0.1 copy.5
  78.5 0.6 fusion.29.gram_ref
  79.1 0.0 copy-done.3
  79.1 2.9 %shard_map.46 = f32[2,16,512]{2,1,0:T(8,128)} custom-call(f32[2,16,16]{2,1,0:T(8,128)} %fusion.29.gram_ref, f32[2,16,512]{2,1,0:T(8,128)} %copy-done.3), custom_call_target="tpu_custom_call" | custom-call | tf_op jit(solution)/shard_map/pallas_call | solution.py:42
  82.0 1.5 %fusion.36.rhs_ref = f32[2,16,512]{2,1,0:T(8,128)S(1)} fusion(f32[2,16,512]{2,1,0:T(8,128)} %shard_map.46, f32[2,512,512]{2,1,0:T(8,128)S(1)} %fusion.33), kind=kOutput, calls=%fused_computation.56 | convolution fusion | flops 50331648 | bytes 2228224 | tf_op jit(solution)/shard_map/bkv,bvw->bkw/dot_general | solution.py:53
  83.5 0.0 copy-start.4
  83.5 0.2 fusion.37
  83.7 0.1 copy.6
  83.7 0.6 fusion.28.gram_ref
  84.4 2.9 %shard_map.47 = f32[2,16,512]{2,1,0:T(8,128)} custom-call(f32[2,16,16]{2,1,0:T(8,128)} %fusion.28.gram_ref, f32[2,16,512]{2,1,0:T(8,128)} %copy-done.4), custom_call_target="tpu_custom_call" | custom-call | tf_op jit(solution)/shard_map/pallas_call | solution.py:42
  87.3 1.5 %fusion.38.rhs_ref = f32[2,16,512]{2,1,0:T(8,128)S(1)} fusion(f32[2,16,512]{2,1,0:T(8,128)} %shard_map.47, f32[2,512,512]{2,1,0:T(8,128)S(1)} %fusion.33), kind=kOutput, calls=%fused_computation.58 | convolution fusion | flops 50331648 | bytes 2228224 | tf_op jit(solution)/shard_map/bkv,bvw->bkw/dot_general | solution.py:53
  88.8 0.0 copy-start.5
  88.8 0.2 fusion.39
  88.9 0.1 copy.7
  89.0 0.6 fusion.27.gram_ref
  89.6 2.9 %shard_map.48 = f32[2,16,512]{2,1,0:T(8,128)} custom-call(f32[2,16,16]{2,1,0:T(8,128)} %fusion.27.gram_ref, f32[2,16,512]{2,1,0:T(8,128)} %copy-done.5), custom_call_target="tpu_custom_call" | custom-call | tf_op jit(solution)/shard_map/pallas_call | solution.py:42
  92.5 3.4 %fusion.42 = f32[2,16,1024]{2,1,0:T(8,128)S(1)} fusion(f32[2,16,512]{2,1,0:T(8,128)} %shard_map.48, f32[2,512,1024]{2,1,0:T(8,128)} %copy-done.1), kind=kOutput, calls=%fused_computation.62 | convolution fusion | flops 100663296 | bytes 4390912 | tf_op jit(solution)/shard_map/bkv,bvf->bkf/dot_general | solution.py:58
  95.9 0.6 fusion.40
  96.6 0.2 fusion.41
  96.7 0.7 pad_maximum_fusion.rhs_ref
  97.4 0.1 copy.8
  97.5 0.6 fusion.26.gram_ref
  98.1 3.1 %shard_map.49 = f32[2,16,1536]{2,1,0:T(8,128)} custom-call(f32[2,16,16]{2,1,0:T(8,128)} %fusion.26.gram_ref, f32[2,16,1536]{2,1,0:T(8,128)} %pad_maximum_fusion.rhs_ref), custom_call_target="tpu_custom_call" | custom-call | tf_op jit(solution)/shard_map/pallas_call | solution.py:42
  101.2 4.2 %convert_select_fusion = bf16[2,512,1024]{2,1,0:T(8,128)(2,1)} fusion(pred[2]{0:T(512)(128)(4,1)S(1)} %broadcast_compare_fusion, f32[2,16,1536]{2,1,0:T(8,128)} %shard_map.49, pred[2,16]{1,0:T(4,128)(4,1)S(1)} %iota_compare_fusion), kind=kOutput, calls=%fused_computation.14 | convolution fusion | flops 102809600 | bytes 2295296 | tf_op jit(solution)/shard_map/bkv,bkf->bvf/dot_general | solution.py:65
  (12 shorter events, 0.0 us)
Async XLA Ops:
  0.0 75.9 %copy-start = (f32[16,1024]{1,0:T(8,128)S(1)}, f32[16,1024]{1,0:T(8,128)}, u32[]{:S(2)}) copy-start(f32[16,1024]{1,0:T(8,128)} %param.7) | copy-start | bytes 196612
  4.2 4.5 %collective-permute-start.1 = (bf16[2,512,1024]{2,1,0:T(8,128)(2,1)}, bf16[2,512,1024]{2,1,0:T(8,128)(2,1)}, u32[]{:S(2)}, u32[]{:S(2)}) collective-permute-start(bf16[2,512,1024]{2,1,0:T(8,128)(2,1)} %get-tuple-element.6), channel_id=1, source_target_pairs={{0,64},{64,0},{128,192},{192,128},{1,65},{65,1},{129,193},{193,129... | collective-permute-start | bytes 6291464 | tf_op jit(solution)/shard_map/ppermute | solution.py:93
  4.2 44.0 %copy-start.8 = (s32[2]{0:T(128)S(1)}, s32[2]{0:T(128)}, u32[]{:S(2)}) copy-start(s32[2]{0:T(128)} %param.5) | copy-start | bytes 28
  4.2 44.0 %copy-start.9 = (s32[2]{0:T(128)S(1)}, s32[2]{0:T(128)}, u32[]{:S(2)}) copy-start(s32[2]{0:T(128)} %param.6) | copy-start | bytes 28
  11.9 27.4 %collective-permute-start.2 = (bf16[2,512,1024]{2,1,0:T(8,128)(2,1)S(1)}, bf16[2,512,1024]{2,1,0:T(8,128)(2,1)}, u32[]{:S(2)}, u32[]{:S(2)}) collective-permute-start(bf16[2,512,1024]{2,1,0:T(8,128)(2,1)S(1)} %fusion), channel_id=1, source_target_pairs={{0,1},{1,128},{2,3},{3,130},{4,5},{5,132},{6,7},{7,134},{8,9},{9,1... | collective-permute-start | bytes 6291464 | tf_op jit(solution)/shard_map/ppermute | solution.py:98
  13.5 34.8 %collective-permute-start = (bf16[2,512,1024]{2,1,0:T(8,128)(2,1)S(1)}, bf16[2,512,1024]{2,1,0:T(8,128)(2,1)}, u32[]{:S(2)}, u32[]{:S(2)}) collective-permute-start(bf16[2,512,1024]{2,1,0:T(8,128)(2,1)S(1)} %get-tuple-element.5), channel_id=1, source_target_pairs={{0,64},{64,0},{128,192},{192,128},{1,65},{65,1},{129,193},{193,129... | collective-permute-start | bytes 6291464 | tf_op jit(solution)/shard_map/ppermute | solution.py:95
  39.4 27.6 %collective-permute-start.3 = (bf16[2,512,1024]{2,1,0:T(8,128)(2,1)}, bf16[2,512,1024]{2,1,0:T(8,128)(2,1)}, u32[]{:S(2)}, u32[]{:S(2)}) collective-permute-start(bf16[2,512,1024]{2,1,0:T(8,128)(2,1)} %collective-permute-done.2), channel_id=1, source_target_pairs={{0,1},{1,128},{2,3},{3,130},{4,5},{5,132},{6,7},{7,134},{8,9},{9,1... | collective-permute-start | bytes 6291464 | tf_op jit(solution)/shard_map/ppermute | solution.py:99
  72.2 3.7 %copy-start.1 = (f32[2,512,1024]{2,1,0:T(8,128)}, f32[2,512,1024]{2,1,0:T(8,128)S(1)}, u32[]{:S(2)}) copy-start(f32[2,512,1024]{2,1,0:T(8,128)S(1)} %fusion.3) | copy-start | bytes 12582916
  78.2 0.9 copy-start.3
  82.0 1.5 %copy-start.6 = (f32[2,16,512]{2,1,0:T(8,128)S(1)}, f32[2,16,512]{2,1,0:T(8,128)}, u32[]{:S(2)}) copy-start(f32[2,16,512]{2,1,0:T(8,128)} %shard_map.46) | copy-start | bytes 196612
  83.5 0.9 copy-start.4
  87.3 1.5 %copy-start.7 = (f32[2,16,512]{2,1,0:T(8,128)S(1)}, f32[2,16,512]{2,1,0:T(8,128)}, u32[]{:S(2)}) copy-start(f32[2,16,512]{2,1,0:T(8,128)} %shard_map.47) | copy-start | bytes 196612
  88.8 0.9 copy-start.5
  92.5 3.4 %copy-start.2 = (f32[2,16,512]{2,1,0:T(8,128)S(1)}, f32[2,16,512]{2,1,0:T(8,128)}, u32[]{:S(2)}) copy-start(f32[2,16,512]{2,1,0:T(8,128)} %shard_map.48) | copy-start | bytes 196612

commit v5 on v4

--- a/solution.py
+++ b/solution.py
@@ -83,28 +83,41 @@
 
 
 def coil_sum(partial_time, n_coil, n_slab):
-    parts = partial_time[0]
     coil = lax.axis_index("coil")
     chip_pair = [(i, i ^ 1) for i in range(n_coil)]
+    pairs = ring_pairs(n_coil, n_slab)
+    sums = []
+    arrived = None
+    for q in range(partial_time.shape[2]):
+        parts = partial_time[0, :, q]
 
-    def pick(o):
-        return lax.dynamic_index_in_dim(parts, o, 0, keepdims=False)
+        def pick(o):
+            return lax.dynamic_index_in_dim(parts, o, 0, keepdims=False)
 
-    got_forward = lax.ppermute(pick(coil ^ 3), "coil", chip_pair)
-    forward = (pick(coil ^ 2).astype(jnp.float32) + got_forward.astype(jnp.float32)).astype(jnp.bfloat16)
-    got_own = lax.ppermute(pick(coil ^ 1), "coil", chip_pair)
-    own = pick(coil).astype(jnp.float32) + got_own.astype(jnp.float32)
-    pairs = ring_pairs(n_coil, n_slab)
-    hop = lax.ppermute(forward, ("coil", "slab"), pairs)
-    hop = lax.ppermute(hop, ("coil", "slab"), pairs)
-    return (own + hop.astype(jnp.float32)).astype(jnp.bfloat16)
+        got_forward = lax.ppermute(pick(coil ^ 3), "coil", chip_pair)
+        forward = (pick(coil ^ 2).astype(jnp.float32) + got_forward.astype(jnp.float32)).astype(jnp.bfloat16)
+        got_own = lax.ppermute(pick(coil ^ 1), "coil", chip_pair)
+        own = pick(coil).astype(jnp.float32) + got_own.astype(jnp.float32)
+        if arrived is not None:
+            forward, arrived = lax.optimization_barrier((forward, arrived))
+            sums[-1] = (sums[-1][0], arrived)
+        hop = lax.ppermute(forward, ("coil", "slab"), pairs)
+        hop = lax.ppermute(hop, ("coil", "slab"), pairs)
+        arrived = hop
+        sums.append((own, hop))
+    return sums
 
 
 def make_body(n_coil, n_slab):
     def body(partial_time, brain_mask, rank_limit, start_basis):
-        patches = coil_sum(partial_time, n_coil, n_slab)
-        transform = spectral_table(patches.shape[-1] // 2)
-        return denoise_batch(patches, brain_mask > 0, rank_limit, transform, start_basis)
+        transform = spectral_table(partial_time.shape[-1] // 2)
+        flags = brain_mask > 0
+        pieces = coil_sum(partial_time, n_coil, n_slab)
+        outs = []
+        for q, (own, hop) in enumerate(pieces):
+            patch = (own + hop.astype(jnp.float32)).astype(jnp.bfloat16)
+            outs.append(denoise_batch(patch[None], flags[q:q + 1], rank_limit[q:q + 1], transform, start_basis))
+        return jnp.concatenate(outs, axis=0)
 
     return body
 

time: 106 us -> 122 us (1.15)
  waiting for transfers between devices: 47.8 us -> 26.7 us
  Pallas kernels: 11.8 us -> 22.3 us
  matrix products: 23.1 us -> 32.3 us
  other arithmetic: 15 us -> 23 us
  local copies, waits for them, and re-layouts: 4.58 us -> 12.4 us
    ppermute x1 -> x2, waiting for transfers between devices: 18.6 us -> 7.66 us  [coil_sum(): hop = lax.ppermute(hop, ('coil', 'slab'), pairs)]
    pallas_call x4 -> x8, Pallas kernels: 11.8 us -> 22.3 us  [factor_solve(): pl.pallas_call(factor_solve_kernel, out_shape=jax.ShapeDtypeStruct(rhs.sh...]
    ppermute x1 -> x2, waiting for transfers between devices: 24.7 us -> 16.4 us  [coil_sum(): hop = lax.ppermute(forward, ('coil', 'slab'), pairs)]
    slice x0 -> x3, local copies, waits for them, and re-layouts: none -> 7.27 us  [the longest x1 6.05 us: coil_sum(): parts = partial_time[0, :, q]]
    dot_general x4 -> x8, matrix products: 0.64 us -> 4.89 us  [denoise_batch(): inner_gram = jnp.einsum('bkw,bjw->bkj', pushed, coeff, precision=HI)]
    mul x4 -> x8, other arithmetic: 2.47 us -> 5.01 us  [factor_solve(): sym = 0.5 * (inner_gram + jnp.swapaxes(inner_gram, -1, -2))]
    convert_element_type x1 -> x2, other arithmetic: 3.19 us -> 5.61 us  [coil_sum(): (pick(coil ^ 2).astype(jnp.float32) + got_forward.astype(jnp.float32)).as...]
    dot_general x4 -> x8, matrix products: 4.28 us -> 6.68 us  [denoise_batch(): pushed = jnp.einsum('bkv,bvw->bkw', coeff, kernel, precision=HI)]
  transfers between devices with their start and end apart: 4 -> 8, of which waited for: 3 -> 5; matrix products, arithmetic and copies ran while one was open for 8% -> 31% of each run, Pallas kernels for 0% -> 9%
where the time goes in v5:
time: 122 us; the launch traced here: 121 us
  matrix products  32.3 us (26%)
  waiting for transfers between devices  26.7 us (22%)
  other arithmetic  23 us (19%)
  Pallas kernels  22.3 us (18%)
  local copies, waits for them, and re-layouts  12.4 us (10%)
  starting transfers between devices  3.73 us (3%)
    pallas_call x8, Pallas kernels, factor_solve(): pl.pallas_call(factor_solve_kernel, out_shape=jax.ShapeDtypeStruct(rhs.sh...  22.3 us
    ppermute x2, waiting for transfers between devices, coil_sum(): hop = lax.ppermute(forward, ('coil', 'slab'), pairs)  16.4 us
    another operation x2, other arithmetic  8.38 us
    ppermute x2, waiting for transfers between devices, coil_sum(): hop = lax.ppermute(hop, ('coil', 'slab'), pairs)  7.66 us
    dot_general x8, matrix products, denoise_batch(): pushed = jnp.einsum('bkv,bvw->bkw', coeff, kernel, precision=HI)  6.68 us
    dot_general x2, matrix products, denoise_batch(): jnp.einsum('bvt,tf->bvf', patches, transform, preferred_element_type=jnp....  6.24 us
    dot_general x2, matrix products, denoise_batch(): result = jnp.einsum('bkv,bkf->bvf', coefficients, truncated, precision=HI)  6.13 us
    slice x1, local copies, waits for them, and re-layouts, coil_sum(): parts = partial_time[0, :, q]  6.05 us
  transfers between devices with their start and end apart: 8, of which 5 were waited for; matrix products, arithmetic and copies ran while one was open for 31% of the time, Pallas kernels for 9%

profile of v5, /device:TPU:64, one launch (start us, length us, event | category | flops | bytes accessed | tf_op | source)
XLA Modules:
  0.0 120.6 jit_solution(15891086967565122204)
XLA Ops:
  0.0 6.1 %fusion.81 = (bf16[1,4,1,512,1024]{4,3,2,1,0:T(8,128)(2,1)}, bf16[1,4,1,512,1024]{4,3,2,1,0:T(8,128)(2,1)}) fusion(bf16[1,4,2,512,1024]{4,3,2,1,0:T(8,128)(2,1)} %param.4), kind=kLoop, calls=%fused_computation.112 | loop fusion | bytes 16777216 | tf_op jit(solution)/shard_map/slice | solution.py:92
  6.1 1.7 %dynamic-slice_bitcast_fusion.3 = (bf16[512,1024]{1,0:T(8,128)(2,1)S(1)}, bf16[512,1024]{1,0:T(8,128)(2,1)S(1)}) fusion(bf16[1,4,1,512,1024]{4,3,2,1,0:T(8,128)(2,1)} %get-tuple-element.9, s32[]{:T(128)S(6)} %select_n.58, s32[]{:T(128)S(6)} %select_n.60), kind=kLoop, calls=%fused_computation.39 | loop fusion | bytes 4194312 | tf_op jit(solution)/shard_map/jit(dynamic_index_in_dim)/squeeze | solution.py:95
  7.9 2.6 %collective-permute-done.2 = bf16[512,1024]{1,0:T(8,128)(2,1)S(1)} collective-permute-done((bf16[512,1024]{1,0:T(8,128)(2,1)S(1)}, bf16[512,1024]{1,0:T(8,128)(2,1)S(1)}, u32[]{:S(2)}, u32[]{:S(2)}) %collective-permute-start.2) | collective-permute-done | bytes 1048608 | tf_op jit(solution)/shard_map/ppermute | solution.py:97
  10.5 2.6 %fusion.2 = bf16[512,1024]{1,0:T(8,128)(2,1)} fusion(bf16[512,1024]{1,0:T(8,128)(2,1)S(1)} %collective-permute-done.2, bf16[1,4,1,512,1024]{4,3,2,1,0:T(8,128)(2,1)} %get-tuple-element.9, s32[]{:T(128)S(6)} %select_n.59), kind=kLoop, calls=%fused_computation.6 | loop fusion | flops 2097152 | bytes 3145732 | tf_op jit(solution)/shard_map/convert_element_type | solution.py:98
  13.1 1.5 %collective-permute-start.3 = (bf16[512,1024]{1,0:T(8,128)(2,1)}, bf16[512,1024]{1,0:T(8,128)(2,1)}, u32[]{:S(2)}, u32[]{:S(2)}) collective-permute-start(bf16[512,1024]{1,0:T(8,128)(2,1)} %fusion.2), channel_id=1, source_target_pairs={{0,1},{1,128},{2,3},{3,130},{4,5},{5,132},{6,7},{7,134},{8,9},{9,1... | collective-permute-start | bytes 3145736 | tf_op jit(solution)/shard_map/ppermute | solution.py:104
  14.6 2.7 %dynamic-slice_bitcast_fusion = (bf16[512,1024]{1,0:T(8,128)(2,1)}, bf16[512,1024]{1,0:T(8,128)(2,1)S(1)}) fusion(bf16[1,4,1,512,1024]{4,3,2,1,0:T(8,128)(2,1)} %get-tuple-element.10, s32[]{:T(128)S(6)} %select_n.58, s32[]{:T(128)S(6)} %select_n.60), kind=kLoop, calls=%fused_computation.30 | loop fusion | bytes 4194312 | tf_op jit(solution)/shard_map/jit(dynamic_index_in_dim)/squeeze | solution.py:95
  17.3 1.1 collective-permute-start.1
  19.0 0.6 fusion.82
  19.6 9.8 %collective-permute-done.3 = bf16[512,1024]{1,0:T(8,128)(2,1)} collective-permute-done((bf16[512,1024]{1,0:T(8,128)(2,1)}, bf16[512,1024]{1,0:T(8,128)(2,1)}, u32[]{:S(2)}, u32[]{:S(2)}) %collective-permute-start.3) | collective-permute-done | bytes 1048608 | tf_op jit(solution)/shard_map/ppermute | solution.py:104
  31.6 4.0 %fusion.24 = bf16[512,512]{1,0:T(8,128)(2,1)S(1)} fusion(), kind=kLoop, calls=%fused_computation.42 | loop fusion | flops 4194304 | bytes 524288 | tf_op jit(solution)/shard_map/convert.6
  35.6 4.4 %negate_convert_fusion = (bf16[512,512]{1,0:T(8,128)(2,1)S(1)}, bf16[512,512]{1,0:T(8,128)(2,1)S(1)}) fusion(), kind=kLoop, calls=%fused_computation.32 | loop fusion | flops 4980736 | bytes 1048576 | tf_op jit(solution)/shard_map/convert.9
  40.0 3.0 %fusion.3 = bf16[512,1024]{1,0:T(8,128)(2,1)} fusion(bf16[512,1024]{1,0:T(8,128)(2,1)S(1)} %collective-permute-done.1, bf16[1,4,1,512,1024]{4,3,2,1,0:T(8,128)(2,1)} %get-tuple-element.10, s32[]{:T(128)S(6)} %select_n.59), kind=kLoop, calls=%fused_computation.8 | loop fusion | flops 2097152 | bytes 3145732 | tf_op jit(solution)/shard_map/convert_element_type | solution.py:98
  43.0 2.7 %collective-permute-done.4 = bf16[512,1024]{1,0:T(8,128)(2,1)S(1)} collective-permute-done((bf16[512,1024]{1,0:T(8,128)(2,1)}, bf16[512,1024]{1,0:T(8,128)(2,1)S(1)}, u32[]{:S(2)}, u32[]{:S(2)}) %collective-permute-start.4) | collective-permute-done | bytes 1048608 | tf_op jit(solution)/shard_map/ppermute | solution.py:105
  45.7 2.8 %fusion.13 = f32[512,1024]{1,0:T(8,128)S(1)} fusion(bf16[512,1024]{1,0:T(8,128)(2,1)S(1)} %collective-permute-done.4, bf16[512,1024]{1,0:T(8,128)(2,1)} %collective-permute-done, bf16[1,4,1,512,1024]{4,3,2,1,0:T(8,128)(2,1)} %get-tuple-element.9, s32[]{:T(128)S(6)} %select_n.57, bf16[512,512]{1,0:T(8,128)(2,1)S(1)} %get-tuple-element.20, ...), kind=kOutput, calls=%fused_computation.26 | convolution fusion | flops 1085276160 | bytes 6815748 | tf_op jit(solution)/shard_map/bvt,tf->bvf/dot_general | solution.py:49
  48.6 1.8 %fusion.85 = f32[512,512]{1,0:T(8,128)S(1)} fusion(f32[512,1024]{1,0:T(8,128)S(1)} %fusion.13), kind=kOutput, calls=%fused_computation.116 | convolution fusion | flops 1610612736 | bytes 3145728 | tf_op jit(solution)/shard_map/bvf,bwf->bvw/dot_general | solution.py:50
  50.4 0.9 fusion.84
  51.9 0.6 fusion.74.gram_ref
  52.6 2.7 %shard_map.46 = f32[1,16,512]{2,1,0:T(8,128)} custom-call(f32[1,16,16]{2,1,0:T(8,128)} %fusion.74.gram_ref, f32[1,16,512]{2,1,0:T(8,128)} %bitcast.171), custom_call_target="tpu_custom_call" | custom-call | tf_op jit(solution)/shard_map/pallas_call | solution.py:42
  55.3 1.1 fusion.57
  56.7 0.9 fusion.55
  58.2 2.7 %shard_map.47 = f32[1,16,512]{2,1,0:T(8,128)} custom-call(f32[1,16,16]{2,1,0:T(8,128)} %fusion.73.gram_ref, f32[1,16,512]{2,1,0:T(8,128)} %bitcast.170), custom_call_target="tpu_custom_call" | custom-call | tf_op jit(solution)/shard_map/pallas_call | solution.py:42
  61.0 1.1 fusion.53
  62.1 0.9 fusion.51
  63.7 2.7 %shard_map.48 = f32[1,16,512]{2,1,0:T(8,128)} custom-call(f32[1,16,16]{2,1,0:T(8,128)} %fusion.72.gram_ref, f32[1,16,512]{2,1,0:T(8,128)} %bitcast.172), custom_call_target="tpu_custom_call" | custom-call | tf_op jit(solution)/shard_map/pallas_call | solution.py:42
  66.5 6.5 %collective-permute-done.6 = bf16[512,1024]{1,0:T(8,128)(2,1)} collective-permute-done((bf16[512,1024]{1,0:T(8,128)(2,1)}, bf16[512,1024]{1,0:T(8,128)(2,1)}, u32[]{:S(2)}, u32[]{:S(2)}) %collective-permute-start.6) | collective-permute-done | bytes 1048608 | tf_op jit(solution)/shard_map/ppermute | solution.py:104
  73.0 1.1 fusion.49
  74.1 1.0 fusion.47
  75.1 1.4 %convolution_bitcast_fusion.1 = f32[1,16,1024]{2,1,0:T(8,128)S(1)} fusion(f32[512,1024]{1,0:T(8,128)S(1)} %fusion.13, f32[1,16,512]{2,1,0:T(8,128)} %shard_map.48), kind=kOutput, calls=%fused_computation.22 | convolution fusion | flops 50331648 | bytes 2195456 | tf_op jit(solution)/shard_map/bkv,bvf->bkf/dot_general | solution.py:58
  77.1 0.6 pad_maximum_fusion.1.rhs_ref
  77.8 2.9 %shard_map.49 = f32[1,16,1536]{2,1,0:T(8,128)} custom-call(f32[1,16,16]{2,1,0:T(8,128)} %fusion.71.gram_ref, f32[1,16,1536]{2,1,0:T(8,128)} %pad_maximum_fusion.1.rhs_ref), custom_call_target="tpu_custom_call" | custom-call | tf_op jit(solution)/shard_map/pallas_call | solution.py:42
  80.7 3.6 %fusion.7 = bf16[1,512,1024]{2,1,0:T(8,128)(2,1)} fusion(pred[]{:T(512)} %bitcast, f32[1,16,1536]{2,1,0:T(8,128)} %shard_map.49, pred[16]{0:T(512)(128)(4,1)S(1)} %iota_compare_fusion.1), kind=kOutput, calls=%fused_computation.18 | convolution fusion | flops 51404800 | bytes 1147905 | tf_op jit(solution)/shard_map/bkv,bkf->bvf/dot_general | solution.py:65
  84.3 5.0 %collective-permute-done.7 = bf16[512,1024]{1,0:T(8,128)(2,1)} collective-permute-done((bf16[512,1024]{1,0:T(8,128)(2,1)}, bf16[512,1024]{1,0:T(8,128)(2,1)}, u32[]{:S(2)}, u32[]{:S(2)}) %collective-permute-start.7) | collective-permute-done | bytes 1048608 | tf_op jit(solution)/shard_map/ppermute | solution.py:105
  89.3 3.4 %fusion.15 = f32[512,1024]{1,0:T(8,128)S(1)} fusion(bf16[512,1024]{1,0:T(8,128)(2,1)} %collective-permute-done.7, bf16[512,1024]{1,0:T(8,128)(2,1)} %collective-permute-done.5, bf16[1,4,1,512,1024]{4,3,2,1,0:T(8,128)(2,1)} %get-tuple-element.10, s32[]{:T(128)S(6)} %select_n.57, bf16[512,512]{1,0:T(8,128)(2,1)} %copy-done.7, ...), kind=kOutput, calls=%fused_computation.27 | convolution fusion | flops 1085276160 | bytes 6815748 | tf_op jit(solution)/shard_map/bvt,tf->bvf/dot_general | solution.py:49
  92.7 1.8 %fusion.89 = f32[512,512]{1,0:T(8,128)S(1)} fusion(f32[512,1024]{1,0:T(8,128)S(1)} %fusion.15), kind=kOutput, calls=%fused_computation.120 | convolution fusion | flops 1610612736 | bytes 3145728 | tf_op jit(solution)/shard_map/bvf,bwf->bvw/dot_general | solution.py:50
  94.5 0.9 fusion.88
  96.7 2.7 %shard_map.50 = f32[1,16,512]{2,1,0:T(8,128)} custom-call(f32[1,16,16]{2,1,0:T(8,128)} %fusion.70.gram_ref, f32[1,16,512]{2,1,0:T(8,128)} %bitcast.173), custom_call_target="tpu_custom_call" | custom-call | tf_op jit(solution)/shard_map/pallas_call | solution.py:42
  99.4 1.1 fusion.44
  100.5 0.9 fusion.42
  102.1 2.7 %shard_map.51 = f32[1,16,512]{2,1,0:T(8,128)} custom-call(f32[1,16,16]{2,1,0:T(8,128)} %fusion.69.gram_ref, f32[1,16,512]{2,1,0:T(8,128)} %bitcast.174), custom_call_target="tpu_custom_call" | custom-call | tf_op jit(solution)/shard_map/pallas_call | solution.py:42
  104.9 1.1 fusion.40
  106.0 0.9 fusion.38
  107.6 2.7 %shard_map.52 = f32[1,16,512]{2,1,0:T(8,128)} custom-call(f32[1,16,16]{2,1,0:T(8,128)} %fusion.68.gram_ref, f32[1,16,512]{2,1,0:T(8,128)} %bitcast.175), custom_call_target="tpu_custom_call" | custom-call | tf_op jit(solution)/shard_map/pallas_call | solution.py:42
  110.3 1.4 %convolution_bitcast_fusion = f32[1,16,1024]{2,1,0:T(8,128)S(1)} fusion(f32[512,1024]{1,0:T(8,128)S(1)} %fusion.15, f32[1,16,512]{2,1,0:T(8,128)} %shard_map.52), kind=kOutput, calls=%fused_computation.21 | convolution fusion | flops 50331648 | bytes 2195456 | tf_op jit(solution)/shard_map/bkv,bvf->bkf/dot_general | solution.py:58
  112.4 0.6 fusion.67.gram_ref
  113.0 0.6 pad_maximum_fusion.2.rhs_ref
  113.6 2.9 %shard_map.53 = f32[1,16,1536]{2,1,0:T(8,128)} custom-call(f32[1,16,16]{2,1,0:T(8,128)} %fusion.67.gram_ref, f32[1,16,1536]{2,1,0:T(8,128)} %pad_maximum_fusion.2.rhs_ref), custom_call_target="tpu_custom_call" | custom-call | tf_op jit(solution)/shard_map/pallas_call | solution.py:42
  116.6 2.5 %fusion.9 = bf16[1,512,1024]{2,1,0:T(8,128)(2,1)S(1)} fusion(pred[]{:T(512)} %bitcast.27, f32[1,16,1536]{2,1,0:T(8,128)} %shard_map.53, pred[16]{0:T(512)(128)(4,1)S(1)} %iota_compare_fusion), kind=kOutput, calls=%fused_computation.20 | convolution fusion | flops 51404800 | bytes 1147905 | tf_op jit(solution)/shard_map/bkv,bkf->bvf/dot_general | solution.py:65
  119.1 1.5 %pad_maximum_fusion = bf16[2,512,1024]{2,1,0:T(8,128)(2,1)} fusion(bf16[1,512,1024]{2,1,0:T(8,128)(2,1)S(1)} %fusion.9, bf16[1,512,1024]{2,1,0:T(8,128)(2,1)S(1)} %copy-done.1), kind=kLoop, calls=%fused_computation.1 | loop fusion | flops 1048576 | bytes 4194304 | tf_op jit(solution)/shard_map/concatenate | solution.py:120
  (65 shorter events, 8.8 us)
Async XLA Ops:
  0.0 50.4 %copy-start = (f32[16,1024]{1,0:T(8,128)S(1)}, f32[16,1024]{1,0:T(8,128)}, u32[]{:S(2)}) copy-start(f32[16,1024]{1,0:T(8,128)} %param.7) | copy-start | bytes 196612
  7.8 2.7 %collective-permute-start.2 = (bf16[512,1024]{1,0:T(8,128)(2,1)S(1)}, bf16[512,1024]{1,0:T(8,128)(2,1)S(1)}, u32[]{:S(2)}, u32[]{:S(2)}) collective-permute-start(bf16[512,1024]{1,0:T(8,128)(2,1)S(1)} %get-tuple-element.12), channel_id=1, source_target_pairs={{0,64},{64,0},{128,192},{192,128},{1,65},{65,1},{129,193},{193,129... | collective-permute-start | bytes 3145736 | tf_op jit(solution)/shard_map/ppermute | solution.py:97
  13.1 16.3 %collective-permute-start.3 = (bf16[512,1024]{1,0:T(8,128)(2,1)}, bf16[512,1024]{1,0:T(8,128)(2,1)}, u32[]{:S(2)}, u32[]{:S(2)}) collective-permute-start(bf16[512,1024]{1,0:T(8,128)(2,1)} %fusion.2), channel_id=1, source_target_pairs={{0,1},{1,128},{2,3},{3,130},{4,5},{5,132},{6,7},{7,134},{8,9},{9,1... | collective-permute-start | bytes 3145736 | tf_op jit(solution)/shard_map/ppermute | solution.py:104
  14.6 4.3 %copy-start.14 = (s32[2]{0:T(128)S(1)}, s32[2]{0:T(128)}, u32[]{:S(2)}) copy-start(s32[2]{0:T(128)} %param.6) | copy-start | bytes 28
  14.6 16.3 %copy-start.15 = (s32[2]{0:T(128)S(1)}, s32[2]{0:T(128)}, u32[]{:S(2)}) copy-start(s32[2]{0:T(128)} %param.5) | copy-start | bytes 28
  17.3 22.6 %collective-permute-start.1 = (bf16[512,1024]{1,0:T(8,128)(2,1)S(1)}, bf16[512,1024]{1,0:T(8,128)(2,1)S(1)}, u32[]{:S(2)}, u32[]{:S(2)}) collective-permute-start(bf16[512,1024]{1,0:T(8,128)(2,1)S(1)} %get-tuple-element.14), channel_id=1, source_target_pairs={{0,64},{64,0},{128,192},{192,128},{1,65},{65,1},{129,193},{193,129... | collective-permute-start | bytes 3145736 | tf_op jit(solution)/shard_map/ppermute | solution.py:97
  18.5 27.2 %collective-permute-start = (bf16[512,1024]{1,0:T(8,128)(2,1)S(1)}, bf16[512,1024]{1,0:T(8,128)(2,1)}, u32[]{:S(2)}, u32[]{:S(2)}) collective-permute-start(bf16[512,1024]{1,0:T(8,128)(2,1)S(1)} %get-tuple-element.11), channel_id=1, source_target_pairs={{0,64},{64,0},{128,192},{192,128},{1,65},{65,1},{129,193},{193,129... | collective-permute-start | bytes 3145736 | tf_op jit(solution)/shard_map/ppermute | solution.py:99
  18.5 65.9 %collective-permute-start.5 = (bf16[512,1024]{1,0:T(8,128)(2,1)}, bf16[512,1024]{1,0:T(8,128)(2,1)}, u32[]{:S(2)}, u32[]{:S(2)}) collective-permute-start(bf16[512,1024]{1,0:T(8,128)(2,1)} %get-tuple-element.13), channel_id=1, source_target_pairs={{0,64},{64,0},{128,192},{192,128},{1,65},{65,1},{129,193},{193,129... | collective-permute-start | bytes 3145736 | tf_op jit(solution)/shard_map/ppermute | solution.py:99
  29.5 16.2 %collective-permute-start.4 = (bf16[512,1024]{1,0:T(8,128)(2,1)}, bf16[512,1024]{1,0:T(8,128)(2,1)S(1)}, u32[]{:S(2)}, u32[]{:S(2)}) collective-permute-start(bf16[512,1024]{1,0:T(8,128)(2,1)} %collective-permute-done.3), channel_id=1, source_target_pairs={{0,1},{1,128},{2,3},{3,130},{4,5},{5,132},{6,7},{7,134},{8,9},{9,1... | collective-permute-start | bytes 3145736 | tf_op jit(solution)/shard_map/ppermute | solution.py:105
  35.6 10.1 %copy-start.3 = (bf16[512,512]{1,0:T(8,128)(2,1)}, bf16[512,512]{1,0:T(8,128)(2,1)S(1)}, u32[]{:S(2)}) copy-start(bf16[512,512]{1,0:T(8,128)(2,1)S(1)} %fusion.24) | copy-start | bytes 1572868
  40.0 8.6 %copy-start.5 = (bf16[512,512]{1,0:T(8,128)(2,1)}, bf16[512,512]{1,0:T(8,128)(2,1)S(1)}, u32[]{:S(2)}) copy-start(bf16[512,512]{1,0:T(8,128)(2,1)S(1)} %get-tuple-element.19) | copy-start | bytes 1572868
  40.0 8.6 %copy-start.7 = (bf16[512,512]{1,0:T(8,128)(2,1)}, bf16[512,512]{1,0:T(8,128)(2,1)S(1)}, u32[]{:S(2)}) copy-start(bf16[512,512]{1,0:T(8,128)(2,1)S(1)} %get-tuple-element.20) | copy-start | bytes 1572868
  51.7 0.8 copy-start.9
  56.4 1.8 %copy-start.8 = (f32[16,512]{1,0:T(8,128)}, f32[16,512]{1,0:T(8,128)S(1)}, u32[]{:S(2)}) copy-start(f32[16,512]{1,0:T(8,128)S(1)} %fusion.57) | copy-start | bytes 98308
  56.4 16.5 %collective-permute-start.6 = (bf16[512,1024]{1,0:T(8,128)(2,1)}, bf16[512,1024]{1,0:T(8,128)(2,1)}, u32[]{:S(2)}, u32[]{:S(2)}) collective-permute-start(bf16[512,1024]{1,0:T(8,128)(2,1)} %fusion.3), channel_id=1, source_target_pairs={{0,1},{1,128},{2,3},{3,130},{4,5},{5,132},{6,7},{7,134},{8,9},{9,1... | collective-permute-start | bytes 3145736 | tf_op jit(solution)/shard_map/ppermute | solution.py:104
  62.1 1.6 %copy-start.10 = (f32[16,512]{1,0:T(8,128)}, f32[16,512]{1,0:T(8,128)S(1)}, u32[]{:S(2)}) copy-start(f32[16,512]{1,0:T(8,128)S(1)} %fusion.53) | copy-start | bytes 98308
  73.0 16.3 %collective-permute-start.7 = (bf16[512,1024]{1,0:T(8,128)(2,1)}, bf16[512,1024]{1,0:T(8,128)(2,1)}, u32[]{:S(2)}, u32[]{:S(2)}) collective-permute-start(bf16[512,1024]{1,0:T(8,128)(2,1)} %collective-permute-done.6), channel_id=1, source_target_pairs={{0,1},{1,128},{2,3},{3,130},{4,5},{5,132},{6,7},{7,134},{8,9},{9,1... | collective-permute-start | bytes 3145736 | tf_op jit(solution)/shard_map/ppermute | solution.py:105
  74.1 15.2 %copy-start.4 = (bf16[512,512]{1,0:T(8,128)(2,1)S(1)}, bf16[512,512]{1,0:T(8,128)(2,1)}, u32[]{:S(2)}) copy-start(bf16[512,512]{1,0:T(8,128)(2,1)} %copy-done.3) | copy-start | bytes 1572868
  74.1 15.2 %copy-start.6 = (bf16[512,512]{1,0:T(8,128)(2,1)S(1)}, bf16[512,512]{1,0:T(8,128)(2,1)}, u32[]{:S(2)}) copy-start(bf16[512,512]{1,0:T(8,128)(2,1)} %copy-done.5) | copy-start | bytes 1572868
  95.8 0.8 copy-start.11
  100.5 1.6 %copy-start.12 = (f32[16,512]{1,0:T(8,128)}, f32[16,512]{1,0:T(8,128)S(1)}, u32[]{:S(2)}) copy-start(f32[16,512]{1,0:T(8,128)S(1)} %fusion.44) | copy-start | bytes 98308
  106.0 1.6 %copy-start.13 = (f32[16,512]{1,0:T(8,128)}, f32[16,512]{1,0:T(8,128)S(1)}, u32[]{:S(2)}) copy-start(f32[16,512]{1,0:T(8,128)S(1)} %fusion.40) | copy-start | bytes 98308
  110.3 1.4 %copy-start.2 = (f32[1,16,512]{2,1,0:T(8,128)S(1)}, f32[1,16,512]{2,1,0:T(8,128)}, u32[]{:S(2)}) copy-start(f32[1,16,512]{2,1,0:T(8,128)} %shard_map.52) | copy-start | bytes 98308
  111.8 7.3 %copy-start.1 = (bf16[1,512,1024]{2,1,0:T(8,128)(2,1)S(1)}, bf16[1,512,1024]{2,1,0:T(8,128)(2,1)}, u32[]{:S(2)}) copy-start(bf16[1,512,1024]{2,1,0:T(8,128)(2,1)} %fusion.7) | copy-start | bytes 3145732

commit v6 on v5

--- a/solution.py
+++ b/solution.py
@@ -87,7 +87,6 @@
     chip_pair = [(i, i ^ 1) for i in range(n_coil)]
     pairs = ring_pairs(n_coil, n_slab)
     sums = []
-    arrived = None
     for q in range(partial_time.shape[2]):
         parts = partial_time[0, :, q]
 
@@ -98,12 +97,8 @@
         forward = (pick(coil ^ 2).astype(jnp.float32) + got_forward.astype(jnp.float32)).astype(jnp.bfloat16)
         got_own = lax.ppermute(pick(coil ^ 1), "coil", chip_pair)
         own = pick(coil).astype(jnp.float32) + got_own.astype(jnp.float32)
-        if arrived is not None:
-            forward, arrived = lax.optimization_barrier((forward, arrived))
-            sums[-1] = (sums[-1][0], arrived)
         hop = lax.ppermute(forward, ("coil", "slab"), pairs)
         hop = lax.ppermute(hop, ("coil", "slab"), pairs)
-        arrived = hop
         sums.append((own, hop))
     return sums
 
@@ -113,11 +108,8 @@
         transform = spectral_table(partial_time.shape[-1] // 2)
         flags = brain_mask > 0
         pieces = coil_sum(partial_time, n_coil, n_slab)
-        outs = []
-        for q, (own, hop) in enumerate(pieces):
-            patch = (own + hop.astype(jnp.float32)).astype(jnp.bfloat16)
-            outs.append(denoise_batch(patch[None], flags[q:q + 1], rank_limit[q:q + 1], transform, start_basis))
-        return jnp.concatenate(outs, axis=0)
+        patches = jnp.stack([(own + hop.astype(jnp.float32)).astype(jnp.bfloat16) for own, hop in pieces])
+        return denoise_batch(patches, flags, rank_limit, transform, start_basis)
 
     return body
 

time: 122 us -> 103 us (0.84)
  matrix products: 32.3 us -> 20.4 us
  Pallas kernels: 22.3 us -> 11.8 us
  waiting for transfers between devices: 26.7 us -> 34.3 us
  local copies, waits for them, and re-layouts: 12.4 us -> 9.36 us
  other arithmetic: 23 us -> 20.3 us
  starting transfers between devices: 3.73 us -> 5.66 us
    pallas_call x8 -> x4, Pallas kernels: 22.3 us -> 11.8 us  [factor_solve(): pl.pallas_call(factor_solve_kernel, out_shape=jax.ShapeDtypeStruct(rhs.sh...]
    another operation x2 -> x4, other arithmetic: 8.38 us -> 13.2 us
    ppermute x2, waiting for transfers between devices: 16.4 us -> 20.7 us  [coil_sum(): hop = lax.ppermute(forward, ('coil', 'slab'), pairs)]
    dot_general x8 -> x4, matrix products: 4.89 us -> 0.64 us  [denoise_batch(): inner_gram = jnp.einsum('bkw,bjw->bkj', pushed, coeff, precision=HI)]
    dot_general x2 -> x1, matrix products: 6.24 us -> 2.34 us  [denoise_batch(): jnp.einsum('bvt,tf->bvf', patches, transform, preferred_element_type=jnp....]
    ppermute x2, waiting for transfers between devices: 7.66 us -> 11.3 us  [coil_sum(): hop = lax.ppermute(hop, ('coil', 'slab'), pairs)]
    mul x8 -> x4, other arithmetic: 5.01 us -> 2.46 us  [factor_solve(): sym = 0.5 * (inner_gram + jnp.swapaxes(inner_gram, -1, -2))]
    dot_general x8 -> x4, matrix products: 6.68 us -> 4.5 us  [denoise_batch(): pushed = jnp.einsum('bkv,bvw->bkw', coeff, kernel, precision=HI)]
  transfers between devices with their start and end apart: 8 -> 8, of which waited for: 5 -> 5; matrix products, arithmetic and copies ran while one was open for 31% -> 15% of each run, Pallas kernels for 9% -> 0%
where the time goes in v6:
time: 103 us; the launch traced here: 102 us
  waiting for transfers between devices  34.3 us (33%)
  matrix products  20.4 us (20%)
  other arithmetic  20.3 us (20%)
  Pallas kernels  11.8 us (11%)
  local copies, waits for them, and re-layouts  9.36 us (9%)
  starting transfers between devices  5.66 us (5%)
    ppermute x2, waiting for transfers between devices, coil_sum(): hop = lax.ppermute(forward, ('coil', 'slab'), pairs)  20.7 us
    pallas_call x4, Pallas kernels, factor_solve(): pl.pallas_call(factor_solve_kernel, out_shape=jax.ShapeDtypeStruct(rhs.sh...  11.8 us
    ppermute x2, waiting for transfers between devices, coil_sum(): hop = lax.ppermute(hop, ('coil', 'slab'), pairs)  11.3 us
    another operation x2, other arithmetic  8.56 us
    slice x1, local copies, waits for them, and re-layouts, coil_sum(): parts = partial_time[0, :, q]  6 us
    another operation x2, other arithmetic, body(): jnp.stack([(own + hop.astype(jnp.float32)).astype(jnp.bfloat16) for own,...  4.63 us
    dot_general x4, matrix products, denoise_batch(): pushed = jnp.einsum('bkv,bvw->bkw', coeff, kernel, precision=HI)  4.5 us
    dot_general x1, matrix products, denoise_batch(): result = jnp.einsum('bkv,bkf->bvf', coefficients, truncated, precision=HI)  4.18 us
  transfers between devices with their start and end apart: 8, of which 5 were waited for; matrix products, arithmetic and copies ran while one was open for 15% of the time, Pallas kernels for 0%

profile of v6, /device:TPU:64, one launch (start us, length us, event | category | flops | bytes accessed | tf_op | source)
XLA Modules:
  0.0 102.0 jit_solution(1494529076610431473)
XLA Ops:
  0.0 6.0 %fusion.37 = (bf16[1,4,1,512,1024]{4,3,2,1,0:T(8,128)(2,1)}, bf16[1,4,1,512,1024]{4,3,2,1,0:T(8,128)(2,1)}) fusion(bf16[1,4,2,512,1024]{4,3,2,1,0:T(8,128)(2,1)} %param.4), kind=kLoop, calls=%fused_computation.62 | loop fusion | bytes 16777216 | tf_op jit(solution)/shard_map/slice | solution.py:91
  6.0 2.8 %dynamic-slice_bitcast_fusion.3 = (bf16[512,1024]{1,0:T(8,128)(2,1)S(1)}, bf16[512,1024]{1,0:T(8,128)(2,1)}) fusion(bf16[1,4,1,512,1024]{4,3,2,1,0:T(8,128)(2,1)} %get-tuple-element.5, s32[]{:T(128)S(6)} %select_n.43, s32[]{:T(128)S(6)} %select_n.45), kind=kLoop, calls=%fused_computation.38 | loop fusion | bytes 4194312 | tf_op jit(solution)/shard_map/jit(dynamic_index_in_dim)/squeeze | solution.py:94
  8.8 0.2 dynamic-slice_bitcast_fusion.1
  9.0 0.6 collective-permute-start.5
  9.6 2.2 %collective-permute-done.1 = bf16[512,1024]{1,0:T(8,128)(2,1)} collective-permute-done((bf16[512,1024]{1,0:T(8,128)(2,1)}, bf16[512,1024]{1,0:T(8,128)(2,1)}, u32[]{:S(2)}, u32[]{:S(2)}) %collective-permute-start.1) | collective-permute-done | bytes 1048608 | tf_op jit(solution)/shard_map/ppermute | solution.py:96
  11.8 1.9 %fusion.13 = bf16[512,1024]{1,0:T(8,128)(2,1)S(1)} fusion(bf16[512,1024]{1,0:T(8,128)(2,1)} %collective-permute-done.1, bf16[1,4,1,512,1024]{4,3,2,1,0:T(8,128)(2,1)} %get-tuple-element.5, s32[]{:T(128)S(6)} %select_n.44), kind=kLoop, calls=%fused_computation.17 | loop fusion | flops 2097152 | bytes 3145732 | tf_op jit(solution)/shard_map/convert_element_type | solution.py:97
  13.8 1.6 %collective-permute-start.2 = (bf16[512,1024]{1,0:T(8,128)(2,1)S(1)}, bf16[512,1024]{1,0:T(8,128)(2,1)}, u32[]{:S(2)}, u32[]{:S(2)}) collective-permute-start(bf16[512,1024]{1,0:T(8,128)(2,1)S(1)} %fusion.13), channel_id=1, source_target_pairs={{0,1},{1,128},{2,3},{3,130},{4,5},{5,132},{6,7},{7,134},{8,9},{9,1... | collective-permute-start | bytes 3145736 | tf_op jit(solution)/shard_map/ppermute | solution.py:100
  15.4 1.9 %fusion.10 = bf16[512,1024]{1,0:T(8,128)(2,1)S(1)} fusion(bf16[512,1024]{1,0:T(8,128)(2,1)} %collective-permute-done.5, bf16[1,4,1,512,1024]{4,3,2,1,0:T(8,128)(2,1)} %get-tuple-element.6, s32[]{:T(128)S(6)} %select_n.44), kind=kLoop, calls=%fused_computation.12 | loop fusion | flops 2097152 | bytes 3145732 | tf_op jit(solution)/shard_map/convert_element_type | solution.py:97
  17.3 1.6 %collective-permute-start.6 = (bf16[512,1024]{1,0:T(8,128)(2,1)S(1)}, bf16[512,1024]{1,0:T(8,128)(2,1)}, u32[]{:S(2)}, u32[]{:S(2)}) collective-permute-start(bf16[512,1024]{1,0:T(8,128)(2,1)S(1)} %fusion.10), channel_id=1, source_target_pairs={{0,1},{1,128},{2,3},{3,130},{4,5},{5,132},{6,7},{7,134},{8,9},{9,1... | collective-permute-start | bytes 3145736 | tf_op jit(solution)/shard_map/ppermute | solution.py:100
  18.9 0.2 collective-permute-start
  19.1 10.9 %collective-permute-done.2 = bf16[512,1024]{1,0:T(8,128)(2,1)} collective-permute-done((bf16[512,1024]{1,0:T(8,128)(2,1)S(1)}, bf16[512,1024]{1,0:T(8,128)(2,1)}, u32[]{:S(2)}, u32[]{:S(2)}) %collective-permute-start.2) | collective-permute-done | bytes 1048608 | tf_op jit(solution)/shard_map/ppermute | solution.py:100
  30.0 0.3 collective-permute-start.3
  30.3 1.2 %collective-permute-start.4 = (bf16[512,1024]{1,0:T(8,128)(2,1)S(1)}, bf16[512,1024]{1,0:T(8,128)(2,1)}, u32[]{:S(2)}, u32[]{:S(2)}) collective-permute-start(bf16[512,1024]{1,0:T(8,128)(2,1)S(1)} %get-tuple-element.9), channel_id=1, source_target_pairs={{0,64},{64,0},{128,192},{192,128},{1,65},{65,1},{129,193},{193,129... | collective-permute-start | bytes 3145736 | tf_op jit(solution)/shard_map/ppermute | solution.py:98
  31.5 9.8 %collective-permute-done.6 = bf16[512,1024]{1,0:T(8,128)(2,1)} collective-permute-done((bf16[512,1024]{1,0:T(8,128)(2,1)S(1)}, bf16[512,1024]{1,0:T(8,128)(2,1)}, u32[]{:S(2)}, u32[]{:S(2)}) %collective-permute-start.6) | collective-permute-done | bytes 1048608 | tf_op jit(solution)/shard_map/ppermute | solution.py:100
  41.2 0.3 collective-permute-start.7
  41.5 4.0 %fusion.24 = bf16[512,512]{1,0:T(8,128)(2,1)S(1)} fusion(), kind=kLoop, calls=%fused_computation.40 | loop fusion | flops 4194304 | bytes 524288 | tf_op jit(solution)/shard_map/convert.6
  45.5 4.6 %negate_convert_fusion = (bf16[512,512]{1,0:T(8,128)(2,1)S(1)}, bf16[512,512]{1,0:T(8,128)(2,1)S(1)}) fusion(), kind=kLoop, calls=%fused_computation.30 | loop fusion | flops 4980736 | bytes 1048576 | tf_op jit(solution)/shard_map/convert.9
  50.1 0.1 iota_compare_fusion
  50.2 2.3 %collective-permute-done.3 = bf16[512,1024]{1,0:T(8,128)(2,1)} collective-permute-done((bf16[512,1024]{1,0:T(8,128)(2,1)}, bf16[512,1024]{1,0:T(8,128)(2,1)}, u32[]{:S(2)}, u32[]{:S(2)}) %collective-permute-start.3) | collective-permute-done | bytes 1048608 | tf_op jit(solution)/shard_map/ppermute | solution.py:101
  52.5 2.2 %fusion.19 = bf16[1,512,1024]{2,1,0:T(8,128)(2,1)S(1)} fusion(bf16[512,1024]{1,0:T(8,128)(2,1)} %collective-permute-done.3, bf16[512,1024]{1,0:T(8,128)(2,1)S(1)} %collective-permute-done, bf16[1,4,1,512,1024]{4,3,2,1,0:T(8,128)(2,1)} %get-tuple-element.5, s32[]{:T(128)S(6)} %select_n.42), kind=kLoop, calls=%fused_computation.28 | loop fusion | flops 3145728 | bytes 4194308 | tf_op jit(solution)/shard_map/stack | solution.py:111
  54.6 9.1 %collective-permute-done.7 = bf16[512,1024]{1,0:T(8,128)(2,1)} collective-permute-done((bf16[512,1024]{1,0:T(8,128)(2,1)}, bf16[512,1024]{1,0:T(8,128)(2,1)}, u32[]{:S(2)}, u32[]{:S(2)}) %collective-permute-start.7) | collective-permute-done | bytes 1048608 | tf_op jit(solution)/shard_map/ppermute | solution.py:101
  63.7 2.5 %fusion.20 = bf16[1,512,1024]{2,1,0:T(8,128)(2,1)S(1)} fusion(bf16[512,1024]{1,0:T(8,128)(2,1)} %collective-permute-done.7, bf16[512,1024]{1,0:T(8,128)(2,1)} %collective-permute-done.4, bf16[1,4,1,512,1024]{4,3,2,1,0:T(8,128)(2,1)} %get-tuple-element.6, s32[]{:T(128)S(6)} %select_n.42), kind=kLoop, calls=%fused_computation.29 | loop fusion | flops 3145728 | bytes 4194308 | tf_op jit(solution)/shard_map/stack | solution.py:111
  66.2 2.3 %fusion = f32[2,512,1024]{2,1,0:T(8,128)S(1)} fusion(bf16[1,512,1024]{2,1,0:T(8,128)(2,1)S(1)} %fusion.20, bf16[1,512,1024]{2,1,0:T(8,128)(2,1)S(1)} %fusion.19, bf16[512,512]{1,0:T(8,128)(2,1)S(1)} %get-tuple-element.12, bf16[512,512]{1,0:T(8,128)(2,1)S(1)} %fusion.24, bf16[512,512]{1,0:T(8,128)(2,1)S(1)} %get-tuple-element.11), kind=kOutput, calls=%fused_computation | convolution fusion | flops 2156920832 | bytes 7864320 | tf_op jit(solution)/shard_map/bvt,tf->bvf/dot_general | solution.py:49
  68.5 3.7 %fusion.38 = f32[2,512,512]{2,1,0:T(8,128)S(1)} fusion(f32[2,512,1024]{2,1,0:T(8,128)S(1)} %fusion), kind=kOutput, calls=%fused_computation.63 | convolution fusion | flops 3221225472 | bytes 6291456 | tf_op jit(solution)/shard_map/bvf,bwf->bvw/dot_general | solution.py:50
  72.2 1.7 %fusion.25 = f32[2,512,16]{1,2,0:T(8,128)S(1)} fusion(f32[2,512,1024]{2,1,0:T(8,128)S(1)} %fusion, f32[16,1024]{1,0:T(8,128)S(1)} %copy-done), kind=kOutput, calls=%fused_computation.44 | convolution fusion | flops 100663296 | bytes 4325376 | tf_op jit(solution)/shard_map/kf,bvf->bkv/dot_general | solution.py:51
  74.0 0.6 fusion.39.rhs_ref
  74.6 0.2 fusion.40
  74.7 0.1 copy.5
  74.8 0.6 fusion.34.gram_ref
  75.4 2.9 %shard_map.46 = f32[2,16,512]{2,1,0:T(8,128)} custom-call(f32[2,16,16]{2,1,0:T(8,128)} %fusion.34.gram_ref, f32[2,16,512]{2,1,0:T(8,128)} %copy-done.4), custom_call_target="tpu_custom_call" | custom-call | tf_op jit(solution)/shard_map/pallas_call | solution.py:42
  78.3 1.5 %fusion.41.rhs_ref = f32[2,16,512]{2,1,0:T(8,128)S(1)} fusion(f32[2,16,512]{2,1,0:T(8,128)} %shard_map.46, f32[2,512,512]{2,1,0:T(8,128)S(1)} %fusion.38), kind=kOutput, calls=%fused_computation.66 | convolution fusion | flops 50331648 | bytes 2228224 | tf_op jit(solution)/shard_map/bkv,bvw->bkw/dot_general | solution.py:53
  79.9 0.2 fusion.42
  80.0 0.1 copy.6
  80.1 0.6 fusion.33.gram_ref
  80.7 2.9 %shard_map.47 = f32[2,16,512]{2,1,0:T(8,128)} custom-call(f32[2,16,16]{2,1,0:T(8,128)} %fusion.33.gram_ref, f32[2,16,512]{2,1,0:T(8,128)} %copy-done.5), custom_call_target="tpu_custom_call" | custom-call | tf_op jit(solution)/shard_map/pallas_call | solution.py:42
  83.6 1.5 %fusion.43.rhs_ref = f32[2,16,512]{2,1,0:T(8,128)S(1)} fusion(f32[2,16,512]{2,1,0:T(8,128)} %shard_map.47, f32[2,512,512]{2,1,0:T(8,128)S(1)} %fusion.38), kind=kOutput, calls=%fused_computation.68 | convolution fusion | flops 50331648 | bytes 2228224 | tf_op jit(solution)/shard_map/bkv,bvw->bkw/dot_general | solution.py:53
  85.2 0.2 fusion.44
  85.3 0.1 copy.7
  85.4 0.6 fusion.32.gram_ref
  86.0 2.9 %shard_map.48 = f32[2,16,512]{2,1,0:T(8,128)} custom-call(f32[2,16,16]{2,1,0:T(8,128)} %fusion.32.gram_ref, f32[2,16,512]{2,1,0:T(8,128)} %copy-done.6), custom_call_target="tpu_custom_call" | custom-call | tf_op jit(solution)/shard_map/pallas_call | solution.py:42
  88.9 3.4 %fusion.47 = f32[2,16,1024]{2,1,0:T(8,128)S(1)} fusion(f32[2,16,512]{2,1,0:T(8,128)} %shard_map.48, f32[2,512,1024]{2,1,0:T(8,128)} %copy-done.1), kind=kOutput, calls=%fused_computation.72 | convolution fusion | flops 100663296 | bytes 4390912 | tf_op jit(solution)/shard_map/bkv,bvf->bkf/dot_general | solution.py:58
  92.3 0.8 fusion.45
  93.2 0.2 fusion.46
  93.3 0.7 pad_maximum_fusion.rhs_ref
  94.0 0.1 copy.8
  94.1 0.6 fusion.31.gram_ref
  94.7 3.1 %shard_map.49 = f32[2,16,1536]{2,1,0:T(8,128)} custom-call(f32[2,16,16]{2,1,0:T(8,128)} %fusion.31.gram_ref, f32[2,16,1536]{2,1,0:T(8,128)} %pad_maximum_fusion.rhs_ref), custom_call_target="tpu_custom_call" | custom-call | tf_op jit(solution)/shard_map/pallas_call | solution.py:42
  97.8 4.2 %convert_select_fusion = bf16[2,512,1024]{2,1,0:T(8,128)(2,1)} fusion(pred[2]{0:T(512)(128)(4,1)S(1)} %broadcast_compare_fusion, f32[2,16,1536]{2,1,0:T(8,128)} %shard_map.49, pred[2,16]{1,0:T(4,128)(4,1)S(1)} %iota_compare_fusion), kind=kOutput, calls=%fused_computation.21 | convolution fusion | flops 102809600 | bytes 2295296 | tf_op jit(solution)/shard_map/bkv,bkf->bvf/dot_general | solution.py:65
  (27 shorter events, 0.1 us)
Async XLA Ops:
  0.0 72.2 %copy-start = (f32[16,1024]{1,0:T(8,128)S(1)}, f32[16,1024]{1,0:T(8,128)}, u32[]{:S(2)}) copy-start(f32[16,1024]{1,0:T(8,128)} %param.7) | copy-start | bytes 196612
  6.0 2.8 %copy-start.2 = (bf16[1,4,1,512,1024]{4,3,2,1,0:T(8,128)(2,1)S(1)}, bf16[1,4,1,512,1024]{4,3,2,1,0:T(8,128)(2,1)}, u32[]{:S(2)}) copy-start(bf16[1,4,1,512,1024]{4,3,2,1,0:T(8,128)(2,1)} %get-tuple-element.6) | copy-start | bytes 12582916
  8.8 3.0 %collective-permute-start.1 = (bf16[512,1024]{1,0:T(8,128)(2,1)}, bf16[512,1024]{1,0:T(8,128)(2,1)}, u32[]{:S(2)}, u32[]{:S(2)}) collective-permute-start(bf16[512,1024]{1,0:T(8,128)(2,1)} %get-tuple-element.8), channel_id=1, source_target_pairs={{0,64},{64,0},{128,192},{192,128},{1,65},{65,1},{129,193},{193,129... | collective-permute-start | bytes 3145736 | tf_op jit(solution)/shard_map/ppermute | solution.py:96
  9.0 6.4 %collective-permute-start.5 = (bf16[512,1024]{1,0:T(8,128)(2,1)S(1)}, bf16[512,1024]{1,0:T(8,128)(2,1)}, u32[]{:S(2)}, u32[]{:S(2)}) collective-permute-start(bf16[512,1024]{1,0:T(8,128)(2,1)S(1)} %get-tuple-element.10), channel_id=1, source_target_pairs={{0,64},{64,0},{128,192},{192,128},{1,65},{65,1},{129,193},{193,129... | collective-permute-start | bytes 3145736 | tf_op jit(solution)/shard_map/ppermute | solution.py:96
  13.8 36.3 %copy-start.9 = (s32[2]{0:T(128)S(1)}, s32[2]{0:T(128)}, u32[]{:S(2)}) copy-start(s32[2]{0:T(128)} %param.5) | copy-start | bytes 28
  13.8 36.3 %copy-start.10 = (s32[2]{0:T(128)S(1)}, s32[2]{0:T(128)}, u32[]{:S(2)}) copy-start(s32[2]{0:T(128)} %param.6) | copy-start | bytes 28
  13.8 16.2 %collective-permute-start.2 = (bf16[512,1024]{1,0:T(8,128)(2,1)S(1)}, bf16[512,1024]{1,0:T(8,128)(2,1)}, u32[]{:S(2)}, u32[]{:S(2)}) collective-permute-start(bf16[512,1024]{1,0:T(8,128)(2,1)S(1)} %fusion.13), channel_id=1, source_target_pairs={{0,1},{1,128},{2,3},{3,130},{4,5},{5,132},{6,7},{7,134},{8,9},{9,1... | collective-permute-start | bytes 3145736 | tf_op jit(solution)/shard_map/ppermute | solution.py:100
  17.3 23.9 %collective-permute-start.6 = (bf16[512,1024]{1,0:T(8,128)(2,1)S(1)}, bf16[512,1024]{1,0:T(8,128)(2,1)}, u32[]{:S(2)}, u32[]{:S(2)}) collective-permute-start(bf16[512,1024]{1,0:T(8,128)(2,1)S(1)} %fusion.10), channel_id=1, source_target_pairs={{0,1},{1,128},{2,3},{3,130},{4,5},{5,132},{6,7},{7,134},{8,9},{9,1... | collective-permute-start | bytes 3145736 | tf_op jit(solution)/shard_map/ppermute | solution.py:100
  18.9 31.3 %collective-permute-start = (bf16[512,1024]{1,0:T(8,128)(2,1)S(1)}, bf16[512,1024]{1,0:T(8,128)(2,1)S(1)}, u32[]{:S(2)}, u32[]{:S(2)}) collective-permute-start(bf16[512,1024]{1,0:T(8,128)(2,1)S(1)} %get-tuple-element.7), channel_id=1, source_target_pairs={{0,64},{64,0},{128,192},{192,128},{1,65},{65,1},{129,193},{193,129... | collective-permute-start | bytes 3145736 | tf_op jit(solution)/shard_map/ppermute | solution.py:98
  30.0 22.5 %collective-permute-start.3 = (bf16[512,1024]{1,0:T(8,128)(2,1)}, bf16[512,1024]{1,0:T(8,128)(2,1)}, u32[]{:S(2)}, u32[]{:S(2)}) collective-permute-start(bf16[512,1024]{1,0:T(8,128)(2,1)} %collective-permute-done.2), channel_id=1, source_target_pairs={{0,1},{1,128},{2,3},{3,130},{4,5},{5,132},{6,7},{7,134},{8,9},{9,1... | collective-permute-start | bytes 3145736 | tf_op jit(solution)/shard_map/ppermute | solution.py:101
  30.3 24.4 %collective-permute-start.4 = (bf16[512,1024]{1,0:T(8,128)(2,1)S(1)}, bf16[512,1024]{1,0:T(8,128)(2,1)}, u32[]{:S(2)}, u32[]{:S(2)}) collective-permute-start(bf16[512,1024]{1,0:T(8,128)(2,1)S(1)} %get-tuple-element.9), channel_id=1, source_target_pairs={{0,64},{64,0},{128,192},{192,128},{1,65},{65,1},{129,193},{193,129... | collective-permute-start | bytes 3145736 | tf_op jit(solution)/shard_map/ppermute | solution.py:98
  41.2 22.5 %collective-permute-start.7 = (bf16[512,1024]{1,0:T(8,128)(2,1)}, bf16[512,1024]{1,0:T(8,128)(2,1)}, u32[]{:S(2)}, u32[]{:S(2)}) collective-permute-start(bf16[512,1024]{1,0:T(8,128)(2,1)} %collective-permute-done.6), channel_id=1, source_target_pairs={{0,1},{1,128},{2,3},{3,130},{4,5},{5,132},{6,7},{7,134},{8,9},{9,1... | collective-permute-start | bytes 3145736 | tf_op jit(solution)/shard_map/ppermute | solution.py:101
  68.5 3.7 %copy-start.1 = (f32[2,512,1024]{2,1,0:T(8,128)}, f32[2,512,1024]{2,1,0:T(8,128)S(1)}, u32[]{:S(2)}) copy-start(f32[2,512,1024]{2,1,0:T(8,128)S(1)} %fusion) | copy-start | bytes 12582916
  74.6 0.9 copy-start.4
  78.3 1.5 %copy-start.7 = (f32[2,16,512]{2,1,0:T(8,128)S(1)}, f32[2,16,512]{2,1,0:T(8,128)}, u32[]{:S(2)}) copy-start(f32[2,16,512]{2,1,0:T(8,128)} %shard_map.46) | copy-start | bytes 196612
  79.9 0.9 copy-start.5
  83.6 1.5 %copy-start.8 = (f32[2,16,512]{2,1,0:T(8,128)S(1)}, f32[2,16,512]{2,1,0:T(8,128)}, u32[]{:S(2)}) copy-start(f32[2,16,512]{2,1,0:T(8,128)} %shard_map.47) | copy-start | bytes 196612
  85.2 0.9 copy-start.6
  88.9 3.4 %copy-start.3 = (f32[2,16,512]{2,1,0:T(8,128)S(1)}, f32[2,16,512]{2,1,0:T(8,128)}, u32[]{:S(2)}) copy-start(f32[2,16,512]{2,1,0:T(8,128)} %shard_map.48) | copy-start | bytes 196612

commit v7 on v6

--- a/solution.py
+++ b/solution.py
@@ -88,10 +88,10 @@
     pairs = ring_pairs(n_coil, n_slab)
     sums = []
     for q in range(partial_time.shape[2]):
-        parts = partial_time[0, :, q]
 
-        def pick(o):
-            return lax.dynamic_index_in_dim(parts, o, 0, keepdims=False)
+        def pick(o, q=q):
+            block = lax.dynamic_slice(partial_time, (0, o, q, 0, 0), (1, 1, 1) + partial_time.shape[3:])
+            return block.reshape(partial_time.shape[3:])
 
         got_forward = lax.ppermute(pick(coil ^ 3), "coil", chip_pair)
         forward = (pick(coil ^ 2).astype(jnp.float32) + got_forward.astype(jnp.float32)).astype(jnp.bfloat16)

time: 103 us -> 102 us (level)
  waiting for transfers between devices: 34.3 us -> 41.1 us
  local copies, waits for them, and re-layouts: 9.36 us -> 4.18 us
  other arithmetic: 20.3 us -> 18.9 us
    slice x1 -> x0, local copies, waits for them, and re-layouts: 6 us -> none  [coil_sum(): parts = partial_time[0, :, q]]
    reshape x0 -> x1, local copies, waits for them, and re-layouts: none -> 3.84 us  [pick(): return block.reshape(partial_time.shape[3:])]
    squeeze x2 -> x0, local copies, waits for them, and re-layouts: 3.01 us -> none  [pick(): return lax.dynamic_index_in_dim(parts, o, 0, keepdims=False)]
    ppermute x2, waiting for transfers between devices: 20.7 us -> 23.6 us  [coil_sum(): hop = lax.ppermute(forward, ('coil', 'slab'), pairs)]
    ppermute x2, waiting for transfers between devices: 11.3 us -> 13.5 us  [coil_sum(): hop = lax.ppermute(hop, ('coil', 'slab'), pairs)]
    ppermute x2, waiting for transfers between devices: 2.23 us -> 3.99 us  [coil_sum(): got_forward = lax.ppermute(pick(coil ^ 3), 'coil', chip_pair)]
    convert_element_type x2 -> x1, other arithmetic: 3.86 us -> 3.13 us  [coil_sum(): (pick(coil ^ 2).astype(jnp.float32) + got_forward.astype(jnp.float32)).as...]
    another operation x2 -> x1, other arithmetic: 4.63 us -> 3.95 us  [body(): jnp.stack([(own + hop.astype(jnp.float32)).astype(jnp.bfloat16) for own,...]
  transfers between devices with their start and end apart: 8 -> 8, of which waited for: 5 -> 6; matrix products, arithmetic and copies ran while one was open for 15% -> 9% of each run, Pallas kernels for 0% -> 0%
where the time goes in v7:
time: 102 us; the launch traced here: 101 us
  waiting for transfers between devices  41.1 us (40%)
  matrix products  20.4 us (20%)
  other arithmetic  18.9 us (19%)
  Pallas kernels  11.8 us (12%)
  starting transfers between devices  4.64 us (5%)
  local copies, waits for them, and re-layouts  4.18 us (4%)
    ppermute x2, waiting for transfers between devices, coil_sum(): hop = lax.ppermute(forward, ('coil', 'slab'), pairs)  23.6 us
    ppermute x2, waiting for transfers between devices, coil_sum(): hop = lax.ppermute(hop, ('coil', 'slab'), pairs)  13.5 us
    pallas_call x4, Pallas kernels, factor_solve(): pl.pallas_call(factor_solve_kernel, out_shape=jax.ShapeDtypeStruct(rhs.sh...  11.8 us
    another operation x2, other arithmetic  8.56 us
    dot_general x4, matrix products, denoise_batch(): pushed = jnp.einsum('bkv,bvw->bkw', coeff, kernel, precision=HI)  4.5 us
    dot_general x1, matrix products, denoise_batch(): result = jnp.einsum('bkv,bkf->bvf', coefficients, truncated, precision=HI)  4.18 us
    ppermute x2, waiting for transfers between devices, coil_sum(): got_forward = lax.ppermute(pick(coil ^ 3), 'coil', chip_pair)  3.99 us
    another operation x1, other arithmetic, body(): jnp.stack([(own + hop.astype(jnp.float32)).astype(jnp.bfloat16) for own,...  3.95 us
  transfers between devices with their start and end apart: 8, of which 6 were waited for; matrix products, arithmetic and copies ran while one was open for 9% of the time, Pallas kernels for 0%

profile of v7, /device:TPU:64, one launch (start us, length us, event | category | flops | bytes accessed | tf_op | source)
XLA Modules:
  0.0 101.1 jit_solution(17571762969847201913)
XLA Ops:
  0.0 3.8 %dynamic-slice_bitcast_fusion.3 = (bf16[512,1024]{1,0:T(8,128)(2,1)S(1)}, bf16[512,1024]{1,0:T(8,128)(2,1)S(1)}, bf16[512,1024]{1,0:T(8,128)(2,1)}, bf16[512,1024]{1,0:T(8,128)(2,1)S(1)}) fusion(bf16[1,4,2,512,1024]{4,3,2,1,0:T(8,128)(2,1)} %param.4, s32[]{:T(128)S(6)} %select_n.42, s32[]{:T(128)S(6)} %select_n.44), kind=kLoop, calls=%fused_computation.38 | loop fusion | bytes 8388616 | tf_op jit(solution)/shard_map/reshape | solution.py:94
  3.8 0.0 collective-permute-start.1
  3.8 0.5 collective-permute-start.5
  4.4 2.5 %collective-permute-done.1 = bf16[512,1024]{1,0:T(8,128)(2,1)} collective-permute-done((bf16[512,1024]{1,0:T(8,128)(2,1)}, bf16[512,1024]{1,0:T(8,128)(2,1)}, u32[]{:S(2)}, u32[]{:S(2)}) %collective-permute-start.1) | collective-permute-done | bytes 1048608 | tf_op jit(solution)/shard_map/ppermute | solution.py:96
  6.8 1.5 %collective-permute-done.5 = bf16[512,1024]{1,0:T(8,128)(2,1)} collective-permute-done((bf16[512,1024]{1,0:T(8,128)(2,1)S(1)}, bf16[512,1024]{1,0:T(8,128)(2,1)}, u32[]{:S(2)}, u32[]{:S(2)}) %collective-permute-start.5) | collective-permute-done | bytes 1048608 | tf_op jit(solution)/shard_map/ppermute | solution.py:96
  8.3 3.1 %fusion.13 = (bf16[512,1024]{1,0:T(8,128)(2,1)S(1)}, bf16[512,1024]{1,0:T(8,128)(2,1)S(1)}) fusion(bf16[512,1024]{1,0:T(8,128)(2,1)} %collective-permute-done.1, bf16[1,4,2,512,1024]{4,3,2,1,0:T(8,128)(2,1)} %param.4, s32[]{:T(128)S(6)} %select_n.43, bf16[512,1024]{1,0:T(8,128)(2,1)} %collective-permute-done.5), kind=kLoop, calls=%fused_computation.17 | loop fusion | flops 4194304 | bytes 6291460 | tf_op jit(solution)/shard_map/convert_element_type | solution.py:97
  11.5 1.6 %collective-permute-start.2 = (bf16[512,1024]{1,0:T(8,128)(2,1)S(1)}, bf16[512,1024]{1,0:T(8,128)(2,1)}, u32[]{:S(2)}, u32[]{:S(2)}) collective-permute-start(bf16[512,1024]{1,0:T(8,128)(2,1)S(1)} %get-tuple-element.11), channel_id=1, source_target_pairs={{0,1},{1,128},{2,3},{3,130},{4,5},{5,132},{6,7},{7,134},{8,9},{9,1... | collective-permute-start | bytes 3145736 | tf_op jit(solution)/shard_map/ppermute | solution.py:100
  13.0 1.5 %collective-permute-start.6 = (bf16[512,1024]{1,0:T(8,128)(2,1)S(1)}, bf16[512,1024]{1,0:T(8,128)(2,1)}, u32[]{:S(2)}, u32[]{:S(2)}) collective-permute-start(bf16[512,1024]{1,0:T(8,128)(2,1)S(1)} %get-tuple-element.12), channel_id=1, source_target_pairs={{0,1},{1,128},{2,3},{3,130},{4,5},{5,132},{6,7},{7,134},{8,9},{9,1... | collective-permute-start | bytes 3145736 | tf_op jit(solution)/shard_map/ppermute | solution.py:100
  14.5 0.2 collective-permute-start
  14.7 0.3 collective-permute-start.4
  15.0 12.6 %collective-permute-done.2 = bf16[512,1024]{1,0:T(8,128)(2,1)} collective-permute-done((bf16[512,1024]{1,0:T(8,128)(2,1)S(1)}, bf16[512,1024]{1,0:T(8,128)(2,1)}, u32[]{:S(2)}, u32[]{:S(2)}) %collective-permute-start.2) | collective-permute-done | bytes 1048608 | tf_op jit(solution)/shard_map/ppermute | solution.py:100
  27.7 0.3 collective-permute-start.3
  27.9 11.0 %collective-permute-done.6 = bf16[512,1024]{1,0:T(8,128)(2,1)} collective-permute-done((bf16[512,1024]{1,0:T(8,128)(2,1)S(1)}, bf16[512,1024]{1,0:T(8,128)(2,1)}, u32[]{:S(2)}, u32[]{:S(2)}) %collective-permute-start.6) | collective-permute-done | bytes 1048608 | tf_op jit(solution)/shard_map/ppermute | solution.py:100
  38.9 0.3 collective-permute-start.7
  39.2 4.0 %fusion.24 = bf16[512,512]{1,0:T(8,128)(2,1)S(1)} fusion(), kind=kLoop, calls=%fused_computation.40 | loop fusion | flops 4194304 | bytes 524288 | tf_op jit(solution)/shard_map/convert.6
  43.2 4.6 %negate_convert_fusion = (bf16[512,512]{1,0:T(8,128)(2,1)S(1)}, bf16[512,512]{1,0:T(8,128)(2,1)S(1)}) fusion(), kind=kLoop, calls=%fused_computation.30 | loop fusion | flops 4980736 | bytes 1048576 | tf_op jit(solution)/shard_map/convert.9
  47.8 0.1 iota_compare_fusion
  47.9 2.3 %collective-permute-done.3 = bf16[512,1024]{1,0:T(8,128)(2,1)} collective-permute-done((bf16[512,1024]{1,0:T(8,128)(2,1)}, bf16[512,1024]{1,0:T(8,128)(2,1)}, u32[]{:S(2)}, u32[]{:S(2)}) %collective-permute-start.3) | collective-permute-done | bytes 1048608 | tf_op jit(solution)/shard_map/ppermute | solution.py:101
  50.1 11.2 %collective-permute-done.7 = bf16[512,1024]{1,0:T(8,128)(2,1)} collective-permute-done((bf16[512,1024]{1,0:T(8,128)(2,1)}, bf16[512,1024]{1,0:T(8,128)(2,1)}, u32[]{:S(2)}, u32[]{:S(2)}) %collective-permute-start.7) | collective-permute-done | bytes 1048608 | tf_op jit(solution)/shard_map/ppermute | solution.py:101
  61.4 4.0 %fusion.19 = (bf16[1,512,1024]{2,1,0:T(8,128)(2,1)S(1)}, bf16[1,512,1024]{2,1,0:T(8,128)(2,1)S(1)}) fusion(bf16[512,1024]{1,0:T(8,128)(2,1)} %collective-permute-done.3, bf16[512,1024]{1,0:T(8,128)(2,1)S(1)} %collective-permute-done, bf16[1,4,2,512,1024]{4,3,2,1,0:T(8,128)(2,1)} %param.4, s32[]{:T(128)S(6)} %select_n.41, ...), kind=kLoop, calls=%fused_computation.28 | loop fusion | flops 6291456 | bytes 8388612 | tf_op jit(solution)/shard_map/stack | solution.py:111
  65.3 2.3 %fusion = f32[2,512,1024]{2,1,0:T(8,128)S(1)} fusion(bf16[1,512,1024]{2,1,0:T(8,128)(2,1)S(1)} %get-tuple-element.6, bf16[1,512,1024]{2,1,0:T(8,128)(2,1)S(1)} %get-tuple-element.5, bf16[512,512]{1,0:T(8,128)(2,1)S(1)} %get-tuple-element.14, bf16[512,512]{1,0:T(8,128)(2,1)S(1)} %fusion.24, bf16[512,512]{1,0:T(8,128)(2,1)S(1)} %get-tuple-element.13), kind=kOutput, calls=%fused_computation | convolution fusion | flops 2156920832 | bytes 7864320 | tf_op jit(solution)/shard_map/bvt,tf->bvf/dot_general | solution.py:49
  67.7 3.7 %fusion.37 = f32[2,512,512]{2,1,0:T(8,128)S(1)} fusion(f32[2,512,1024]{2,1,0:T(8,128)S(1)} %fusion), kind=kOutput, calls=%fused_computation.62 | convolution fusion | flops 3221225472 | bytes 6291456 | tf_op jit(solution)/shard_map/bvf,bwf->bvw/dot_general | solution.py:50
  71.3 1.7 %fusion.25 = f32[2,512,16]{1,2,0:T(8,128)S(1)} fusion(f32[2,512,1024]{2,1,0:T(8,128)S(1)} %fusion, f32[16,1024]{1,0:T(8,128)S(1)} %copy-done), kind=kOutput, calls=%fused_computation.44 | convolution fusion | flops 100663296 | bytes 4325376 | tf_op jit(solution)/shard_map/kf,bvf->bkv/dot_general | solution.py:51
  73.1 0.6 fusion.38.rhs_ref
  73.7 0.2 fusion.39
  73.9 0.1 copy.5
  73.9 0.6 fusion.34.gram_ref
  74.6 2.9 %shard_map.46 = f32[2,16,512]{2,1,0:T(8,128)} custom-call(f32[2,16,16]{2,1,0:T(8,128)} %fusion.34.gram_ref, f32[2,16,512]{2,1,0:T(8,128)} %copy-done.3), custom_call_target="tpu_custom_call" | custom-call | tf_op jit(solution)/shard_map/pallas_call | solution.py:42
  77.5 1.5 %fusion.40.rhs_ref = f32[2,16,512]{2,1,0:T(8,128)S(1)} fusion(f32[2,16,512]{2,1,0:T(8,128)} %shard_map.46, f32[2,512,512]{2,1,0:T(8,128)S(1)} %fusion.37), kind=kOutput, calls=%fused_computation.65 | convolution fusion | flops 50331648 | bytes 2228224 | tf_op jit(solution)/shard_map/bkv,bvw->bkw/dot_general | solution.py:53
  79.0 0.0 copy-start.4
  79.0 0.2 fusion.41
  79.2 0.1 copy.6
  79.2 0.6 fusion.33.gram_ref
  79.9 2.9 %shard_map.47 = f32[2,16,512]{2,1,0:T(8,128)} custom-call(f32[2,16,16]{2,1,0:T(8,128)} %fusion.33.gram_ref, f32[2,16,512]{2,1,0:T(8,128)} %copy-done.4), custom_call_target="tpu_custom_call" | custom-call | tf_op jit(solution)/shard_map/pallas_call | solution.py:42
  82.7 1.5 %fusion.42.rhs_ref = f32[2,16,512]{2,1,0:T(8,128)S(1)} fusion(f32[2,16,512]{2,1,0:T(8,128)} %shard_map.47, f32[2,512,512]{2,1,0:T(8,128)S(1)} %fusion.37), kind=kOutput, calls=%fused_computation.67 | convolution fusion | flops 50331648 | bytes 2228224 | tf_op jit(solution)/shard_map/bkv,bvw->bkw/dot_general | solution.py:53
  84.3 0.0 copy-start.5
  84.3 0.2 fusion.43
  84.4 0.1 copy.7
  84.5 0.6 fusion.32.gram_ref
  85.1 2.9 %shard_map.48 = f32[2,16,512]{2,1,0:T(8,128)} custom-call(f32[2,16,16]{2,1,0:T(8,128)} %fusion.32.gram_ref, f32[2,16,512]{2,1,0:T(8,128)} %copy-done.5), custom_call_target="tpu_custom_call" | custom-call | tf_op jit(solution)/shard_map/pallas_call | solution.py:42
  88.0 3.4 %fusion.46 = f32[2,16,1024]{2,1,0:T(8,128)S(1)} fusion(f32[2,16,512]{2,1,0:T(8,128)} %shard_map.48, f32[2,512,1024]{2,1,0:T(8,128)} %copy-done.1), kind=kOutput, calls=%fused_computation.71 | convolution fusion | flops 100663296 | bytes 4390912 | tf_op jit(solution)/shard_map/bkv,bvf->bkf/dot_general | solution.py:58
  91.4 0.8 fusion.44
  92.3 0.2 fusion.45
  92.4 0.7 pad_maximum_fusion.rhs_ref
  93.1 0.1 copy.8
  93.2 0.6 fusion.31.gram_ref
  93.8 3.1 %shard_map.49 = f32[2,16,1536]{2,1,0:T(8,128)} custom-call(f32[2,16,16]{2,1,0:T(8,128)} %fusion.31.gram_ref, f32[2,16,1536]{2,1,0:T(8,128)} %pad_maximum_fusion.rhs_ref), custom_call_target="tpu_custom_call" | custom-call | tf_op jit(solution)/shard_map/pallas_call | solution.py:42
  96.9 4.2 %convert_select_fusion = bf16[2,512,1024]{2,1,0:T(8,128)(2,1)} fusion(pred[2]{0:T(512)(128)(4,1)S(1)} %broadcast_compare_fusion, f32[2,16,1536]{2,1,0:T(8,128)} %shard_map.49, pred[2,16]{1,0:T(4,128)(4,1)S(1)} %iota_compare_fusion), kind=kOutput, calls=%fused_computation.21 | convolution fusion | flops 102809600 | bytes 2295296 | tf_op jit(solution)/shard_map/bkv,bkf->bvf/dot_general | solution.py:65
  (21 shorter events, 0.0 us)
Async XLA Ops:
  0.0 71.3 %copy-start = (f32[16,1024]{1,0:T(8,128)S(1)}, f32[16,1024]{1,0:T(8,128)}, u32[]{:S(2)}) copy-start(f32[16,1024]{1,0:T(8,128)} %param.7) | copy-start | bytes 196612
  3.8 3.0 %collective-permute-start.1 = (bf16[512,1024]{1,0:T(8,128)(2,1)}, bf16[512,1024]{1,0:T(8,128)(2,1)}, u32[]{:S(2)}, u32[]{:S(2)}) collective-permute-start(bf16[512,1024]{1,0:T(8,128)(2,1)} %get-tuple-element.9), channel_id=1, source_target_pairs={{0,64},{64,0},{128,192},{192,128},{1,65},{65,1},{129,193},{193,129... | collective-permute-start | bytes 3145736 | tf_op jit(solution)/shard_map/ppermute | solution.py:96
  3.8 4.5 %collective-permute-start.5 = (bf16[512,1024]{1,0:T(8,128)(2,1)S(1)}, bf16[512,1024]{1,0:T(8,128)(2,1)}, u32[]{:S(2)}, u32[]{:S(2)}) collective-permute-start(bf16[512,1024]{1,0:T(8,128)(2,1)S(1)} %get-tuple-element.10), channel_id=1, source_target_pairs={{0,64},{64,0},{128,192},{192,128},{1,65},{65,1},{129,193},{193,129... | collective-permute-start | bytes 3145736 | tf_op jit(solution)/shard_map/ppermute | solution.py:96
  4.4 43.4 %copy-start.8 = (s32[2]{0:T(128)S(1)}, s32[2]{0:T(128)}, u32[]{:S(2)}) copy-start(s32[2]{0:T(128)} %param.5) | copy-start | bytes 28
  4.4 43.4 %copy-start.9 = (s32[2]{0:T(128)S(1)}, s32[2]{0:T(128)}, u32[]{:S(2)}) copy-start(s32[2]{0:T(128)} %param.6) | copy-start | bytes 28
  11.5 16.2 %collective-permute-start.2 = (bf16[512,1024]{1,0:T(8,128)(2,1)S(1)}, bf16[512,1024]{1,0:T(8,128)(2,1)}, u32[]{:S(2)}, u32[]{:S(2)}) collective-permute-start(bf16[512,1024]{1,0:T(8,128)(2,1)S(1)} %get-tuple-element.11), channel_id=1, source_target_pairs={{0,1},{1,128},{2,3},{3,130},{4,5},{5,132},{6,7},{7,134},{8,9},{9,1... | collective-permute-start | bytes 3145736 | tf_op jit(solution)/shard_map/ppermute | solution.py:100
  13.0 25.9 %collective-permute-start.6 = (bf16[512,1024]{1,0:T(8,128)(2,1)S(1)}, bf16[512,1024]{1,0:T(8,128)(2,1)}, u32[]{:S(2)}, u32[]{:S(2)}) collective-permute-start(bf16[512,1024]{1,0:T(8,128)(2,1)S(1)} %get-tuple-element.12), channel_id=1, source_target_pairs={{0,1},{1,128},{2,3},{3,130},{4,5},{5,132},{6,7},{7,134},{8,9},{9,1... | collective-permute-start | bytes 3145736 | tf_op jit(solution)/shard_map/ppermute | solution.py:100
  14.5 33.3 %collective-permute-start = (bf16[512,1024]{1,0:T(8,128)(2,1)S(1)}, bf16[512,1024]{1,0:T(8,128)(2,1)S(1)}, u32[]{:S(2)}, u32[]{:S(2)}) collective-permute-start(bf16[512,1024]{1,0:T(8,128)(2,1)S(1)} %get-tuple-element.7), channel_id=1, source_target_pairs={{0,64},{64,0},{128,192},{192,128},{1,65},{65,1},{129,193},{193,129... | collective-permute-start | bytes 3145736 | tf_op jit(solution)/shard_map/ppermute | solution.py:98
  14.7 33.2 %collective-permute-start.4 = (bf16[512,1024]{1,0:T(8,128)(2,1)S(1)}, bf16[512,1024]{1,0:T(8,128)(2,1)}, u32[]{:S(2)}, u32[]{:S(2)}) collective-permute-start(bf16[512,1024]{1,0:T(8,128)(2,1)S(1)} %get-tuple-element.8), channel_id=1, source_target_pairs={{0,64},{64,0},{128,192},{192,128},{1,65},{65,1},{129,193},{193,129... | collective-permute-start | bytes 3145736 | tf_op jit(solution)/shard_map/ppermute | solution.py:98
  27.7 22.5 %collective-permute-start.3 = (bf16[512,1024]{1,0:T(8,128)(2,1)}, bf16[512,1024]{1,0:T(8,128)(2,1)}, u32[]{:S(2)}, u32[]{:S(2)}) collective-permute-start(bf16[512,1024]{1,0:T(8,128)(2,1)} %collective-permute-done.2), channel_id=1, source_target_pairs={{0,1},{1,128},{2,3},{3,130},{4,5},{5,132},{6,7},{7,134},{8,9},{9,1... | collective-permute-start | bytes 3145736 | tf_op jit(solution)/shard_map/ppermute | solution.py:101
  38.9 22.5 %collective-permute-start.7 = (bf16[512,1024]{1,0:T(8,128)(2,1)}, bf16[512,1024]{1,0:T(8,128)(2,1)}, u32[]{:S(2)}, u32[]{:S(2)}) collective-permute-start(bf16[512,1024]{1,0:T(8,128)(2,1)} %collective-permute-done.6), channel_id=1, source_target_pairs={{0,1},{1,128},{2,3},{3,130},{4,5},{5,132},{6,7},{7,134},{8,9},{9,1... | collective-permute-start | bytes 3145736 | tf_op jit(solution)/shard_map/ppermute | solution.py:101
  67.7 3.7 %copy-start.1 = (f32[2,512,1024]{2,1,0:T(8,128)}, f32[2,512,1024]{2,1,0:T(8,128)S(1)}, u32[]{:S(2)}) copy-start(f32[2,512,1024]{2,1,0:T(8,128)S(1)} %fusion) | copy-start | bytes 12582916
  73.7 0.9 copy-start.3
  77.5 1.5 %copy-start.6 = (f32[2,16,512]{2,1,0:T(8,128)S(1)}, f32[2,16,512]{2,1,0:T(8,128)}, u32[]{:S(2)}) copy-start(f32[2,16,512]{2,1,0:T(8,128)} %shard_map.46) | copy-start | bytes 196612
  79.0 0.9 copy-start.4
  82.7 1.5 %copy-start.7 = (f32[2,16,512]{2,1,0:T(8,128)S(1)}, f32[2,16,512]{2,1,0:T(8,128)}, u32[]{:S(2)}) copy-start(f32[2,16,512]{2,1,0:T(8,128)} %shard_map.47) | copy-start | bytes 196612
  84.3 0.9 copy-start.5
  88.0 3.4 %copy-start.2 = (f32[2,16,512]{2,1,0:T(8,128)S(1)}, f32[2,16,512]{2,1,0:T(8,128)}, u32[]{:S(2)}) copy-start(f32[2,16,512]{2,1,0:T(8,128)} %shard_map.48) | copy-start | bytes 196612

commit v8 on v7

--- a/solution.py
+++ b/solution.py
@@ -87,14 +87,16 @@
     chip_pair = [(i, i ^ 1) for i in range(n_coil)]
     pairs = ring_pairs(n_coil, n_slab)
     sums = []
+    source = [partial_time]
     for q in range(partial_time.shape[2]):
 
         def pick(o, q=q):
-            block = lax.dynamic_slice(partial_time, (0, o, q, 0, 0), (1, 1, 1) + partial_time.shape[3:])
-            return block.reshape(partial_time.shape[3:])
+            block = lax.dynamic_slice(source[0], (0, o, q, 0, 0), (1, 1, 1) + source[0].shape[3:])
+            return block.reshape(source[0].shape[3:])
 
         got_forward = lax.ppermute(pick(coil ^ 3), "coil", chip_pair)
         forward = (pick(coil ^ 2).astype(jnp.float32) + got_forward.astype(jnp.float32)).astype(jnp.bfloat16)
+        source[0], forward = lax.optimization_barrier((source[0], forward))
         got_own = lax.ppermute(pick(coil ^ 1), "coil", chip_pair)
         own = pick(coil).astype(jnp.float32) + got_own.astype(jnp.float32)
         hop = lax.ppermute(forward, ("coil", "slab"), pairs)

time: 102 us -> 112 us (1.098)
  waiting for transfers between devices: 41.1 us -> 51.8 us
    ppermute x2, waiting for transfers between devices: 13.5 us -> 23.2 us  [coil_sum(): hop = lax.ppermute(hop, ('coil', 'slab'), pairs)]
    ppermute x2, waiting for transfers between devices: 23.6 us -> 25.9 us  [coil_sum(): hop = lax.ppermute(forward, ('coil', 'slab'), pairs)]
    convert_element_type x1, other arithmetic: 3.13 us -> 1.62 us  [coil_sum(): (pick(coil ^ 2).astype(jnp.float32) + got_forward.astype(jnp.float32)).as...]
    ppermute x2, starting transfers between devices: 3.06 us -> 1.65 us  [coil_sum(): hop = lax.ppermute(forward, ('coil', 'slab'), pairs)]
    ppermute x2, waiting for transfers between devices: 3.99 us -> 2.64 us  [coil_sum(): got_forward = lax.ppermute(pick(coil ^ 3), 'coil', chip_pair)]
    another operation x1 -> x2, other arithmetic: 3.95 us -> 5.23 us  [body(): jnp.stack([(own + hop.astype(jnp.float32)).astype(jnp.bfloat16) for own,...]
    reshape x1 -> x3, local copies, waits for them, and re-layouts: 3.84 us -> 4.34 us  [pick(): return block.reshape(source[0].shape[3:])]
  transfers between devices with their start and end apart: 8 -> 8, of which waited for: 6 -> 5; matrix products, arithmetic and copies ran while one was open for 9% -> 10% of each run, Pallas kernels for 0% -> 0%
where the time goes in v8:
time: 112 us; the launch traced here: 111 us
  waiting for transfers between devices  51.8 us (46%)
  matrix products  20.2 us (18%)
  other arithmetic  18.7 us (17%)
  Pallas kernels  11.8 us (11%)
  local copies, waits for them, and re-layouts  4.69 us (4%)
  starting transfers between devices  3.72 us (3%)
    ppermute x2, waiting for transfers between devices, coil_sum(): hop = lax.ppermute(forward, ('coil', 'slab'), pairs)  25.9 us
    ppermute x2, waiting for transfers between devices, coil_sum(): hop = lax.ppermute(hop, ('coil', 'slab'), pairs)  23.2 us
    pallas_call x4, Pallas kernels, factor_solve(): pl.pallas_call(factor_solve_kernel, out_shape=jax.ShapeDtypeStruct(rhs.sh...  11.8 us
    another operation x2, other arithmetic  8.57 us
    another operation x2, other arithmetic, body(): jnp.stack([(own + hop.astype(jnp.float32)).astype(jnp.bfloat16) for own,...  5.23 us
    reshape x3, local copies, waits for them, and re-layouts, pick(): return block.reshape(source[0].shape[3:])  4.34 us
    dot_general x4, matrix products, denoise_batch(): pushed = jnp.einsum('bkv,bvw->bkw', coeff, kernel, precision=HI)  4.28 us
    dot_general x1, matrix products, denoise_batch(): result = jnp.einsum('bkv,bkf->bvf', coefficients, truncated, precision=HI)  4.18 us
  transfers between devices with their start and end apart: 8, of which 5 were waited for; matrix products, arithmetic and copies ran while one was open for 10% of the time, Pallas kernels for 0%

profile of v8, /device:TPU:64, one launch (start us, length us, event | category | flops | bytes accessed | tf_op | source)
XLA Modules:
  0.0 111.1 jit_solution(8657896358291187360)
XLA Ops:
  0.0 1.3 %dynamic-slice_bitcast_fusion.3 = bf16[512,1024]{1,0:T(8,128)(2,1)S(1)} fusion(bf16[1,4,2,512,1024]{4,3,2,1,0:T(8,128)(2,1)} %param.4, s32[]{:T(128)S(6)} %select_n.42), kind=kLoop, calls=%fused_computation.38 | loop fusion | bytes 2097156 | tf_op jit(solution)/shard_map/reshape | solution.py:95
  1.3 0.1 collective-permute-start
  1.4 2.6 %collective-permute-done = bf16[512,1024]{1,0:T(8,128)(2,1)S(1)} collective-permute-done((bf16[512,1024]{1,0:T(8,128)(2,1)S(1)}, bf16[512,1024]{1,0:T(8,128)(2,1)S(1)}, u32[]{:S(2)}, u32[]{:S(2)}) %collective-permute-start) | collective-permute-done | bytes 1048608 | tf_op jit(solution)/shard_map/ppermute | solution.py:97
  4.1 1.6 %fusion.15 = bf16[512,1024]{1,0:T(8,128)(2,1)S(1)} fusion(bf16[512,1024]{1,0:T(8,128)(2,1)S(1)} %collective-permute-done, bf16[1,4,2,512,1024]{4,3,2,1,0:T(8,128)(2,1)} %param.4, s32[]{:T(128)S(6)} %select_n.41), kind=kLoop, calls=%fused_computation.20 | loop fusion | flops 2097152 | bytes 3145732 | tf_op jit(solution)/shard_map/convert_element_type | solution.py:98
  5.7 1.6 %collective-permute-start.2 = (bf16[512,1024]{1,0:T(8,128)(2,1)S(1)}, bf16[512,1024]{1,0:T(8,128)(2,1)}, u32[]{:S(2)}, u32[]{:S(2)}) collective-permute-start(bf16[512,1024]{1,0:T(8,128)(2,1)S(1)} %fusion.15), channel_id=1, source_target_pairs={{0,1},{1,128},{2,3},{3,130},{4,5},{5,132},{6,7},{7,134},{8,9},{9,1... | collective-permute-start | bytes 3145736 | tf_op jit(solution)/shard_map/ppermute | solution.py:102
  7.3 1.7 %dynamic-slice_bitcast_fusion.2 = (bf16[512,1024]{1,0:T(8,128)(2,1)S(1)}, bf16[512,1024]{1,0:T(8,128)(2,1)S(1)}) fusion(bf16[1,4,2,512,1024]{4,3,2,1,0:T(8,128)(2,1)} %param.4, s32[]{:T(128)S(6)} %select_n.44, s32[]{:T(128)S(6)} %select_n.42), kind=kLoop, calls=%fused_computation.37 | loop fusion | bytes 4194312 | tf_op jit(solution)/shard_map/reshape | solution.py:95
  9.0 1.2 %collective-permute-start.1 = (bf16[512,1024]{1,0:T(8,128)(2,1)S(1)}, bf16[512,1024]{1,0:T(8,128)(2,1)}, u32[]{:S(2)}, u32[]{:S(2)}) collective-permute-start(bf16[512,1024]{1,0:T(8,128)(2,1)S(1)} %get-tuple-element.15), channel_id=1, source_target_pairs={{0,64},{64,0},{128,192},{192,128},{1,65},{65,1},{129,193},{193,129... | collective-permute-start | bytes 3145736 | tf_op jit(solution)/shard_map/ppermute | solution.py:100
  10.2 0.1 collective-permute-start.4
  10.3 11.6 %collective-permute-done.2 = bf16[512,1024]{1,0:T(8,128)(2,1)} collective-permute-done((bf16[512,1024]{1,0:T(8,128)(2,1)S(1)}, bf16[512,1024]{1,0:T(8,128)(2,1)}, u32[]{:S(2)}, u32[]{:S(2)}) %collective-permute-start.2) | collective-permute-done | bytes 1048608 | tf_op jit(solution)/shard_map/ppermute | solution.py:102
  21.9 0.3 collective-permute-start.3
  22.2 15.9 %collective-permute-done.3 = bf16[512,1024]{1,0:T(8,128)(2,1)S(1)} collective-permute-done((bf16[512,1024]{1,0:T(8,128)(2,1)}, bf16[512,1024]{1,0:T(8,128)(2,1)S(1)}, u32[]{:S(2)}, u32[]{:S(2)}) %collective-permute-start.3) | collective-permute-done | bytes 1048608 | tf_op jit(solution)/shard_map/ppermute | solution.py:103
  38.1 3.4 %fusion.19 = (bf16[1,512,1024]{2,1,0:T(8,128)(2,1)S(1)}, bf16[512,1024]{1,0:T(8,128)(2,1)S(1)}) fusion(bf16[512,1024]{1,0:T(8,128)(2,1)S(1)} %collective-permute-done.3, bf16[512,1024]{1,0:T(8,128)(2,1)} %collective-permute-done.1, bf16[1,4,2,512,1024]{4,3,2,1,0:T(8,128)(2,1)} %param.4, s32[]{:T(128)S(6)} %select_n.43, ...), kind=kLoop, calls=%fused_computation.28 | loop fusion | flops 5242880 | bytes 7340040 | tf_op jit(solution)/shard_map/stack | solution.py:113
  41.5 0.1 collective-permute-start.6
  41.6 1.3 %dynamic-slice_bitcast_fusion = bf16[512,1024]{1,0:T(8,128)(2,1)S(1)} fusion(bf16[1,4,2,512,1024]{4,3,2,1,0:T(8,128)(2,1)} %param.4, s32[]{:T(128)S(6)} %select_n.44), kind=kLoop, calls=%fused_computation.35 | loop fusion | bytes 2097156 | tf_op jit(solution)/shard_map/reshape | solution.py:95
  42.9 0.4 collective-permute-start.5
  43.3 14.3 %collective-permute-done.6 = bf16[512,1024]{1,0:T(8,128)(2,1)S(1)} collective-permute-done((bf16[512,1024]{1,0:T(8,128)(2,1)S(1)}, bf16[512,1024]{1,0:T(8,128)(2,1)S(1)}, u32[]{:S(2)}, u32[]{:S(2)}) %collective-permute-start.6) | collective-permute-done | bytes 1048608 | tf_op jit(solution)/shard_map/ppermute | solution.py:102
  57.6 4.0 %fusion.24 = bf16[512,512]{1,0:T(8,128)(2,1)S(1)} fusion(), kind=kLoop, calls=%fused_computation.40 | loop fusion | flops 4194304 | bytes 524288 | tf_op jit(solution)/shard_map/convert.6
  61.6 4.6 %negate_convert_fusion = (bf16[512,512]{1,0:T(8,128)(2,1)S(1)}, bf16[512,512]{1,0:T(8,128)(2,1)S(1)}) fusion(), kind=kLoop, calls=%fused_computation.30 | loop fusion | flops 4980736 | bytes 1048576 | tf_op jit(solution)/shard_map/convert.9
  66.2 0.1 iota_compare_fusion
  66.3 7.3 %collective-permute-done.7 = bf16[512,1024]{1,0:T(8,128)(2,1)S(1)} collective-permute-done((bf16[512,1024]{1,0:T(8,128)(2,1)S(1)}, bf16[512,1024]{1,0:T(8,128)(2,1)S(1)}, u32[]{:S(2)}, u32[]{:S(2)}) %collective-permute-start.7) | collective-permute-done | bytes 1048608 | tf_op jit(solution)/shard_map/ppermute | solution.py:103
  73.6 1.9 %fusion.20 = bf16[1,512,1024]{2,1,0:T(8,128)(2,1)S(1)} fusion(bf16[512,1024]{1,0:T(8,128)(2,1)S(1)} %collective-permute-done.7, bf16[512,1024]{1,0:T(8,128)(2,1)S(1)} %collective-permute-done.5, bf16[1,4,2,512,1024]{4,3,2,1,0:T(8,128)(2,1)} %param.4, s32[]{:T(128)S(6)} %select_n.43), kind=kLoop, calls=%fused_computation.29 | loop fusion | flops 3145728 | bytes 4194308 | tf_op jit(solution)/shard_map/stack | solution.py:113
  75.5 2.3 %fusion = f32[2,512,1024]{2,1,0:T(8,128)S(1)} fusion(bf16[1,512,1024]{2,1,0:T(8,128)(2,1)S(1)} %fusion.20, bf16[1,512,1024]{2,1,0:T(8,128)(2,1)S(1)} %get-tuple-element.13, bf16[512,512]{1,0:T(8,128)(2,1)S(1)} %get-tuple-element.18, bf16[512,512]{1,0:T(8,128)(2,1)S(1)} %fusion.24, bf16[512,512]{1,0:T(8,128)(2,1)S(1)} %get-tuple-element.17), kind=kOutput, calls=%fused_computation | convolution fusion | flops 2156920832 | bytes 7864320 | tf_op jit(solution)/shard_map/bvt,tf->bvf/dot_general | solution.py:49
  77.8 3.7 %fusion.37 = f32[2,512,512]{2,1,0:T(8,128)S(1)} fusion(f32[2,512,1024]{2,1,0:T(8,128)S(1)} %fusion), kind=kOutput, calls=%fused_computation.62 | convolution fusion | flops 3221225472 | bytes 6291456 | tf_op jit(solution)/shard_map/bvf,bwf->bvw/dot_general | solution.py:50
  81.5 1.7 %fusion.25 = f32[2,512,16]{1,2,0:T(8,128)S(1)} fusion(f32[2,512,1024]{2,1,0:T(8,128)S(1)} %fusion, f32[16,1024]{1,0:T(8,128)S(1)} %copy-done), kind=kOutput, calls=%fused_computation.44 | convolution fusion | flops 100663296 | bytes 4325376 | tf_op jit(solution)/shard_map/kf,bvf->bkv/dot_general | solution.py:51
  83.2 0.6 fusion.38.rhs_ref
  83.9 0.2 fusion.39
  84.0 0.1 copy.5
  84.1 0.6 fusion.34.gram_ref
  84.7 2.9 %shard_map.46 = f32[2,16,512]{2,1,0:T(8,128)} custom-call(f32[2,16,16]{2,1,0:T(8,128)} %fusion.34.gram_ref, f32[2,16,512]{2,1,0:T(8,128)} %copy-done.3), custom_call_target="tpu_custom_call" | custom-call | tf_op jit(solution)/shard_map/pallas_call | solution.py:42
  87.6 1.5 %fusion.40.rhs_ref = f32[2,16,512]{2,1,0:T(8,128)S(1)} fusion(f32[2,16,512]{2,1,0:T(8,128)} %shard_map.46, f32[2,512,512]{2,1,0:T(8,128)S(1)} %fusion.37), kind=kOutput, calls=%fused_computation.65 | convolution fusion | flops 50331648 | bytes 2228224 | tf_op jit(solution)/shard_map/bkv,bvw->bkw/dot_general | solution.py:53
  89.2 0.0 copy-start.4
  89.2 0.2 fusion.41
  89.3 0.1 copy.6
  89.4 0.6 fusion.33.gram_ref
  90.0 2.9 %shard_map.47 = f32[2,16,512]{2,1,0:T(8,128)} custom-call(f32[2,16,16]{2,1,0:T(8,128)} %fusion.33.gram_ref, f32[2,16,512]{2,1,0:T(8,128)} %copy-done.4), custom_call_target="tpu_custom_call" | custom-call | tf_op jit(solution)/shard_map/pallas_call | solution.py:42
  92.9 1.5 %fusion.42.rhs_ref = f32[2,16,512]{2,1,0:T(8,128)S(1)} fusion(f32[2,16,512]{2,1,0:T(8,128)} %shard_map.47, f32[2,512,512]{2,1,0:T(8,128)S(1)} %fusion.37), kind=kOutput, calls=%fused_computation.67 | convolution fusion | flops 50331648 | bytes 2228224 | tf_op jit(solution)/shard_map/bkv,bvw->bkw/dot_general | solution.py:53
  94.5 0.2 fusion.43
  94.6 0.1 copy.7
  94.7 0.6 fusion.32.gram_ref
  95.3 2.9 %shard_map.48 = f32[2,16,512]{2,1,0:T(8,128)} custom-call(f32[2,16,16]{2,1,0:T(8,128)} %fusion.32.gram_ref, f32[2,16,512]{2,1,0:T(8,128)} %copy-done.5), custom_call_target="tpu_custom_call" | custom-call | tf_op jit(solution)/shard_map/pallas_call | solution.py:42
  98.2 3.4 %fusion.46 = f32[2,16,1024]{2,1,0:T(8,128)S(1)} fusion(f32[2,16,512]{2,1,0:T(8,128)} %shard_map.48, f32[2,512,1024]{2,1,0:T(8,128)} %copy-done.1), kind=kOutput, calls=%fused_computation.71 | convolution fusion | flops 100663296 | bytes 4390912 | tf_op jit(solution)/shard_map/bkv,bvf->bkf/dot_general | solution.py:58
  101.6 0.6 fusion.44
  102.2 0.2 fusion.45
  102.4 0.7 pad_maximum_fusion.rhs_ref
  103.1 0.1 copy.8
  103.2 0.6 fusion.31.gram_ref
  103.8 3.1 %shard_map.49 = f32[2,16,1536]{2,1,0:T(8,128)} custom-call(f32[2,16,16]{2,1,0:T(8,128)} %fusion.31.gram_ref, f32[2,16,1536]{2,1,0:T(8,128)} %pad_maximum_fusion.rhs_ref), custom_call_target="tpu_custom_call" | custom-call | tf_op jit(solution)/shard_map/pallas_call | solution.py:42
  106.9 4.2 %convert_select_fusion = bf16[2,512,1024]{2,1,0:T(8,128)(2,1)} fusion(pred[2]{0:T(512)(128)(4,1)S(1)} %broadcast_compare_fusion, f32[2,16,1536]{2,1,0:T(8,128)} %shard_map.49, pred[2,16]{1,0:T(4,128)(4,1)S(1)} %iota_compare_fusion), kind=kOutput, calls=%fused_computation.21 | convolution fusion | flops 102809600 | bytes 2295296 | tf_op jit(solution)/shard_map/bkv,bkf->bvf/dot_general | solution.py:65
  (24 shorter events, 0.1 us)
Async XLA Ops:
  0.0 81.5 %copy-start = (f32[16,1024]{1,0:T(8,128)S(1)}, f32[16,1024]{1,0:T(8,128)}, u32[]{:S(2)}) copy-start(f32[16,1024]{1,0:T(8,128)} %param.7) | copy-start | bytes 196612
  1.3 2.7 %collective-permute-start = (bf16[512,1024]{1,0:T(8,128)(2,1)S(1)}, bf16[512,1024]{1,0:T(8,128)(2,1)S(1)}, u32[]{:S(2)}, u32[]{:S(2)}) collective-permute-start(bf16[512,1024]{1,0:T(8,128)(2,1)S(1)} %dynamic-slice_bitcast_fusion.3), channel_id=1, source_target_pairs={{0,64},{64,0},{128,192},{192,128},{1,65},{65,1},{129,193},{193,129... | collective-permute-start | bytes 3145736 | tf_op jit(solution)/shard_map/ppermute | solution.py:97
  5.7 16.2 %collective-permute-start.2 = (bf16[512,1024]{1,0:T(8,128)(2,1)S(1)}, bf16[512,1024]{1,0:T(8,128)(2,1)}, u32[]{:S(2)}, u32[]{:S(2)}) collective-permute-start(bf16[512,1024]{1,0:T(8,128)(2,1)S(1)} %fusion.15), channel_id=1, source_target_pairs={{0,1},{1,128},{2,3},{3,130},{4,5},{5,132},{6,7},{7,134},{8,9},{9,1... | collective-permute-start | bytes 3145736 | tf_op jit(solution)/shard_map/ppermute | solution.py:102
  9.0 13.2 %collective-permute-start.1 = (bf16[512,1024]{1,0:T(8,128)(2,1)S(1)}, bf16[512,1024]{1,0:T(8,128)(2,1)}, u32[]{:S(2)}, u32[]{:S(2)}) collective-permute-start(bf16[512,1024]{1,0:T(8,128)(2,1)S(1)} %get-tuple-element.15), channel_id=1, source_target_pairs={{0,64},{64,0},{128,192},{192,128},{1,65},{65,1},{129,193},{193,129... | collective-permute-start | bytes 3145736 | tf_op jit(solution)/shard_map/ppermute | solution.py:100
  10.2 12.0 %collective-permute-start.4 = (bf16[512,1024]{1,0:T(8,128)(2,1)S(1)}, bf16[512,1024]{1,0:T(8,128)(2,1)}, u32[]{:S(2)}, u32[]{:S(2)}) collective-permute-start(bf16[512,1024]{1,0:T(8,128)(2,1)S(1)} %get-tuple-element.16), channel_id=1, source_target_pairs={{0,64},{64,0},{128,192},{192,128},{1,65},{65,1},{129,193},{193,129... | collective-permute-start | bytes 3145736 | tf_op jit(solution)/shard_map/ppermute | solution.py:97
  21.9 16.2 %collective-permute-start.3 = (bf16[512,1024]{1,0:T(8,128)(2,1)}, bf16[512,1024]{1,0:T(8,128)(2,1)S(1)}, u32[]{:S(2)}, u32[]{:S(2)}) collective-permute-start(bf16[512,1024]{1,0:T(8,128)(2,1)} %collective-permute-done.2), channel_id=1, source_target_pairs={{0,1},{1,128},{2,3},{3,130},{4,5},{5,132},{6,7},{7,134},{8,9},{9,1... | collective-permute-start | bytes 3145736 | tf_op jit(solution)/shard_map/ppermute | solution.py:103
  41.5 24.7 %copy-start.8 = (s32[2]{0:T(128)S(1)}, s32[2]{0:T(128)}, u32[]{:S(2)}) copy-start(s32[2]{0:T(128)} %param.5) | copy-start | bytes 28
  41.5 24.7 %copy-start.9 = (s32[2]{0:T(128)S(1)}, s32[2]{0:T(128)}, u32[]{:S(2)}) copy-start(s32[2]{0:T(128)} %param.6) | copy-start | bytes 28
  41.5 16.1 %collective-permute-start.6 = (bf16[512,1024]{1,0:T(8,128)(2,1)S(1)}, bf16[512,1024]{1,0:T(8,128)(2,1)S(1)}, u32[]{:S(2)}, u32[]{:S(2)}) collective-permute-start(bf16[512,1024]{1,0:T(8,128)(2,1)S(1)} %get-tuple-element.12), channel_id=1, source_target_pairs={{0,1},{1,128},{2,3},{3,130},{4,5},{5,132},{6,7},{7,134},{8,9},{9,1... | collective-permute-start | bytes 3145736 | tf_op jit(solution)/shard_map/ppermute | solution.py:102
  42.9 23.4 %collective-permute-start.5 = (bf16[512,1024]{1,0:T(8,128)(2,1)S(1)}, bf16[512,1024]{1,0:T(8,128)(2,1)S(1)}, u32[]{:S(2)}, u32[]{:S(2)}) collective-permute-start(bf16[512,1024]{1,0:T(8,128)(2,1)S(1)} %dynamic-slice_bitcast_fusion), channel_id=1, source_target_pairs={{0,64},{64,0},{128,192},{192,128},{1,65},{65,1},{129,193},{193,129... | collective-permute-start | bytes 3145736 | tf_op jit(solution)/shard_map/ppermute | solution.py:100
  57.6 16.0 %collective-permute-start.7 = (bf16[512,1024]{1,0:T(8,128)(2,1)S(1)}, bf16[512,1024]{1,0:T(8,128)(2,1)S(1)}, u32[]{:S(2)}, u32[]{:S(2)}) collective-permute-start(bf16[512,1024]{1,0:T(8,128)(2,1)S(1)} %collective-permute-done.6), channel_id=1, source_target_pairs={{0,1},{1,128},{2,3},{3,130},{4,5},{5,132},{6,7},{7,134},{8,9},{9,1... | collective-permute-start | bytes 3145736 | tf_op jit(solution)/shard_map/ppermute | solution.py:103
  77.8 3.7 %copy-start.1 = (f32[2,512,1024]{2,1,0:T(8,128)}, f32[2,512,1024]{2,1,0:T(8,128)S(1)}, u32[]{:S(2)}) copy-start(f32[2,512,1024]{2,1,0:T(8,128)S(1)} %fusion) | copy-start | bytes 12582916
  83.9 0.9 copy-start.3
  87.6 1.5 %copy-start.6 = (f32[2,16,512]{2,1,0:T(8,128)S(1)}, f32[2,16,512]{2,1,0:T(8,128)}, u32[]{:S(2)}) copy-start(f32[2,16,512]{2,1,0:T(8,128)} %shard_map.46) | copy-start | bytes 196612
  89.2 0.9 copy-start.4
  92.9 1.5 %copy-start.7 = (f32[2,16,512]{2,1,0:T(8,128)S(1)}, f32[2,16,512]{2,1,0:T(8,128)}, u32[]{:S(2)}) copy-start(f32[2,16,512]{2,1,0:T(8,128)} %shard_map.47) | copy-start | bytes 196612
  94.4 0.9 copy-start.5
  98.2 3.4 %copy-start.2 = (f32[2,16,512]{2,1,0:T(8,128)S(1)}, f32[2,16,512]{2,1,0:T(8,128)}, u32[]{:S(2)}) copy-start(f32[2,16,512]{2,1,0:T(8,128)} %shard_map.48) | copy-start | bytes 196612

commit v9 on v7

--- a/solution.py
+++ b/solution.py
@@ -55,14 +55,14 @@
         if sweep_index < ITERS - 1:
             coeff = factor_solve(inner_gram, pushed)
         else:
-            image = jnp.einsum("bkv,bvf->bkf", coeff, spectra, precision=HI)
+            image = jnp.einsum("bkv,bvf->bkf", coeff, spectra, preferred_element_type=jnp.float32)
             both = factor_solve(inner_gram, jnp.concatenate([pushed, image], axis=-1))
             coeff = both[..., : pushed.shape[-1]]
             subspace = both[..., pushed.shape[-1]:]
     keep_rows = jnp.arange(subspace.shape[1], dtype=jnp.int32)[None, :, None] < ranks[:, None, None]
     truncated = jnp.where(keep_rows, subspace, 0.0)
     coefficients = jnp.where(keep_rows, coeff, 0.0)
-    result = jnp.einsum("bkv,bkf->bvf", coefficients, truncated, precision=HI)
+    result = jnp.einsum("bkv,bkf->bvf", coefficients, truncated, preferred_element_type=jnp.float32)
     result = result.astype(jnp.bfloat16)
     return jnp.where(flags[:, None, None], result, jnp.zeros_like(result))
 

time: 102 us -> 100 us (0.980)
  matrix products: 20.4 us -> 18.4 us
    dot_general x2, matrix products: 7.58 us -> 5.77 us  [the longest x1 3.13 us: denoise_batch(): jnp.einsum('bkv,bkf->bvf', coefficients, truncated, preferred_element_typ...]
where the time goes in v9:
time: 100 us; the launch traced here: 99.1 us
  waiting for transfers between devices  41.1 us (41%)
  other arithmetic  18.9 us (19%)
  matrix products  18.4 us (18%)
  Pallas kernels  11.8 us (12%)
  starting transfers between devices  4.64 us (5%)
  local copies, waits for them, and re-layouts  4.18 us (4%)
    ppermute x2, waiting for transfers between devices, coil_sum(): hop = lax.ppermute(forward, ('coil', 'slab'), pairs)  23.6 us
    ppermute x2, waiting for transfers between devices, coil_sum(): hop = lax.ppermute(hop, ('coil', 'slab'), pairs)  13.5 us
    pallas_call x4, Pallas kernels, factor_solve(): pl.pallas_call(factor_solve_kernel, out_shape=jax.ShapeDtypeStruct(rhs.sh...  11.8 us
    another operation x2, other arithmetic  8.56 us
    dot_general x4, matrix products, denoise_batch(): pushed = jnp.einsum('bkv,bvw->bkw', coeff, kernel, precision=HI)  4.29 us
    ppermute x2, waiting for transfers between devices, coil_sum(): got_forward = lax.ppermute(pick(coil ^ 3), 'coil', chip_pair)  3.99 us
    another operation x1, other arithmetic, body(): jnp.stack([(own + hop.astype(jnp.float32)).astype(jnp.bfloat16) for own,...  3.95 us
    reshape x1, local copies, waits for them, and re-layouts, pick(): return block.reshape(partial_time.shape[3:])  3.84 us
  transfers between devices with their start and end apart: 8, of which 6 were waited for; matrix products, arithmetic and copies ran while one was open for 9% of the time, Pallas kernels for 0%

profile of v9, /device:TPU:64, one launch (start us, length us, event | category | flops | bytes accessed | tf_op | source)
XLA Modules:
  0.0 99.1 jit_solution(12967227094125847751)
XLA Ops:
  0.0 3.8 %dynamic-slice_bitcast_fusion.3 = (bf16[512,1024]{1,0:T(8,128)(2,1)S(1)}, bf16[512,1024]{1,0:T(8,128)(2,1)S(1)}, bf16[512,1024]{1,0:T(8,128)(2,1)}, bf16[512,1024]{1,0:T(8,128)(2,1)S(1)}) fusion(bf16[1,4,2,512,1024]{4,3,2,1,0:T(8,128)(2,1)} %param.4, s32[]{:T(128)S(6)} %select_n.42, s32[]{:T(128)S(6)} %select_n.44), kind=kLoop, calls=%fused_computation.38 | loop fusion | bytes 8388616 | tf_op jit(solution)/shard_map/reshape | solution.py:94
  3.8 0.0 collective-permute-start.1
  3.8 0.5 collective-permute-start.5
  4.4 2.5 %collective-permute-done.1 = bf16[512,1024]{1,0:T(8,128)(2,1)} collective-permute-done((bf16[512,1024]{1,0:T(8,128)(2,1)}, bf16[512,1024]{1,0:T(8,128)(2,1)}, u32[]{:S(2)}, u32[]{:S(2)}) %collective-permute-start.1) | collective-permute-done | bytes 1048608 | tf_op jit(solution)/shard_map/ppermute | solution.py:96
  6.8 1.5 %collective-permute-done.5 = bf16[512,1024]{1,0:T(8,128)(2,1)} collective-permute-done((bf16[512,1024]{1,0:T(8,128)(2,1)S(1)}, bf16[512,1024]{1,0:T(8,128)(2,1)}, u32[]{:S(2)}, u32[]{:S(2)}) %collective-permute-start.5) | collective-permute-done | bytes 1048608 | tf_op jit(solution)/shard_map/ppermute | solution.py:96
  8.3 3.1 %fusion.13 = (bf16[512,1024]{1,0:T(8,128)(2,1)S(1)}, bf16[512,1024]{1,0:T(8,128)(2,1)S(1)}) fusion(bf16[512,1024]{1,0:T(8,128)(2,1)} %collective-permute-done.1, bf16[1,4,2,512,1024]{4,3,2,1,0:T(8,128)(2,1)} %param.4, s32[]{:T(128)S(6)} %select_n.43, bf16[512,1024]{1,0:T(8,128)(2,1)} %collective-permute-done.5), kind=kLoop, calls=%fused_computation.17 | loop fusion | flops 4194304 | bytes 6291460 | tf_op jit(solution)/shard_map/convert_element_type | solution.py:97
  11.5 1.6 %collective-permute-start.2 = (bf16[512,1024]{1,0:T(8,128)(2,1)S(1)}, bf16[512,1024]{1,0:T(8,128)(2,1)}, u32[]{:S(2)}, u32[]{:S(2)}) collective-permute-start(bf16[512,1024]{1,0:T(8,128)(2,1)S(1)} %get-tuple-element.11), channel_id=1, source_target_pairs={{0,1},{1,128},{2,3},{3,130},{4,5},{5,132},{6,7},{7,134},{8,9},{9,1... | collective-permute-start | bytes 3145736 | tf_op jit(solution)/shard_map/ppermute | solution.py:100
  13.0 1.5 %collective-permute-start.6 = (bf16[512,1024]{1,0:T(8,128)(2,1)S(1)}, bf16[512,1024]{1,0:T(8,128)(2,1)}, u32[]{:S(2)}, u32[]{:S(2)}) collective-permute-start(bf16[512,1024]{1,0:T(8,128)(2,1)S(1)} %get-tuple-element.12), channel_id=1, source_target_pairs={{0,1},{1,128},{2,3},{3,130},{4,5},{5,132},{6,7},{7,134},{8,9},{9,1... | collective-permute-start | bytes 3145736 | tf_op jit(solution)/shard_map/ppermute | solution.py:100
  14.5 0.2 collective-permute-start
  14.7 0.3 collective-permute-start.4
  15.0 12.6 %collective-permute-done.2 = bf16[512,1024]{1,0:T(8,128)(2,1)} collective-permute-done((bf16[512,1024]{1,0:T(8,128)(2,1)S(1)}, bf16[512,1024]{1,0:T(8,128)(2,1)}, u32[]{:S(2)}, u32[]{:S(2)}) %collective-permute-start.2) | collective-permute-done | bytes 1048608 | tf_op jit(solution)/shard_map/ppermute | solution.py:100
  27.7 0.3 collective-permute-start.3
  27.9 11.0 %collective-permute-done.6 = bf16[512,1024]{1,0:T(8,128)(2,1)} collective-permute-done((bf16[512,1024]{1,0:T(8,128)(2,1)S(1)}, bf16[512,1024]{1,0:T(8,128)(2,1)}, u32[]{:S(2)}, u32[]{:S(2)}) %collective-permute-start.6) | collective-permute-done | bytes 1048608 | tf_op jit(solution)/shard_map/ppermute | solution.py:100
  38.9 0.3 collective-permute-start.7
  39.2 4.0 %fusion.24 = bf16[512,512]{1,0:T(8,128)(2,1)S(1)} fusion(), kind=kLoop, calls=%fused_computation.40 | loop fusion | flops 4194304 | bytes 524288 | tf_op jit(solution)/shard_map/convert.6
  43.2 4.6 %negate_convert_fusion = (bf16[512,512]{1,0:T(8,128)(2,1)S(1)}, bf16[512,512]{1,0:T(8,128)(2,1)S(1)}) fusion(), kind=kLoop, calls=%fused_computation.30 | loop fusion | flops 4980736 | bytes 1048576 | tf_op jit(solution)/shard_map/convert.9
  47.8 0.1 iota_compare_fusion
  47.9 2.3 %collective-permute-done.3 = bf16[512,1024]{1,0:T(8,128)(2,1)} collective-permute-done((bf16[512,1024]{1,0:T(8,128)(2,1)}, bf16[512,1024]{1,0:T(8,128)(2,1)}, u32[]{:S(2)}, u32[]{:S(2)}) %collective-permute-start.3) | collective-permute-done | bytes 1048608 | tf_op jit(solution)/shard_map/ppermute | solution.py:101
  50.1 11.2 %collective-permute-done.7 = bf16[512,1024]{1,0:T(8,128)(2,1)} collective-permute-done((bf16[512,1024]{1,0:T(8,128)(2,1)}, bf16[512,1024]{1,0:T(8,128)(2,1)}, u32[]{:S(2)}, u32[]{:S(2)}) %collective-permute-start.7) | collective-permute-done | bytes 1048608 | tf_op jit(solution)/shard_map/ppermute | solution.py:101
  61.4 4.0 %fusion.19 = (bf16[1,512,1024]{2,1,0:T(8,128)(2,1)S(1)}, bf16[1,512,1024]{2,1,0:T(8,128)(2,1)S(1)}) fusion(bf16[512,1024]{1,0:T(8,128)(2,1)} %collective-permute-done.3, bf16[512,1024]{1,0:T(8,128)(2,1)S(1)} %collective-permute-done, bf16[1,4,2,512,1024]{4,3,2,1,0:T(8,128)(2,1)} %param.4, s32[]{:T(128)S(6)} %select_n.41, ...), kind=kLoop, calls=%fused_computation.28 | loop fusion | flops 6291456 | bytes 8388612 | tf_op jit(solution)/shard_map/stack | solution.py:111
  65.3 2.3 %fusion = f32[2,512,1024]{2,1,0:T(8,128)S(1)} fusion(bf16[1,512,1024]{2,1,0:T(8,128)(2,1)S(1)} %get-tuple-element.6, bf16[1,512,1024]{2,1,0:T(8,128)(2,1)S(1)} %get-tuple-element.5, bf16[512,512]{1,0:T(8,128)(2,1)S(1)} %get-tuple-element.14, bf16[512,512]{1,0:T(8,128)(2,1)S(1)} %fusion.24, bf16[512,512]{1,0:T(8,128)(2,1)S(1)} %get-tuple-element.13), kind=kOutput, calls=%fused_computation | convolution fusion | flops 2156920832 | bytes 7864320 | tf_op jit(solution)/shard_map/bvt,tf->bvf/dot_general | solution.py:49
  67.7 3.7 %fusion.37 = f32[2,512,512]{2,1,0:T(8,128)S(1)} fusion(f32[2,512,1024]{2,1,0:T(8,128)S(1)} %fusion), kind=kOutput, calls=%fused_computation.62 | convolution fusion | flops 3221225472 | bytes 6291456 | tf_op jit(solution)/shard_map/bvf,bwf->bvw/dot_general | solution.py:50
  71.3 1.7 %fusion.25 = f32[2,512,16]{1,2,0:T(8,128)S(1)} fusion(f32[2,512,1024]{2,1,0:T(8,128)S(1)} %fusion, f32[16,1024]{1,0:T(8,128)S(1)} %copy-done), kind=kOutput, calls=%fused_computation.44 | convolution fusion | flops 100663296 | bytes 4325376 | tf_op jit(solution)/shard_map/kf,bvf->bkv/dot_general | solution.py:51
  73.1 0.6 fusion.38.rhs_ref
  73.7 0.2 fusion.39
  73.9 0.1 copy.5
  73.9 0.6 fusion.34.gram_ref
  74.6 2.9 %shard_map.46 = f32[2,16,512]{2,1,0:T(8,128)} custom-call(f32[2,16,16]{2,1,0:T(8,128)} %fusion.34.gram_ref, f32[2,16,512]{2,1,0:T(8,128)} %copy-done.3), custom_call_target="tpu_custom_call" | custom-call | tf_op jit(solution)/shard_map/pallas_call | solution.py:42
  77.5 1.5 %fusion.40.rhs_ref = f32[2,16,512]{2,1,0:T(8,128)S(1)} fusion(f32[2,16,512]{2,1,0:T(8,128)} %shard_map.46, f32[2,512,512]{2,1,0:T(8,128)S(1)} %fusion.37), kind=kOutput, calls=%fused_computation.65 | convolution fusion | flops 50331648 | bytes 2228224 | tf_op jit(solution)/shard_map/bkv,bvw->bkw/dot_general | solution.py:53
  79.0 0.0 copy-start.4
  79.0 0.2 fusion.41
  79.2 0.1 copy.6
  79.2 0.6 fusion.33.gram_ref
  79.9 2.9 %shard_map.47 = f32[2,16,512]{2,1,0:T(8,128)} custom-call(f32[2,16,16]{2,1,0:T(8,128)} %fusion.33.gram_ref, f32[2,16,512]{2,1,0:T(8,128)} %copy-done.4), custom_call_target="tpu_custom_call" | custom-call | tf_op jit(solution)/shard_map/pallas_call | solution.py:42
  82.7 1.5 %fusion.42.rhs_ref = f32[2,16,512]{2,1,0:T(8,128)S(1)} fusion(f32[2,16,512]{2,1,0:T(8,128)} %shard_map.47, f32[2,512,512]{2,1,0:T(8,128)S(1)} %fusion.37), kind=kOutput, calls=%fused_computation.67 | convolution fusion | flops 50331648 | bytes 2228224 | tf_op jit(solution)/shard_map/bkv,bvw->bkw/dot_general | solution.py:53
  84.3 0.0 copy-start.5
  84.3 0.2 fusion.43
  84.4 0.1 copy.7
  84.5 0.6 fusion.32.gram_ref
  85.1 2.9 %shard_map.48 = f32[2,16,512]{2,1,0:T(8,128)} custom-call(f32[2,16,16]{2,1,0:T(8,128)} %fusion.32.gram_ref, f32[2,16,512]{2,1,0:T(8,128)} %copy-done.5), custom_call_target="tpu_custom_call" | custom-call | tf_op jit(solution)/shard_map/pallas_call | solution.py:42
  88.0 2.6 %fusion.46 = f32[2,16,1024]{2,1,0:T(8,128)S(1)} fusion(f32[2,16,512]{2,1,0:T(8,128)} %shard_map.48, f32[2,512,1024]{2,1,0:T(8,128)} %copy-done.1), kind=kOutput, calls=%fused_computation.71 | convolution fusion | flops 33554432 | bytes 4390912 | tf_op jit(solution)/shard_map/bkv,bvf->bkf/dot_general | solution.py:58
  90.7 0.6 fusion.44
  91.3 0.2 fusion.45
  91.4 0.7 pad_maximum_fusion.rhs_ref
  92.1 0.1 copy.8
  92.2 0.6 fusion.31.gram_ref
  92.8 3.1 %shard_map.49 = f32[2,16,1536]{2,1,0:T(8,128)} custom-call(f32[2,16,16]{2,1,0:T(8,128)} %fusion.31.gram_ref, f32[2,16,1536]{2,1,0:T(8,128)} %pad_maximum_fusion.rhs_ref), custom_call_target="tpu_custom_call" | custom-call | tf_op jit(solution)/shard_map/pallas_call | solution.py:42
  95.9 3.1 %convert_select_fusion = bf16[2,512,1024]{2,1,0:T(8,128)(2,1)} fusion(pred[2]{0:T(512)(128)(4,1)S(1)} %broadcast_compare_fusion, f32[2,16,1536]{2,1,0:T(8,128)} %shard_map.49, pred[2,16]{1,0:T(4,128)(4,1)S(1)} %iota_compare_fusion), kind=kOutput, calls=%fused_computation.21 | convolution fusion | flops 34652160 | bytes 2196992 | tf_op jit(solution)/shard_map/bkv,bkf->bvf/dot_general | solution.py:65
  (21 shorter events, 0.0 us)
Async XLA Ops:
  0.0 71.3 %copy-start = (f32[16,1024]{1,0:T(8,128)S(1)}, f32[16,1024]{1,0:T(8,128)}, u32[]{:S(2)}) copy-start(f32[16,1024]{1,0:T(8,128)} %param.7) | copy-start | bytes 196612
  3.8 3.0 %collective-permute-start.1 = (bf16[512,1024]{1,0:T(8,128)(2,1)}, bf16[512,1024]{1,0:T(8,128)(2,1)}, u32[]{:S(2)}, u32[]{:S(2)}) collective-permute-start(bf16[512,1024]{1,0:T(8,128)(2,1)} %get-tuple-element.9), channel_id=1, source_target_pairs={{0,64},{64,0},{128,192},{192,128},{1,65},{65,1},{129,193},{193,129... | collective-permute-start | bytes 3145736 | tf_op jit(solution)/shard_map/ppermute | solution.py:96
  3.8 4.5 %collective-permute-start.5 = (bf16[512,1024]{1,0:T(8,128)(2,1)S(1)}, bf16[512,1024]{1,0:T(8,128)(2,1)}, u32[]{:S(2)}, u32[]{:S(2)}) collective-permute-start(bf16[512,1024]{1,0:T(8,128)(2,1)S(1)} %get-tuple-element.10), channel_id=1, source_target_pairs={{0,64},{64,0},{128,192},{192,128},{1,65},{65,1},{129,193},{193,129... | collective-permute-start | bytes 3145736 | tf_op jit(solution)/shard_map/ppermute | solution.py:96
  4.4 43.4 %copy-start.8 = (s32[2]{0:T(128)S(1)}, s32[2]{0:T(128)}, u32[]{:S(2)}) copy-start(s32[2]{0:T(128)} %param.5) | copy-start | bytes 28
  4.4 43.4 %copy-start.9 = (s32[2]{0:T(128)S(1)}, s32[2]{0:T(128)}, u32[]{:S(2)}) copy-start(s32[2]{0:T(128)} %param.6) | copy-start | bytes 28
  11.5 16.2 %collective-permute-start.2 = (bf16[512,1024]{1,0:T(8,128)(2,1)S(1)}, bf16[512,1024]{1,0:T(8,128)(2,1)}, u32[]{:S(2)}, u32[]{:S(2)}) collective-permute-start(bf16[512,1024]{1,0:T(8,128)(2,1)S(1)} %get-tuple-element.11), channel_id=1, source_target_pairs={{0,1},{1,128},{2,3},{3,130},{4,5},{5,132},{6,7},{7,134},{8,9},{9,1... | collective-permute-start | bytes 3145736 | tf_op jit(solution)/shard_map/ppermute | solution.py:100
  13.0 25.9 %collective-permute-start.6 = (bf16[512,1024]{1,0:T(8,128)(2,1)S(1)}, bf16[512,1024]{1,0:T(8,128)(2,1)}, u32[]{:S(2)}, u32[]{:S(2)}) collective-permute-start(bf16[512,1024]{1,0:T(8,128)(2,1)S(1)} %get-tuple-element.12), channel_id=1, source_target_pairs={{0,1},{1,128},{2,3},{3,130},{4,5},{5,132},{6,7},{7,134},{8,9},{9,1... | collective-permute-start | bytes 3145736 | tf_op jit(solution)/shard_map/ppermute | solution.py:100
  14.5 33.3 %collective-permute-start = (bf16[512,1024]{1,0:T(8,128)(2,1)S(1)}, bf16[512,1024]{1,0:T(8,128)(2,1)S(1)}, u32[]{:S(2)}, u32[]{:S(2)}) collective-permute-start(bf16[512,1024]{1,0:T(8,128)(2,1)S(1)} %get-tuple-element.7), channel_id=1, source_target_pairs={{0,64},{64,0},{128,192},{192,128},{1,65},{65,1},{129,193},{193,129... | collective-permute-start | bytes 3145736 | tf_op jit(solution)/shard_map/ppermute | solution.py:98
  14.7 33.2 %collective-permute-start.4 = (bf16[512,1024]{1,0:T(8,128)(2,1)S(1)}, bf16[512,1024]{1,0:T(8,128)(2,1)}, u32[]{:S(2)}, u32[]{:S(2)}) collective-permute-start(bf16[512,1024]{1,0:T(8,128)(2,1)S(1)} %get-tuple-element.8), channel_id=1, source_target_pairs={{0,64},{64,0},{128,192},{192,128},{1,65},{65,1},{129,193},{193,129... | collective-permute-start | bytes 3145736 | tf_op jit(solution)/shard_map/ppermute | solution.py:98
  27.7 22.5 %collective-permute-start.3 = (bf16[512,1024]{1,0:T(8,128)(2,1)}, bf16[512,1024]{1,0:T(8,128)(2,1)}, u32[]{:S(2)}, u32[]{:S(2)}) collective-permute-start(bf16[512,1024]{1,0:T(8,128)(2,1)} %collective-permute-done.2), channel_id=1, source_target_pairs={{0,1},{1,128},{2,3},{3,130},{4,5},{5,132},{6,7},{7,134},{8,9},{9,1... | collective-permute-start | bytes 3145736 | tf_op jit(solution)/shard_map/ppermute | solution.py:101
  38.9 22.5 %collective-permute-start.7 = (bf16[512,1024]{1,0:T(8,128)(2,1)}, bf16[512,1024]{1,0:T(8,128)(2,1)}, u32[]{:S(2)}, u32[]{:S(2)}) collective-permute-start(bf16[512,1024]{1,0:T(8,128)(2,1)} %collective-permute-done.6), channel_id=1, source_target_pairs={{0,1},{1,128},{2,3},{3,130},{4,5},{5,132},{6,7},{7,134},{8,9},{9,1... | collective-permute-start | bytes 3145736 | tf_op jit(solution)/shard_map/ppermute | solution.py:101
  67.7 3.7 %copy-start.1 = (f32[2,512,1024]{2,1,0:T(8,128)}, f32[2,512,1024]{2,1,0:T(8,128)S(1)}, u32[]{:S(2)}) copy-start(f32[2,512,1024]{2,1,0:T(8,128)S(1)} %fusion) | copy-start | bytes 12582916
  73.7 0.9 copy-start.3
  77.5 1.5 %copy-start.6 = (f32[2,16,512]{2,1,0:T(8,128)S(1)}, f32[2,16,512]{2,1,0:T(8,128)}, u32[]{:S(2)}) copy-start(f32[2,16,512]{2,1,0:T(8,128)} %shard_map.46) | copy-start | bytes 196612
  79.0 0.9 copy-start.4
  82.7 1.5 %copy-start.7 = (f32[2,16,512]{2,1,0:T(8,128)S(1)}, f32[2,16,512]{2,1,0:T(8,128)}, u32[]{:S(2)}) copy-start(f32[2,16,512]{2,1,0:T(8,128)} %shard_map.47) | copy-start | bytes 196612
  84.3 0.9 copy-start.5
  88.0 2.6 %copy-start.2 = (f32[2,16,512]{2,1,0:T(8,128)S(1)}, f32[2,16,512]{2,1,0:T(8,128)}, u32[]{:S(2)}) copy-start(f32[2,16,512]{2,1,0:T(8,128)} %shard_map.48) | copy-start | bytes 196612

commit v10 on v9

--- a/solution.py
+++ b/solution.py
@@ -45,8 +45,7 @@
     )(sym, rhs)
 
 
-def denoise_batch(patches, flags, ranks, transform, start_basis):
-    spectra = jnp.einsum("bvt,tf->bvf", patches, transform, preferred_element_type=jnp.float32)
+def denoise_batch(spectra, flags, ranks, start_basis):
     kernel = jnp.einsum("bvf,bwf->bvw", spectra, spectra, precision=HI)
     coeff = jnp.einsum("kf,bvf->bkv", start_basis, spectra, precision=HI)
     for sweep_index in range(ITERS):
@@ -108,8 +107,11 @@
         transform = spectral_table(partial_time.shape[-1] // 2)
         flags = brain_mask > 0
         pieces = coil_sum(partial_time, n_coil, n_slab)
-        patches = jnp.stack([(own + hop.astype(jnp.float32)).astype(jnp.bfloat16) for own, hop in pieces])
-        return denoise_batch(patches, flags, rank_limit, transform, start_basis)
+        owns = jnp.stack([own.astype(jnp.bfloat16) for own, hop in pieces])
+        hops = jnp.stack([hop for own, hop in pieces])
+        spectra = jnp.einsum("bvt,tf->bvf", owns, transform, preferred_element_type=jnp.float32)
+        spectra = spectra + jnp.einsum("bvt,tf->bvf", hops, transform, preferred_element_type=jnp.float32)
+        return denoise_batch(spectra, flags, rank_limit, start_basis)
 
     return body
 

time: 100 us -> 101 us (1.010)
  matrix products: 18.4 us -> 20.7 us
  other arithmetic: 18.9 us -> 16.7 us
    another operation x3 -> x2, other arithmetic: 12.5 us -> 8.56 us
    ppermute x2, waiting for transfers between devices: 0.01 us -> 3.34 us  [coil_sum(): got_own = lax.ppermute(pick(coil ^ 1), 'coil', chip_pair)]
    dot_general x1 -> x2, matrix products: 2.32 us -> 4.67 us  [the longest x1 2.34 us: body(): jnp.einsum('bvt,tf->bvf', hops, transform, preferred_element_type=jnp.flo...]
    ppermute x2, waiting for transfers between devices: 13.5 us -> 11.2 us  [coil_sum(): hop = lax.ppermute(hop, ('coil', 'slab'), pairs)]
    convert_element_type x1, other arithmetic: 3.13 us -> 4.91 us  [coil_sum(): (pick(coil ^ 2).astype(jnp.float32) + got_forward.astype(jnp.float32)).as...]
  transfers between devices with their start and end apart: 8 -> 8, of which waited for: 6 -> 7; matrix products, arithmetic and copies ran while one was open for 9% -> 11% of each run, Pallas kernels for 0% -> 0%
where the time goes in v10:
time: 101 us; the launch traced here: 100 us
  waiting for transfers between devices  41.6 us (41%)
  matrix products  20.7 us (20%)
  other arithmetic  16.7 us (17%)
  Pallas kernels  11.8 us (12%)
  starting transfers between devices  4.64 us (5%)
  local copies, waits for them, and re-layouts  4.29 us (4%)
    ppermute x2, waiting for transfers between devices, coil_sum(): hop = lax.ppermute(forward, ('coil', 'slab'), pairs)  24 us
    pallas_call x4, Pallas kernels, factor_solve(): pl.pallas_call(factor_solve_kernel, out_shape=jax.ShapeDtypeStruct(rhs.sh...  11.8 us
    ppermute x2, waiting for transfers between devices, coil_sum(): hop = lax.ppermute(hop, ('coil', 'slab'), pairs)  11.2 us
    another operation x2, other arithmetic  8.56 us
    convert_element_type x1, other arithmetic, coil_sum(): (pick(coil ^ 2).astype(jnp.float32) + got_forward.astype(jnp.float32)).as...  4.91 us
    dot_general x4, matrix products, denoise_batch(): pushed = jnp.einsum('bkv,bvw->bkw', coeff, kernel, precision=HI)  4.29 us
    reshape x1, local copies, waits for them, and re-layouts, pick(): return block.reshape(partial_time.shape[3:])  3.94 us
    dot_general x1, matrix products, denoise_batch(): kernel = jnp.einsum('bvf,bwf->bvw', spectra, spectra, precision=HI)  3.66 us
  transfers between devices with their start and end apart: 8, of which 7 were waited for; matrix products, arithmetic and copies ran while one was open for 11% of the time, Pallas kernels for 0%

profile of v10, /device:TPU:64, one launch (start us, length us, event | category | flops | bytes accessed | tf_op | source)
XLA Modules:
  0.0 100.0 jit_solution(3456599671656057041)
XLA Ops:
  0.0 3.9 %dynamic-slice_bitcast_fusion.1 = (bf16[512,1024]{1,0:T(8,128)(2,1)}, bf16[512,1024]{1,0:T(8,128)(2,1)}, bf16[512,1024]{1,0:T(8,128)(2,1)}, bf16[512,1024]{1,0:T(8,128)(2,1)S(1)}) fusion(bf16[1,4,2,512,1024]{4,3,2,1,0:T(8,128)(2,1)} %param.4, s32[]{:T(128)S(6)} %select_n.45, s32[]{:T(128)S(6)} %select_n.42), kind=kLoop, calls=%fused_computation.28 | loop fusion | bytes 8388616 | tf_op jit(solution)/shard_map/reshape | solution.py:93
  3.9 0.0 collective-permute-start
  3.9 0.5 collective-permute-start.1
  4.5 0.5 collective-permute-start.5
  5.0 1.8 %collective-permute-done = bf16[512,1024]{1,0:T(8,128)(2,1)S(1)} collective-permute-done((bf16[512,1024]{1,0:T(8,128)(2,1)}, bf16[512,1024]{1,0:T(8,128)(2,1)S(1)}, u32[]{:S(2)}, u32[]{:S(2)}) %collective-permute-start) | collective-permute-done | bytes 1048608 | tf_op jit(solution)/shard_map/ppermute | solution.py:97
  6.8 1.5 %collective-permute-done.1 = bf16[512,1024]{1,0:T(8,128)(2,1)S(1)} collective-permute-done((bf16[512,1024]{1,0:T(8,128)(2,1)}, bf16[512,1024]{1,0:T(8,128)(2,1)S(1)}, u32[]{:S(2)}, u32[]{:S(2)}) %collective-permute-start.1) | collective-permute-done | bytes 1048608 | tf_op jit(solution)/shard_map/ppermute | solution.py:97
  8.3 1.6 %collective-permute-done.2 = bf16[512,1024]{1,0:T(8,128)(2,1)} collective-permute-done((bf16[512,1024]{1,0:T(8,128)(2,1)}, bf16[512,1024]{1,0:T(8,128)(2,1)}, u32[]{:S(2)}, u32[]{:S(2)}) %collective-permute-start.2) | collective-permute-done | bytes 1048608 | tf_op jit(solution)/shard_map/ppermute | solution.py:95
  9.9 1.5 %collective-permute-done.5 = bf16[512,1024]{1,0:T(8,128)(2,1)} collective-permute-done((bf16[512,1024]{1,0:T(8,128)(2,1)S(1)}, bf16[512,1024]{1,0:T(8,128)(2,1)}, u32[]{:S(2)}, u32[]{:S(2)}) %collective-permute-start.5) | collective-permute-done | bytes 1048608 | tf_op jit(solution)/shard_map/ppermute | solution.py:95
  11.4 4.9 %fusion.9 = (bf16[512,1024]{1,0:T(8,128)(2,1)S(1)}, bf16[1,512,1024]{2,1,0:T(8,128)(2,1)S(1)}, bf16[1,512,1024]{2,1,0:T(8,128)(2,1)S(1)}, bf16[512,1024]{1,0:T(8,128)(2,1)S(1)}) fusion(bf16[512,1024]{1,0:T(8,128)(2,1)} %collective-permute-done.2, bf16[1,4,2,512,1024]{4,3,2,1,0:T(8,128)(2,1)} %param.4, s32[]{:T(128)S(6)} %select_n.44, ...), kind=kLoop, calls=%fused_computation.12 | loop fusion | flops 8388608 | bytes 12582920 | tf_op jit(solution)/shard_map/convert_element_type | solution.py:96
  16.4 1.6 %collective-permute-start.6 = (bf16[512,1024]{1,0:T(8,128)(2,1)S(1)}, bf16[512,1024]{1,0:T(8,128)(2,1)S(1)}, u32[]{:S(2)}, u32[]{:S(2)}) collective-permute-start(bf16[512,1024]{1,0:T(8,128)(2,1)S(1)} %get-tuple-element.8), channel_id=1, source_target_pairs={{0,1},{1,128},{2,3},{3,130},{4,5},{5,132},{6,7},{7,134},{8,9},{9,1... | collective-permute-start | bytes 3145736 | tf_op jit(solution)/shard_map/ppermute | solution.py:99
  17.9 1.5 %collective-permute-start.3 = (bf16[512,1024]{1,0:T(8,128)(2,1)S(1)}, bf16[512,1024]{1,0:T(8,128)(2,1)S(1)}, u32[]{:S(2)}, u32[]{:S(2)}) collective-permute-start(bf16[512,1024]{1,0:T(8,128)(2,1)S(1)} %get-tuple-element.5), channel_id=1, source_target_pairs={{0,1},{1,128},{2,3},{3,130},{4,5},{5,132},{6,7},{7,134},{8,9},{9,1... | collective-permute-start | bytes 3145736 | tf_op jit(solution)/shard_map/ppermute | solution.py:99
  19.4 13.0 %collective-permute-done.6 = bf16[512,1024]{1,0:T(8,128)(2,1)S(1)} collective-permute-done((bf16[512,1024]{1,0:T(8,128)(2,1)S(1)}, bf16[512,1024]{1,0:T(8,128)(2,1)S(1)}, u32[]{:S(2)}, u32[]{:S(2)}) %collective-permute-start.6) | collective-permute-done | bytes 1048608 | tf_op jit(solution)/shard_map/ppermute | solution.py:99
  32.4 0.3 collective-permute-start.7
  32.7 11.0 %collective-permute-done.3 = bf16[512,1024]{1,0:T(8,128)(2,1)S(1)} collective-permute-done((bf16[512,1024]{1,0:T(8,128)(2,1)S(1)}, bf16[512,1024]{1,0:T(8,128)(2,1)S(1)}, u32[]{:S(2)}, u32[]{:S(2)}) %collective-permute-start.3) | collective-permute-done | bytes 1048608 | tf_op jit(solution)/shard_map/ppermute | solution.py:99
  43.7 0.3 collective-permute-start.4
  44.0 4.0 %fusion.23 = bf16[512,512]{1,0:T(8,128)(2,1)S(1)} fusion(), kind=kLoop, calls=%fused_computation.37 | loop fusion | flops 4194304 | bytes 524288 | tf_op jit(solution)/shard_map/convert.6
  48.0 4.6 %negate_convert_fusion = (bf16[512,512]{1,0:T(8,128)(2,1)S(1)}, bf16[512,512]{1,0:T(8,128)(2,1)S(1)}) fusion(), kind=kLoop, calls=%fused_computation.29 | loop fusion | flops 4980736 | bytes 1048576 | tf_op jit(solution)/shard_map/convert.9
  52.6 0.1 iota_compare_fusion
  52.7 2.3 %fusion = f32[2,512,1024]{2,1,0:T(8,128)S(1)} fusion(bf16[1,512,1024]{2,1,0:T(8,128)(2,1)S(1)} %get-tuple-element.6, bf16[1,512,1024]{2,1,0:T(8,128)(2,1)S(1)} %get-tuple-element.7, bf16[512,512]{1,0:T(8,128)(2,1)S(1)} %get-tuple-element.14, bf16[512,512]{1,0:T(8,128)(2,1)S(1)} %fusion.23, bf16[512,512]{1,0:T(8,128)(2,1)S(1)} %get-tuple-element.13), kind=kOutput, calls=%fused_computation | convolution fusion | flops 2156920832 | bytes 7864320 | tf_op jit(solution)/shard_map/bvt,tf->bvf/dot_general | solution.py:112
  55.0 11.2 %collective-permute-done.4 = bf16[512,1024]{1,0:T(8,128)(2,1)S(1)} collective-permute-done((bf16[512,1024]{1,0:T(8,128)(2,1)S(1)}, bf16[512,1024]{1,0:T(8,128)(2,1)S(1)}, u32[]{:S(2)}, u32[]{:S(2)}) %collective-permute-start.4) | collective-permute-done | bytes 1048608 | tf_op jit(solution)/shard_map/ppermute | solution.py:100
  66.2 2.3 %fusion.12 = f32[2,512,1024]{2,1,0:T(8,128)S(1)} fusion(f32[2,512,1024]{2,1,0:T(8,128)S(1)} %fusion, bf16[1,512,1024]{2,1,0:T(8,128)(2,1)S(1)} %bitcast.70, bf16[1,512,1024]{2,1,0:T(8,128)(2,1)S(1)} %bitcast.71, bf16[512,512]{1,0:T(8,128)(2,1)S(1)} %get-tuple-element.14, bf16[512,512]{1,0:T(8,128)(2,1)S(1)} %fusion.23, ...), kind=kOutput, calls=%fused_computation.18 | convolution fusion | flops 2157969408 | bytes 12058624 | tf_op jit(solution)/shard_map/bvt,tf->bvf/dot_general | solution.py:113
  68.5 3.7 %fusion.37 = f32[2,512,512]{2,1,0:T(8,128)S(1)} fusion(f32[2,512,1024]{2,1,0:T(8,128)S(1)} %fusion.12), kind=kOutput, calls=%fused_computation.60 | convolution fusion | flops 3221225472 | bytes 6291456 | tf_op jit(solution)/shard_map/bvf,bwf->bvw/dot_general | solution.py:49
  72.2 1.7 %fusion.24 = f32[2,512,16]{1,2,0:T(8,128)S(1)} fusion(f32[2,512,1024]{2,1,0:T(8,128)S(1)} %fusion.12, f32[16,1024]{1,0:T(8,128)S(1)} %copy-done), kind=kOutput, calls=%fused_computation.41 | convolution fusion | flops 100663296 | bytes 4325376 | tf_op jit(solution)/shard_map/kf,bvf->bkv/dot_general | solution.py:50
  73.9 0.6 fusion.38.rhs_ref
  74.6 0.2 fusion.39
  74.7 0.1 copy.5
  74.8 0.6 fusion.33.gram_ref
  75.4 2.9 %shard_map.46 = f32[2,16,512]{2,1,0:T(8,128)} custom-call(f32[2,16,16]{2,1,0:T(8,128)} %fusion.33.gram_ref, f32[2,16,512]{2,1,0:T(8,128)} %copy-done.3), custom_call_target="tpu_custom_call" | custom-call | tf_op jit(solution)/shard_map/pallas_call | solution.py:42
  78.3 1.5 %fusion.40.rhs_ref = f32[2,16,512]{2,1,0:T(8,128)S(1)} fusion(f32[2,16,512]{2,1,0:T(8,128)} %shard_map.46, f32[2,512,512]{2,1,0:T(8,128)S(1)} %fusion.37), kind=kOutput, calls=%fused_computation.63 | convolution fusion | flops 50331648 | bytes 2228224 | tf_op jit(solution)/shard_map/bkv,bvw->bkw/dot_general | solution.py:52
  79.8 0.0 copy-start.4
  79.9 0.2 fusion.41
  80.0 0.1 copy.6
  80.1 0.6 fusion.32.gram_ref
  80.7 2.9 %shard_map.47 = f32[2,16,512]{2,1,0:T(8,128)} custom-call(f32[2,16,16]{2,1,0:T(8,128)} %fusion.32.gram_ref, f32[2,16,512]{2,1,0:T(8,128)} %copy-done.4), custom_call_target="tpu_custom_call" | custom-call | tf_op jit(solution)/shard_map/pallas_call | solution.py:42
  83.6 1.5 %fusion.42.rhs_ref = f32[2,16,512]{2,1,0:T(8,128)S(1)} fusion(f32[2,16,512]{2,1,0:T(8,128)} %shard_map.47, f32[2,512,512]{2,1,0:T(8,128)S(1)} %fusion.37), kind=kOutput, calls=%fused_computation.65 | convolution fusion | flops 50331648 | bytes 2228224 | tf_op jit(solution)/shard_map/bkv,bvw->bkw/dot_general | solution.py:52
  85.1 0.0 copy-start.5
  85.2 0.2 fusion.43
  85.3 0.1 copy.7
  85.4 0.6 fusion.31.gram_ref
  86.0 2.9 %shard_map.48 = f32[2,16,512]{2,1,0:T(8,128)} custom-call(f32[2,16,16]{2,1,0:T(8,128)} %fusion.31.gram_ref, f32[2,16,512]{2,1,0:T(8,128)} %copy-done.5), custom_call_target="tpu_custom_call" | custom-call | tf_op jit(solution)/shard_map/pallas_call | solution.py:42
  88.9 2.6 %fusion.46 = f32[2,16,1024]{2,1,0:T(8,128)S(1)} fusion(f32[2,16,512]{2,1,0:T(8,128)} %shard_map.48, f32[2,512,1024]{2,1,0:T(8,128)} %copy-done.1), kind=kOutput, calls=%fused_computation.69 | convolution fusion | flops 33554432 | bytes 4390912 | tf_op jit(solution)/shard_map/bkv,bvf->bkf/dot_general | solution.py:57
  91.5 0.6 fusion.44
  92.2 0.2 fusion.45
  92.3 0.7 pad_maximum_fusion.rhs_ref
  93.0 0.1 copy.8
  93.1 0.6 fusion.30.gram_ref
  93.7 3.1 %shard_map.49 = f32[2,16,1536]{2,1,0:T(8,128)} custom-call(f32[2,16,16]{2,1,0:T(8,128)} %fusion.30.gram_ref, f32[2,16,1536]{2,1,0:T(8,128)} %pad_maximum_fusion.rhs_ref), custom_call_target="tpu_custom_call" | custom-call | tf_op jit(solution)/shard_map/pallas_call | solution.py:42
  96.8 3.1 %convert_select_fusion = bf16[2,512,1024]{2,1,0:T(8,128)(2,1)} fusion(pred[2]{0:T(512)(128)(4,1)S(1)} %broadcast_compare_fusion, f32[2,16,1536]{2,1,0:T(8,128)} %shard_map.49, pred[2,16]{1,0:T(4,128)(4,1)S(1)} %iota_compare_fusion), kind=kOutput, calls=%fused_computation.17 | convolution fusion | flops 34652160 | bytes 2196992 | tf_op jit(solution)/shard_map/bkv,bkf->bvf/dot_general | solution.py:64
  (21 shorter events, 0.0 us)
Async XLA Ops:
  0.0 72.2 %copy-start = (f32[16,1024]{1,0:T(8,128)S(1)}, f32[16,1024]{1,0:T(8,128)}, u32[]{:S(2)}) copy-start(f32[16,1024]{1,0:T(8,128)} %param.7) | copy-start | bytes 196612
  3.9 2.9 %collective-permute-start = (bf16[512,1024]{1,0:T(8,128)(2,1)}, bf16[512,1024]{1,0:T(8,128)(2,1)S(1)}, u32[]{:S(2)}, u32[]{:S(2)}) collective-permute-start(bf16[512,1024]{1,0:T(8,128)(2,1)} %get-tuple-element.11), channel_id=1, source_target_pairs={{0,64},{64,0},{128,192},{192,128},{1,65},{65,1},{129,193},{193,129... | collective-permute-start | bytes 3145736 | tf_op jit(solution)/shard_map/ppermute | solution.py:97
  3.9 4.4 %collective-permute-start.1 = (bf16[512,1024]{1,0:T(8,128)(2,1)}, bf16[512,1024]{1,0:T(8,128)(2,1)S(1)}, u32[]{:S(2)}, u32[]{:S(2)}) collective-permute-start(bf16[512,1024]{1,0:T(8,128)(2,1)} %get-tuple-element.10), channel_id=1, source_target_pairs={{0,64},{64,0},{128,192},{192,128},{1,65},{65,1},{129,193},{193,129... | collective-permute-start | bytes 3145736 | tf_op jit(solution)/shard_map/ppermute | solution.py:97
  4.5 5.5 %collective-permute-start.2 = (bf16[512,1024]{1,0:T(8,128)(2,1)}, bf16[512,1024]{1,0:T(8,128)(2,1)}, u32[]{:S(2)}, u32[]{:S(2)}) collective-permute-start(bf16[512,1024]{1,0:T(8,128)(2,1)} %get-tuple-element.9), channel_id=1, source_target_pairs={{0,64},{64,0},{128,192},{192,128},{1,65},{65,1},{129,193},{193,129... | collective-permute-start | bytes 3145736 | tf_op jit(solution)/shard_map/ppermute | solution.py:95
  4.5 7.0 %collective-permute-start.5 = (bf16[512,1024]{1,0:T(8,128)(2,1)S(1)}, bf16[512,1024]{1,0:T(8,128)(2,1)}, u32[]{:S(2)}, u32[]{:S(2)}) collective-permute-start(bf16[512,1024]{1,0:T(8,128)(2,1)S(1)} %get-tuple-element.12), channel_id=1, source_target_pairs={{0,64},{64,0},{128,192},{192,128},{1,65},{65,1},{129,193},{193,129... | collective-permute-start | bytes 3145736 | tf_op jit(solution)/shard_map/ppermute | solution.py:95
  5.0 47.6 %copy-start.8 = (s32[2]{0:T(128)S(1)}, s32[2]{0:T(128)}, u32[]{:S(2)}) copy-start(s32[2]{0:T(128)} %param.5) | copy-start | bytes 28
  5.0 47.6 %copy-start.9 = (s32[2]{0:T(128)S(1)}, s32[2]{0:T(128)}, u32[]{:S(2)}) copy-start(s32[2]{0:T(128)} %param.6) | copy-start | bytes 28
  16.4 16.1 %collective-permute-start.6 = (bf16[512,1024]{1,0:T(8,128)(2,1)S(1)}, bf16[512,1024]{1,0:T(8,128)(2,1)S(1)}, u32[]{:S(2)}, u32[]{:S(2)}) collective-permute-start(bf16[512,1024]{1,0:T(8,128)(2,1)S(1)} %get-tuple-element.8), channel_id=1, source_target_pairs={{0,1},{1,128},{2,3},{3,130},{4,5},{5,132},{6,7},{7,134},{8,9},{9,1... | collective-permute-start | bytes 3145736 | tf_op jit(solution)/shard_map/ppermute | solution.py:99
  17.9 25.8 %collective-permute-start.3 = (bf16[512,1024]{1,0:T(8,128)(2,1)S(1)}, bf16[512,1024]{1,0:T(8,128)(2,1)S(1)}, u32[]{:S(2)}, u32[]{:S(2)}) collective-permute-start(bf16[512,1024]{1,0:T(8,128)(2,1)S(1)} %get-tuple-element.5), channel_id=1, source_target_pairs={{0,1},{1,128},{2,3},{3,130},{4,5},{5,132},{6,7},{7,134},{8,9},{9,1... | collective-permute-start | bytes 3145736 | tf_op jit(solution)/shard_map/ppermute | solution.py:99
  32.4 22.5 %collective-permute-start.7 = (bf16[512,1024]{1,0:T(8,128)(2,1)S(1)}, bf16[512,1024]{1,0:T(8,128)(2,1)S(1)}, u32[]{:S(2)}, u32[]{:S(2)}) collective-permute-start(bf16[512,1024]{1,0:T(8,128)(2,1)S(1)} %collective-permute-done.6), channel_id=1, source_target_pairs={{0,1},{1,128},{2,3},{3,130},{4,5},{5,132},{6,7},{7,134},{8,9},{9,1... | collective-permute-start | bytes 3145736 | tf_op jit(solution)/shard_map/ppermute | solution.py:100
  43.7 22.5 %collective-permute-start.4 = (bf16[512,1024]{1,0:T(8,128)(2,1)S(1)}, bf16[512,1024]{1,0:T(8,128)(2,1)S(1)}, u32[]{:S(2)}, u32[]{:S(2)}) collective-permute-start(bf16[512,1024]{1,0:T(8,128)(2,1)S(1)} %collective-permute-done.3), channel_id=1, source_target_pairs={{0,1},{1,128},{2,3},{3,130},{4,5},{5,132},{6,7},{7,134},{8,9},{9,1... | collective-permute-start | bytes 3145736 | tf_op jit(solution)/shard_map/ppermute | solution.py:100
  68.5 3.7 %copy-start.1 = (f32[2,512,1024]{2,1,0:T(8,128)}, f32[2,512,1024]{2,1,0:T(8,128)S(1)}, u32[]{:S(2)}) copy-start(f32[2,512,1024]{2,1,0:T(8,128)S(1)} %fusion.12) | copy-start | bytes 12582916
  74.6 0.9 copy-start.3
  78.3 1.5 %copy-start.6 = (f32[2,16,512]{2,1,0:T(8,128)S(1)}, f32[2,16,512]{2,1,0:T(8,128)}, u32[]{:S(2)}) copy-start(f32[2,16,512]{2,1,0:T(8,128)} %shard_map.46) | copy-start | bytes 196612
  79.8 0.9 copy-start.4
  83.6 1.5 %copy-start.7 = (f32[2,16,512]{2,1,0:T(8,128)S(1)}, f32[2,16,512]{2,1,0:T(8,128)}, u32[]{:S(2)}) copy-start(f32[2,16,512]{2,1,0:T(8,128)} %shard_map.47) | copy-start | bytes 196612
  85.1 0.9 copy-start.5
  88.9 2.6 %copy-start.2 = (f32[2,16,512]{2,1,0:T(8,128)S(1)}, f32[2,16,512]{2,1,0:T(8,128)}, u32[]{:S(2)}) copy-start(f32[2,16,512]{2,1,0:T(8,128)} %shard_map.48) | copy-start | bytes 196612

commit v11 on v10

--- a/solution.py
+++ b/solution.py
@@ -85,19 +85,24 @@
     coil = lax.axis_index("coil")
     chip_pair = [(i, i ^ 1) for i in range(n_coil)]
     pairs = ring_pairs(n_coil, n_slab)
+    patch_count = partial_time.shape[2]
+
+    def pick(source, o, q):
+        block = lax.dynamic_slice(source, (0, o, q, 0, 0), (1, 1, 1) + source.shape[3:])
+        return block.reshape(source.shape[3:])
+
+    forwards = []
+    for q in range(patch_count):
+        got_forward = lax.ppermute(pick(partial_time, coil ^ 3, q), "coil", chip_pair)
+        forward = pick(partial_time, coil ^ 2, q).astype(jnp.float32) + got_forward.astype(jnp.float32)
+        forwards.append(forward.astype(jnp.bfloat16))
+    source, forwards = lax.optimization_barrier((partial_time, forwards))
     sums = []
-    for q in range(partial_time.shape[2]):
-
-        def pick(o, q=q):
-            block = lax.dynamic_slice(partial_time, (0, o, q, 0, 0), (1, 1, 1) + partial_time.shape[3:])
-            return block.reshape(partial_time.shape[3:])
-
-        got_forward = lax.ppermute(pick(coil ^ 3), "coil", chip_pair)
-        forward = (pick(coil ^ 2).astype(jnp.float32) + got_forward.astype(jnp.float32)).astype(jnp.bfloat16)
-        got_own = lax.ppermute(pick(coil ^ 1), "coil", chip_pair)
-        own = pick(coil).astype(jnp.float32) + got_own.astype(jnp.float32)
-        hop = lax.ppermute(forward, ("coil", "slab"), pairs)
+    for q in range(patch_count):
+        hop = lax.ppermute(forwards[q], ("coil", "slab"), pairs)
         hop = lax.ppermute(hop, ("coil", "slab"), pairs)
+        got_own = lax.ppermute(pick(source, coil ^ 1, q), "coil", chip_pair)
+        own = pick(source, coil, q).astype(jnp.float32) + got_own.astype(jnp.float32)
         sums.append((own, hop))
     return sums
 

time: 101 us -> 97.2 us (0.962)
  waiting for transfers between devices: 41.6 us -> 32.2 us
  other arithmetic: 16.7 us -> 19.2 us
  matrix products: 20.7 us -> 22.3 us
  local copies, waits for them, and re-layouts: 4.29 us -> 5.77 us
    ppermute x6, waiting for transfers between devices: 30.5 us -> 19.5 us  [the longest x2 15.6 us: coil_sum(): hop = lax.ppermute(forwards[q], ('coil', 'slab'), pairs)]
    another operation x2 -> x3, other arithmetic: 8.56 us -> 12.5 us
    dot_general x1, matrix products: 2.34 us -> 3.9 us  [body(): jnp.einsum('bvt,tf->bvf', hops, transform, preferred_element_type=jnp.flo...]
    ppermute x2, waiting for transfers between devices: 11.2 us -> 12.6 us  [coil_sum(): hop = lax.ppermute(hop, ('coil', 'slab'), pairs)]
    reshape x1 -> x2, local copies, waits for them, and re-layouts: 3.94 us -> 5.42 us  [pick(): return block.reshape(source.shape[3:])]
    convert_element_type x1, other arithmetic: 4.91 us -> 3.5 us  [coil_sum(): forwards.append(forward.astype(jnp.bfloat16))]
  transfers between devices with their start and end apart: 8 -> 8, of which waited for: 7 -> 6; matrix products, arithmetic and copies ran while one was open for 11% -> 18% of each run, Pallas kernels for 0% -> 0%
where the time goes in v11:
time: 97.2 us; the launch traced here: 96 us
  waiting for transfers between devices  32.2 us (33%)
  matrix products  22.3 us (23%)
  other arithmetic  19.2 us (20%)
  Pallas kernels  11.8 us (12%)
  local copies, waits for them, and re-layouts  5.77 us (6%)
  starting transfers between devices  4.56 us (5%)
    ppermute x2, waiting for transfers between devices, coil_sum(): hop = lax.ppermute(forwards[q], ('coil', 'slab'), pairs)  15.6 us
    ppermute x2, waiting for transfers between devices, coil_sum(): hop = lax.ppermute(hop, ('coil', 'slab'), pairs)  12.6 us
    pallas_call x4, Pallas kernels, factor_solve(): pl.pallas_call(factor_solve_kernel, out_shape=jax.ShapeDtypeStruct(rhs.sh...  11.8 us
    another operation x2, other arithmetic  9.59 us
    reshape x2, local copies, waits for them, and re-layouts, pick(): return block.reshape(source.shape[3:])  5.42 us
    dot_general x4, matrix products, denoise_batch(): pushed = jnp.einsum('bkv,bvw->bkw', coeff, kernel, precision=HI)  4.29 us
    dot_general x1, matrix products, body(): jnp.einsum('bvt,tf->bvf', hops, transform, preferred_element_type=jnp.flo...  3.9 us
    ppermute x2, waiting for transfers between devices, coil_sum(): lax.ppermute(pick(partial_time, coil ^ 3, q), 'coil', chip_pair)  3.86 us
  transfers between devices with their start and end apart: 8, of which 6 were waited for; matrix products, arithmetic and copies ran while one was open for 18% of the time, Pallas kernels for 0%

profile of v11, /device:TPU:64, one launch (start us, length us, event | category | flops | bytes accessed | tf_op | source)
XLA Modules:
  0.0 96.0 jit_solution(224589855623645912)
XLA Ops:
  0.0 2.7 %dynamic-slice_bitcast_fusion.2 = (bf16[512,1024]{1,0:T(8,128)(2,1)S(1)}, bf16[512,1024]{1,0:T(8,128)(2,1)}) fusion(bf16[1,4,2,512,1024]{4,3,2,1,0:T(8,128)(2,1)} %param.4, s32[]{:T(128)S(6)} %select_n.42), kind=kLoop, calls=%fused_computation.34 | loop fusion | bytes 4194308 | tf_op jit(solution)/shard_map/reshape | solution.py:92
  2.7 0.5 collective-permute-start.1
  3.2 2.4 %collective-permute-done = bf16[512,1024]{1,0:T(8,128)(2,1)S(1)} collective-permute-done((bf16[512,1024]{1,0:T(8,128)(2,1)}, bf16[512,1024]{1,0:T(8,128)(2,1)S(1)}, u32[]{:S(2)}, u32[]{:S(2)}) %collective-permute-start) | collective-permute-done | bytes 1048608 | tf_op jit(solution)/shard_map/ppermute | solution.py:96
  5.6 1.5 %collective-permute-done.1 = bf16[512,1024]{1,0:T(8,128)(2,1)S(1)} collective-permute-done((bf16[512,1024]{1,0:T(8,128)(2,1)S(1)}, bf16[512,1024]{1,0:T(8,128)(2,1)S(1)}, u32[]{:S(2)}, u32[]{:S(2)}) %collective-permute-start.1) | collective-permute-done | bytes 1048608 | tf_op jit(solution)/shard_map/ppermute | solution.py:96
  7.1 3.5 %fusion.10 = (bf16[512,1024]{1,0:T(8,128)(2,1)S(1)}, bf16[512,1024]{1,0:T(8,128)(2,1)}) fusion(bf16[512,1024]{1,0:T(8,128)(2,1)S(1)} %collective-permute-done.1, bf16[1,4,2,512,1024]{4,3,2,1,0:T(8,128)(2,1)} %param.4, s32[]{:T(128)S(6)} %select_n.41, bf16[512,1024]{1,0:T(8,128)(2,1)S(1)} %collective-permute-done), kind=kLoop, calls=%fused_computation.14 | loop fusion | flops 4194304 | bytes 6291460 | tf_op jit(solution)/shard_map/convert_element_type | solution.py:98
  10.6 1.5 %collective-permute-start.4 = (bf16[512,1024]{1,0:T(8,128)(2,1)}, bf16[512,1024]{1,0:T(8,128)(2,1)}, u32[]{:S(2)}, u32[]{:S(2)}) collective-permute-start(bf16[512,1024]{1,0:T(8,128)(2,1)} %get-tuple-element.9), channel_id=1, source_target_pairs={{0,1},{1,128},{2,3},{3,130},{4,5},{5,132},{6,7},{7,134},{8,9},{9,1... | collective-permute-start | bytes 3145736 | tf_op jit(solution)/shard_map/ppermute | solution.py:102
  12.1 1.5 %collective-permute-start.6 = (bf16[512,1024]{1,0:T(8,128)(2,1)S(1)}, bf16[512,1024]{1,0:T(8,128)(2,1)}, u32[]{:S(2)}, u32[]{:S(2)}) collective-permute-start(bf16[512,1024]{1,0:T(8,128)(2,1)S(1)} %get-tuple-element.10), channel_id=1, source_target_pairs={{0,1},{1,128},{2,3},{3,130},{4,5},{5,132},{6,7},{7,134},{8,9},{9,1... | collective-permute-start | bytes 3145736 | tf_op jit(solution)/shard_map/ppermute | solution.py:102
  13.6 2.7 %dynamic-slice_bitcast_fusion.1 = (bf16[512,1024]{1,0:T(8,128)(2,1)}, bf16[512,1024]{1,0:T(8,128)(2,1)S(1)}) fusion(bf16[1,4,2,512,1024]{4,3,2,1,0:T(8,128)(2,1)} %param.4, s32[]{:T(128)S(6)} %select_n.44), kind=kLoop, calls=%fused_computation.33 | loop fusion | bytes 4194308 | tf_op jit(solution)/shard_map/reshape | solution.py:92
  16.3 0.2 collective-permute-start.2
  16.5 0.3 collective-permute-start.3
  16.8 5.4 %negate_convert_fusion = (bf16[512,512]{1,0:T(8,128)(2,1)}, bf16[512,512]{1,0:T(8,128)(2,1)}) fusion(), kind=kLoop, calls=%fused_computation.27 | loop fusion | flops 4980736 | bytes 1048576 | tf_op jit(solution)/shard_map/convert.9
  22.2 4.7 %collective-permute-done.4 = bf16[512,1024]{1,0:T(8,128)(2,1)} collective-permute-done((bf16[512,1024]{1,0:T(8,128)(2,1)}, bf16[512,1024]{1,0:T(8,128)(2,1)}, u32[]{:S(2)}, u32[]{:S(2)}) %collective-permute-start.4) | collective-permute-done | bytes 1048608 | tf_op jit(solution)/shard_map/ppermute | solution.py:102
  26.9 0.3 collective-permute-start.5
  27.2 11.0 %collective-permute-done.6 = bf16[512,1024]{1,0:T(8,128)(2,1)} collective-permute-done((bf16[512,1024]{1,0:T(8,128)(2,1)S(1)}, bf16[512,1024]{1,0:T(8,128)(2,1)}, u32[]{:S(2)}, u32[]{:S(2)}) %collective-permute-start.6) | collective-permute-done | bytes 1048608 | tf_op jit(solution)/shard_map/ppermute | solution.py:102
  38.1 0.3 collective-permute-start.7
  38.4 4.2 %fusion.23 = bf16[512,512]{1,0:T(8,128)(2,1)S(1)} fusion(), kind=kLoop, calls=%fused_computation.37 | loop fusion | flops 4194304 | bytes 524288 | tf_op jit(solution)/shard_map/convert.6
  42.6 0.1 iota_compare_fusion
  42.7 2.9 %fusion.18 = (bf16[1,512,1024]{2,1,0:T(8,128)(2,1)S(1)}, bf16[1,512,1024]{2,1,0:T(8,128)(2,1)S(1)}) fusion(bf16[512,1024]{1,0:T(8,128)(2,1)S(1)} %collective-permute-done.2, bf16[1,4,2,512,1024]{4,3,2,1,0:T(8,128)(2,1)} %param.4, s32[]{:T(128)S(6)} %select_n.43, bf16[512,1024]{1,0:T(8,128)(2,1)} %collective-permute-done.3), kind=kLoop, calls=%fused_computation.25 | loop fusion | flops 4194304 | bytes 6291460 | tf_op jit(solution)/shard_map/stack | solution.py:115
  45.6 2.3 %fusion = f32[2,512,1024]{2,1,0:T(8,128)S(1)} fusion(bf16[1,512,1024]{2,1,0:T(8,128)(2,1)S(1)} %get-tuple-element.12, bf16[1,512,1024]{2,1,0:T(8,128)(2,1)S(1)} %get-tuple-element.11, bf16[512,512]{1,0:T(8,128)(2,1)S(1)} %copy-done.9, bf16[512,512]{1,0:T(8,128)(2,1)S(1)} %fusion.23, bf16[512,512]{1,0:T(8,128)(2,1)S(1)} %copy-done.8), kind=kOutput, calls=%fused_computation | convolution fusion | flops 2156920832 | bytes 7864320 | tf_op jit(solution)/shard_map/bvt,tf->bvf/dot_general | solution.py:117
  48.0 1.4 %collective-permute-done.5 = bf16[512,1024]{1,0:T(8,128)(2,1)} collective-permute-done((bf16[512,1024]{1,0:T(8,128)(2,1)}, bf16[512,1024]{1,0:T(8,128)(2,1)}, u32[]{:S(2)}, u32[]{:S(2)}) %collective-permute-start.5) | collective-permute-done | bytes 1048608 | tf_op jit(solution)/shard_map/ppermute | solution.py:103
  49.4 11.2 %collective-permute-done.7 = bf16[512,1024]{1,0:T(8,128)(2,1)} collective-permute-done((bf16[512,1024]{1,0:T(8,128)(2,1)}, bf16[512,1024]{1,0:T(8,128)(2,1)}, u32[]{:S(2)}, u32[]{:S(2)}) %collective-permute-start.7) | collective-permute-done | bytes 1048608 | tf_op jit(solution)/shard_map/ppermute | solution.py:103
  60.6 3.9 %fusion.12 = f32[2,512,1024]{2,1,0:T(8,128)S(1)} fusion(f32[2,512,1024]{2,1,0:T(8,128)S(1)} %fusion, bf16[1,512,1024]{2,1,0:T(8,128)(2,1)} %bitcast.12, bf16[1,512,1024]{2,1,0:T(8,128)(2,1)} %bitcast.11, bf16[512,512]{1,0:T(8,128)(2,1)S(1)} %copy-done.9, bf16[512,512]{1,0:T(8,128)(2,1)S(1)} %fusion.23, bf16[512,512]{1,0:T(8,128)(2,1)S(1)} %copy-done.8), kind=kOutput, calls=%fused_computation.18 | convolution fusion | flops 2157969408 | bytes 12058624 | tf_op jit(solution)/shard_map/bvt,tf->bvf/dot_general | solution.py:118
  64.5 3.7 %fusion.37 = f32[2,512,512]{2,1,0:T(8,128)S(1)} fusion(f32[2,512,1024]{2,1,0:T(8,128)S(1)} %fusion.12), kind=kOutput, calls=%fused_computation.60 | convolution fusion | flops 3221225472 | bytes 6291456 | tf_op jit(solution)/shard_map/bvf,bwf->bvw/dot_general | solution.py:49
  68.2 1.7 %fusion.24 = f32[2,512,16]{1,2,0:T(8,128)S(1)} fusion(f32[2,512,1024]{2,1,0:T(8,128)S(1)} %fusion.12, f32[16,1024]{1,0:T(8,128)S(1)} %copy-done), kind=kOutput, calls=%fused_computation.41 | convolution fusion | flops 100663296 | bytes 4325376 | tf_op jit(solution)/shard_map/kf,bvf->bkv/dot_general | solution.py:50
  69.9 0.6 fusion.38.rhs_ref
  70.6 0.2 fusion.39
  70.7 0.1 copy.5
  70.8 0.6 fusion.33.gram_ref
  71.4 2.9 %shard_map.46 = f32[2,16,512]{2,1,0:T(8,128)} custom-call(f32[2,16,16]{2,1,0:T(8,128)} %fusion.33.gram_ref, f32[2,16,512]{2,1,0:T(8,128)} %copy-done.3), custom_call_target="tpu_custom_call" | custom-call | tf_op jit(solution)/shard_map/pallas_call | solution.py:42
  74.3 1.5 %fusion.40.rhs_ref = f32[2,16,512]{2,1,0:T(8,128)S(1)} fusion(f32[2,16,512]{2,1,0:T(8,128)} %shard_map.46, f32[2,512,512]{2,1,0:T(8,128)S(1)} %fusion.37), kind=kOutput, calls=%fused_computation.63 | convolution fusion | flops 50331648 | bytes 2228224 | tf_op jit(solution)/shard_map/bkv,bvw->bkw/dot_general | solution.py:52
  75.8 0.0 copy-start.4
  75.9 0.2 fusion.41
  76.0 0.1 copy.6
  76.1 0.6 fusion.32.gram_ref
  76.7 2.9 %shard_map.47 = f32[2,16,512]{2,1,0:T(8,128)} custom-call(f32[2,16,16]{2,1,0:T(8,128)} %fusion.32.gram_ref, f32[2,16,512]{2,1,0:T(8,128)} %copy-done.4), custom_call_target="tpu_custom_call" | custom-call | tf_op jit(solution)/shard_map/pallas_call | solution.py:42
  79.6 1.5 %fusion.42.rhs_ref = f32[2,16,512]{2,1,0:T(8,128)S(1)} fusion(f32[2,16,512]{2,1,0:T(8,128)} %shard_map.47, f32[2,512,512]{2,1,0:T(8,128)S(1)} %fusion.37), kind=kOutput, calls=%fused_computation.65 | convolution fusion | flops 50331648 | bytes 2228224 | tf_op jit(solution)/shard_map/bkv,bvw->bkw/dot_general | solution.py:52
  81.2 0.2 fusion.43
  81.3 0.1 copy.7
  81.4 0.6 fusion.31.gram_ref
  82.0 2.9 %shard_map.48 = f32[2,16,512]{2,1,0:T(8,128)} custom-call(f32[2,16,16]{2,1,0:T(8,128)} %fusion.31.gram_ref, f32[2,16,512]{2,1,0:T(8,128)} %copy-done.5), custom_call_target="tpu_custom_call" | custom-call | tf_op jit(solution)/shard_map/pallas_call | solution.py:42
  84.9 2.6 %fusion.46 = f32[2,16,1024]{2,1,0:T(8,128)S(1)} fusion(f32[2,16,512]{2,1,0:T(8,128)} %shard_map.48, f32[2,512,1024]{2,1,0:T(8,128)} %copy-done.1), kind=kOutput, calls=%fused_computation.69 | convolution fusion | flops 33554432 | bytes 4390912 | tf_op jit(solution)/shard_map/bkv,bvf->bkf/dot_general | solution.py:57
  87.5 0.6 fusion.44
  88.2 0.2 fusion.45
  88.3 0.7 pad_maximum_fusion.rhs_ref
  89.0 0.1 copy.8
  89.1 0.6 fusion.30.gram_ref
  89.7 3.1 %shard_map.49 = f32[2,16,1536]{2,1,0:T(8,128)} custom-call(f32[2,16,16]{2,1,0:T(8,128)} %fusion.30.gram_ref, f32[2,16,1536]{2,1,0:T(8,128)} %pad_maximum_fusion.rhs_ref), custom_call_target="tpu_custom_call" | custom-call | tf_op jit(solution)/shard_map/pallas_call | solution.py:42
  92.8 3.1 %convert_select_fusion = bf16[2,512,1024]{2,1,0:T(8,128)(2,1)} fusion(pred[2]{0:T(512)(128)(4,1)S(1)} %broadcast_compare_fusion, f32[2,16,1536]{2,1,0:T(8,128)} %shard_map.49, pred[2,16]{1,0:T(4,128)(4,1)S(1)} %iota_compare_fusion), kind=kOutput, calls=%fused_computation.17 | convolution fusion | flops 34652160 | bytes 2196992 | tf_op jit(solution)/shard_map/bkv,bkf->bvf/dot_general | solution.py:64
  (27 shorter events, 0.1 us)
Async XLA Ops:
  0.0 68.2 %copy-start = (f32[16,1024]{1,0:T(8,128)S(1)}, f32[16,1024]{1,0:T(8,128)}, u32[]{:S(2)}) copy-start(f32[16,1024]{1,0:T(8,128)} %param.7) | copy-start | bytes 196612
  2.7 2.9 %collective-permute-start = (bf16[512,1024]{1,0:T(8,128)(2,1)}, bf16[512,1024]{1,0:T(8,128)(2,1)S(1)}, u32[]{:S(2)}, u32[]{:S(2)}) collective-permute-start(bf16[512,1024]{1,0:T(8,128)(2,1)} %get-tuple-element.18), channel_id=1, source_target_pairs={{0,64},{64,0},{128,192},{192,128},{1,65},{65,1},{129,193},{193,129... | collective-permute-start | bytes 3145736 | tf_op jit(solution)/shard_map/ppermute | solution.py:96
  2.7 4.4 %collective-permute-start.1 = (bf16[512,1024]{1,0:T(8,128)(2,1)S(1)}, bf16[512,1024]{1,0:T(8,128)(2,1)S(1)}, u32[]{:S(2)}, u32[]{:S(2)}) collective-permute-start(bf16[512,1024]{1,0:T(8,128)(2,1)S(1)} %get-tuple-element.17), channel_id=1, source_target_pairs={{0,64},{64,0},{128,192},{192,128},{1,65},{65,1},{129,193},{193,129... | collective-permute-start | bytes 3145736 | tf_op jit(solution)/shard_map/ppermute | solution.py:96
  10.6 16.3 %collective-permute-start.4 = (bf16[512,1024]{1,0:T(8,128)(2,1)}, bf16[512,1024]{1,0:T(8,128)(2,1)}, u32[]{:S(2)}, u32[]{:S(2)}) collective-permute-start(bf16[512,1024]{1,0:T(8,128)(2,1)} %get-tuple-element.9), channel_id=1, source_target_pairs={{0,1},{1,128},{2,3},{3,130},{4,5},{5,132},{6,7},{7,134},{8,9},{9,1... | collective-permute-start | bytes 3145736 | tf_op jit(solution)/shard_map/ppermute | solution.py:102
  12.1 26.1 %collective-permute-start.6 = (bf16[512,1024]{1,0:T(8,128)(2,1)S(1)}, bf16[512,1024]{1,0:T(8,128)(2,1)}, u32[]{:S(2)}, u32[]{:S(2)}) collective-permute-start(bf16[512,1024]{1,0:T(8,128)(2,1)S(1)} %get-tuple-element.10), channel_id=1, source_target_pairs={{0,1},{1,128},{2,3},{3,130},{4,5},{5,132},{6,7},{7,134},{8,9},{9,1... | collective-permute-start | bytes 3145736 | tf_op jit(solution)/shard_map/ppermute | solution.py:102
  13.6 8.6 %copy-start.10 = (s32[2]{0:T(128)S(1)}, s32[2]{0:T(128)}, u32[]{:S(2)}) copy-start(s32[2]{0:T(128)} %param.5) | copy-start | bytes 28
  13.6 29.0 %copy-start.11 = (s32[2]{0:T(128)S(1)}, s32[2]{0:T(128)}, u32[]{:S(2)}) copy-start(s32[2]{0:T(128)} %param.6) | copy-start | bytes 28
  16.3 26.4 %collective-permute-start.2 = (bf16[512,1024]{1,0:T(8,128)(2,1)}, bf16[512,1024]{1,0:T(8,128)(2,1)S(1)}, u32[]{:S(2)}, u32[]{:S(2)}) collective-permute-start(bf16[512,1024]{1,0:T(8,128)(2,1)} %get-tuple-element.13), channel_id=1, source_target_pairs={{0,64},{64,0},{128,192},{192,128},{1,65},{65,1},{129,193},{193,129... | collective-permute-start | bytes 3145736 | tf_op jit(solution)/shard_map/ppermute | solution.py:104
  16.5 26.2 %collective-permute-start.3 = (bf16[512,1024]{1,0:T(8,128)(2,1)S(1)}, bf16[512,1024]{1,0:T(8,128)(2,1)}, u32[]{:S(2)}, u32[]{:S(2)}) collective-permute-start(bf16[512,1024]{1,0:T(8,128)(2,1)S(1)} %get-tuple-element.14), channel_id=1, source_target_pairs={{0,64},{64,0},{128,192},{192,128},{1,65},{65,1},{129,193},{193,129... | collective-permute-start | bytes 3145736 | tf_op jit(solution)/shard_map/ppermute | solution.py:104
  26.9 22.5 %collective-permute-start.5 = (bf16[512,1024]{1,0:T(8,128)(2,1)}, bf16[512,1024]{1,0:T(8,128)(2,1)}, u32[]{:S(2)}, u32[]{:S(2)}) collective-permute-start(bf16[512,1024]{1,0:T(8,128)(2,1)} %collective-permute-done.4), channel_id=1, source_target_pairs={{0,1},{1,128},{2,3},{3,130},{4,5},{5,132},{6,7},{7,134},{8,9},{9,1... | collective-permute-start | bytes 3145736 | tf_op jit(solution)/shard_map/ppermute | solution.py:103
  38.1 22.5 %collective-permute-start.7 = (bf16[512,1024]{1,0:T(8,128)(2,1)}, bf16[512,1024]{1,0:T(8,128)(2,1)}, u32[]{:S(2)}, u32[]{:S(2)}) collective-permute-start(bf16[512,1024]{1,0:T(8,128)(2,1)} %collective-permute-done.6), channel_id=1, source_target_pairs={{0,1},{1,128},{2,3},{3,130},{4,5},{5,132},{6,7},{7,134},{8,9},{9,1... | collective-permute-start | bytes 3145736 | tf_op jit(solution)/shard_map/ppermute | solution.py:103
  42.7 2.9 %copy-start.8 = (bf16[512,512]{1,0:T(8,128)(2,1)S(1)}, bf16[512,512]{1,0:T(8,128)(2,1)}, u32[]{:S(2)}) copy-start(bf16[512,512]{1,0:T(8,128)(2,1)} %get-tuple-element.19) | copy-start | bytes 1572868
  42.7 2.9 %copy-start.9 = (bf16[512,512]{1,0:T(8,128)(2,1)S(1)}, bf16[512,512]{1,0:T(8,128)(2,1)}, u32[]{:S(2)}) copy-start(bf16[512,512]{1,0:T(8,128)(2,1)} %get-tuple-element.20) | copy-start | bytes 1572868
  64.5 3.7 %copy-start.1 = (f32[2,512,1024]{2,1,0:T(8,128)}, f32[2,512,1024]{2,1,0:T(8,128)S(1)}, u32[]{:S(2)}) copy-start(f32[2,512,1024]{2,1,0:T(8,128)S(1)} %fusion.12) | copy-start | bytes 12582916
  70.6 0.9 copy-start.3
  74.3 1.5 %copy-start.6 = (f32[2,16,512]{2,1,0:T(8,128)S(1)}, f32[2,16,512]{2,1,0:T(8,128)}, u32[]{:S(2)}) copy-start(f32[2,16,512]{2,1,0:T(8,128)} %shard_map.46) | copy-start | bytes 196612
  75.8 0.9 copy-start.4
  79.6 1.5 %copy-start.7 = (f32[2,16,512]{2,1,0:T(8,128)S(1)}, f32[2,16,512]{2,1,0:T(8,128)}, u32[]{:S(2)}) copy-start(f32[2,16,512]{2,1,0:T(8,128)} %shard_map.47) | copy-start | bytes 196612
  81.1 0.9 copy-start.5
  84.9 2.6 %copy-start.2 = (f32[2,16,512]{2,1,0:T(8,128)S(1)}, f32[2,16,512]{2,1,0:T(8,128)}, u32[]{:S(2)}) copy-start(f32[2,16,512]{2,1,0:T(8,128)} %shard_map.48) | copy-start | bytes 196612

commit v12 on v11

--- a/solution.py
+++ b/solution.py
@@ -113,9 +113,11 @@
         flags = brain_mask > 0
         pieces = coil_sum(partial_time, n_coil, n_slab)
         owns = jnp.stack([own.astype(jnp.bfloat16) for own, hop in pieces])
-        hops = jnp.stack([hop for own, hop in pieces])
         spectra = jnp.einsum("bvt,tf->bvf", owns, transform, preferred_element_type=jnp.float32)
-        spectra = spectra + jnp.einsum("bvt,tf->bvf", hops, transform, preferred_element_type=jnp.float32)
+        spectra = jnp.stack([
+            spectra[q] + jnp.dot(hop, transform, preferred_element_type=jnp.float32)
+            for q, (own, hop) in enumerate(pieces)
+        ])
         return denoise_batch(spectra, flags, rank_limit, start_basis)
 
     return body

time: 97.2 us -> 94.5 us (0.972)
  waiting for transfers between devices: 32.2 us -> 29.1 us
    ppermute x2, waiting for transfers between devices: 15.6 us -> 10.9 us  [coil_sum(): hop = lax.ppermute(forwards[q], ('coil', 'slab'), pairs)]
    ppermute x2, waiting for transfers between devices: 12.6 us -> 14.4 us  [coil_sum(): hop = lax.ppermute(hop, ('coil', 'slab'), pairs)]
    dot_general x1 -> x2, matrix products: 3.9 us -> 3.78 us  [body(): jnp.dot(hop, transform, preferred_element_type=jnp.float32)]
  transfers between devices with their start and end apart: 8 -> 8, of which waited for: 6 -> 6; matrix products, arithmetic and copies ran while one was open for 18% -> 22% of each run, Pallas kernels for 0% -> 0%
where the time goes in v12:
time: 94.5 us; the launch traced here: 93.2 us
  waiting for transfers between devices  29.1 us (31%)
  matrix products  22.2 us (23%)
  other arithmetic  19.6 us (21%)
  Pallas kernels  11.8 us (12%)
  local copies, waits for them, and re-layouts  5.76 us (6%)
  starting transfers between devices  4.56 us (5%)
    ppermute x2, waiting for transfers between devices, coil_sum(): hop = lax.ppermute(hop, ('coil', 'slab'), pairs)  14.4 us
    pallas_call x4, Pallas kernels, factor_solve(): pl.pallas_call(factor_solve_kernel, out_shape=jax.ShapeDtypeStruct(rhs.sh...  11.8 us
    ppermute x2, waiting for transfers between devices, coil_sum(): hop = lax.ppermute(forwards[q], ('coil', 'slab'), pairs)  10.9 us
    another operation x2, other arithmetic  10.1 us
    reshape x2, local copies, waits for them, and re-layouts, pick(): return block.reshape(source.shape[3:])  5.39 us
    dot_general x4, matrix products, denoise_batch(): pushed = jnp.einsum('bkv,bvw->bkw', coeff, kernel, precision=HI)  4.28 us
    ppermute x2, waiting for transfers between devices, coil_sum(): lax.ppermute(pick(partial_time, coil ^ 3, q), 'coil', chip_pair)  3.86 us
    dot_general x2, matrix products, body(): jnp.dot(hop, transform, preferred_element_type=jnp.float32)  3.78 us
  transfers between devices with their start and end apart: 8, of which 6 were waited for; matrix products, arithmetic and copies ran while one was open for 22% of the time, Pallas kernels for 0%

profile of v12, /device:TPU:64, one launch (start us, length us, event | category | flops | bytes accessed | tf_op | source)
XLA Modules:
  0.0 93.2 jit_solution(10130731578186816883)
XLA Ops:
  0.0 2.7 %dynamic-slice_bitcast_fusion.2 = (bf16[512,1024]{1,0:T(8,128)(2,1)S(1)}, bf16[512,1024]{1,0:T(8,128)(2,1)}) fusion(bf16[1,4,2,512,1024]{4,3,2,1,0:T(8,128)(2,1)} %param.4, s32[]{:T(128)S(6)} %select_n.42), kind=kLoop, calls=%fused_computation.40 | loop fusion | bytes 4194308 | tf_op jit(solution)/shard_map/reshape | solution.py:92
  2.7 0.5 collective-permute-start.1
  3.2 2.4 %collective-permute-done = bf16[512,1024]{1,0:T(8,128)(2,1)S(1)} collective-permute-done((bf16[512,1024]{1,0:T(8,128)(2,1)}, bf16[512,1024]{1,0:T(8,128)(2,1)S(1)}, u32[]{:S(2)}, u32[]{:S(2)}) %collective-permute-start) | collective-permute-done | bytes 1048608 | tf_op jit(solution)/shard_map/ppermute | solution.py:96
  5.6 1.5 %collective-permute-done.1 = bf16[512,1024]{1,0:T(8,128)(2,1)S(1)} collective-permute-done((bf16[512,1024]{1,0:T(8,128)(2,1)S(1)}, bf16[512,1024]{1,0:T(8,128)(2,1)S(1)}, u32[]{:S(2)}, u32[]{:S(2)}) %collective-permute-start.1) | collective-permute-done | bytes 1048608 | tf_op jit(solution)/shard_map/ppermute | solution.py:96
  7.1 3.5 %fusion.13 = (bf16[512,1024]{1,0:T(8,128)(2,1)S(1)}, bf16[512,1024]{1,0:T(8,128)(2,1)}) fusion(bf16[512,1024]{1,0:T(8,128)(2,1)S(1)} %collective-permute-done.1, bf16[1,4,2,512,1024]{4,3,2,1,0:T(8,128)(2,1)} %param.4, s32[]{:T(128)S(6)} %select_n.41, bf16[512,1024]{1,0:T(8,128)(2,1)S(1)} %collective-permute-done), kind=kLoop, calls=%fused_computation.20 | loop fusion | flops 4194304 | bytes 6291460 | tf_op jit(solution)/shard_map/convert_element_type | solution.py:98
  10.6 1.5 %collective-permute-start.4 = (bf16[512,1024]{1,0:T(8,128)(2,1)}, bf16[512,1024]{1,0:T(8,128)(2,1)}, u32[]{:S(2)}, u32[]{:S(2)}) collective-permute-start(bf16[512,1024]{1,0:T(8,128)(2,1)} %get-tuple-element.9), channel_id=1, source_target_pairs={{0,1},{1,128},{2,3},{3,130},{4,5},{5,132},{6,7},{7,134},{8,9},{9,1... | collective-permute-start | bytes 3145736 | tf_op jit(solution)/shard_map/ppermute | solution.py:102
  12.1 1.5 %collective-permute-start.6 = (bf16[512,1024]{1,0:T(8,128)(2,1)S(1)}, bf16[512,1024]{1,0:T(8,128)(2,1)}, u32[]{:S(2)}, u32[]{:S(2)}) collective-permute-start(bf16[512,1024]{1,0:T(8,128)(2,1)S(1)} %get-tuple-element.10), channel_id=1, source_target_pairs={{0,1},{1,128},{2,3},{3,130},{4,5},{5,132},{6,7},{7,134},{8,9},{9,1... | collective-permute-start | bytes 3145736 | tf_op jit(solution)/shard_map/ppermute | solution.py:102
  13.5 2.7 %dynamic-slice_bitcast_fusion.1 = (bf16[512,1024]{1,0:T(8,128)(2,1)}, bf16[512,1024]{1,0:T(8,128)(2,1)S(1)}) fusion(bf16[1,4,2,512,1024]{4,3,2,1,0:T(8,128)(2,1)} %param.4, s32[]{:T(128)S(6)} %select_n.44), kind=kLoop, calls=%fused_computation.39 | loop fusion | bytes 4194308 | tf_op jit(solution)/shard_map/reshape | solution.py:92
  16.2 0.2 collective-permute-start.2
  16.4 0.3 collective-permute-start.3
  16.7 5.4 %negate_convert_fusion = (bf16[512,512]{1,0:T(8,128)(2,1)}, bf16[512,512]{1,0:T(8,128)(2,1)}) fusion(), kind=kLoop, calls=%fused_computation.33 | loop fusion | flops 4980736 | bytes 1048576 | tf_op jit(solution)/shard_map/convert.9
  22.2 4.7 %collective-permute-done.4 = bf16[512,1024]{1,0:T(8,128)(2,1)} collective-permute-done((bf16[512,1024]{1,0:T(8,128)(2,1)}, bf16[512,1024]{1,0:T(8,128)(2,1)}, u32[]{:S(2)}, u32[]{:S(2)}) %collective-permute-start.4) | collective-permute-done | bytes 1048608 | tf_op jit(solution)/shard_map/ppermute | solution.py:102
  26.9 0.3 collective-permute-start.5
  27.2 4.7 %fusion.24 = bf16[512,512]{1,0:T(8,128)(2,1)} fusion(), kind=kLoop, calls=%fused_computation.43 | loop fusion | flops 4194304 | bytes 524288 | tf_op jit(solution)/shard_map/convert.6
  31.8 0.1 iota_compare_fusion
  31.9 6.2 %collective-permute-done.6 = bf16[512,1024]{1,0:T(8,128)(2,1)} collective-permute-done((bf16[512,1024]{1,0:T(8,128)(2,1)S(1)}, bf16[512,1024]{1,0:T(8,128)(2,1)}, u32[]{:S(2)}, u32[]{:S(2)}) %collective-permute-start.6) | collective-permute-done | bytes 1048608 | tf_op jit(solution)/shard_map/ppermute | solution.py:102
  38.1 0.3 collective-permute-start.7
  38.4 2.8 %fusion.19 = (bf16[1,512,1024]{2,1,0:T(8,128)(2,1)S(1)}, bf16[1,512,1024]{2,1,0:T(8,128)(2,1)S(1)}) fusion(bf16[512,1024]{1,0:T(8,128)(2,1)S(1)} %collective-permute-done.2, bf16[1,4,2,512,1024]{4,3,2,1,0:T(8,128)(2,1)} %param.4, s32[]{:T(128)S(6)} %select_n.43, bf16[512,1024]{1,0:T(8,128)(2,1)} %collective-permute-done.3), kind=kLoop, calls=%fused_computation.31 | loop fusion | flops 4194304 | bytes 6291460 | tf_op jit(solution)/shard_map/stack | solution.py:115
  41.3 2.3 %fusion.7 = f32[2,512,1024]{2,1,0:T(8,128)S(1)} fusion(bf16[1,512,1024]{2,1,0:T(8,128)(2,1)S(1)} %get-tuple-element.12, bf16[1,512,1024]{2,1,0:T(8,128)(2,1)S(1)} %get-tuple-element.11, bf16[512,512]{1,0:T(8,128)(2,1)S(1)} %copy-done.10, bf16[512,512]{1,0:T(8,128)(2,1)S(1)} %copy-done.11, bf16[512,512]{1,0:T(8,128)(2,1)S(1)} %copy-done.9), kind=kOutput, calls=%fused_computation.10 | convolution fusion | flops 2156920832 | bytes 7864320 | tf_op jit(solution)/shard_map/bvt,tf->bvf/dot_general | solution.py:116
  43.6 5.8 %collective-permute-done.5 = bf16[512,1024]{1,0:T(8,128)(2,1)} collective-permute-done((bf16[512,1024]{1,0:T(8,128)(2,1)}, bf16[512,1024]{1,0:T(8,128)(2,1)}, u32[]{:S(2)}, u32[]{:S(2)}) %collective-permute-start.5) | collective-permute-done | bytes 1048608 | tf_op jit(solution)/shard_map/ppermute | solution.py:103
  49.4 2.5 %fusion.6 = f32[1,512,1024]{2,1,0:T(8,128)S(1)} fusion(f32[2,512,1024]{2,1,0:T(8,128)S(1)} %fusion.7, bf16[512,1024]{1,0:T(8,128)(2,1)} %collective-permute-done.5, bf16[512,512]{1,0:T(8,128)(2,1)S(1)} %copy-done.10, bf16[512,512]{1,0:T(8,128)(2,1)S(1)} %copy-done.11, bf16[512,512]{1,0:T(8,128)(2,1)S(1)} %copy-done.9), kind=kOutput, calls=%fused_computation.9 | convolution fusion | flops 1082654720 | bytes 6815744 | tf_op jit(solution)/shard_map/dot_general | solution.py:118
  51.9 8.6 %collective-permute-done.7 = bf16[512,1024]{1,0:T(8,128)(2,1)S(1)} collective-permute-done((bf16[512,1024]{1,0:T(8,128)(2,1)}, bf16[512,1024]{1,0:T(8,128)(2,1)S(1)}, u32[]{:S(2)}, u32[]{:S(2)}) %collective-permute-start.7) | collective-permute-done | bytes 1048608 | tf_op jit(solution)/shard_map/ppermute | solution.py:103
  60.5 1.3 %fusion.4 = f32[1,512,1024]{2,1,0:T(8,128)S(1)} fusion(f32[2,512,1024]{2,1,0:T(8,128)S(1)} %fusion.7, bf16[512,1024]{1,0:T(8,128)(2,1)S(1)} %collective-permute-done.7, bf16[512,512]{1,0:T(8,128)(2,1)S(1)} %copy-done.10, bf16[512,512]{1,0:T(8,128)(2,1)S(1)} %copy-done.11, bf16[512,512]{1,0:T(8,128)(2,1)S(1)} %copy-done.9), kind=kOutput, calls=%fused_computation.6 | convolution fusion | flops 1082654720 | bytes 6815744 | tf_op jit(solution)/shard_map/dot_general | solution.py:118
  61.8 3.7 %fusion.1 = f32[2,512,512]{2,1,0:T(8,128)S(1)} fusion(f32[1,512,1024]{2,1,0:T(8,128)S(1)} %fusion.4, f32[1,512,1024]{2,1,0:T(8,128)S(1)} %fusion.6), kind=kOutput, calls=%fused_computation.2 | convolution fusion | flops 3222274048 | bytes 6291456 | tf_op jit(solution)/shard_map/bvf,bwf->bvw/dot_general | solution.py:49
  65.5 1.7 %fusion.2 = f32[2,512,16]{1,2,0:T(8,128)S(1)} fusion(f32[1,512,1024]{2,1,0:T(8,128)S(1)} %fusion.4, f32[1,512,1024]{2,1,0:T(8,128)S(1)} %fusion.6, f32[16,1024]{1,0:T(8,128)S(1)} %copy-done), kind=kOutput, calls=%fused_computation.3 | convolution fusion | flops 101711872 | bytes 4325376 | tf_op jit(solution)/shard_map/kf,bvf->bkv/dot_general | solution.py:50
  67.2 0.6 fusion.39.rhs_ref
  67.8 0.2 fusion.40
  68.0 0.1 copy.5
  68.1 0.6 fusion.33.gram_ref
  68.7 2.9 %shard_map.46 = f32[2,16,512]{2,1,0:T(8,128)} custom-call(f32[2,16,16]{2,1,0:T(8,128)} %fusion.33.gram_ref, f32[2,16,512]{2,1,0:T(8,128)} %copy-done.4), custom_call_target="tpu_custom_call" | custom-call | tf_op jit(solution)/shard_map/pallas_call | solution.py:42
  71.6 1.5 %fusion.41.rhs_ref = f32[2,16,512]{2,1,0:T(8,128)S(1)} fusion(f32[2,16,512]{2,1,0:T(8,128)} %shard_map.46, f32[2,512,512]{2,1,0:T(8,128)S(1)} %fusion.1), kind=kOutput, calls=%fused_computation.69 | convolution fusion | flops 50331648 | bytes 2228224 | tf_op jit(solution)/shard_map/bkv,bvw->bkw/dot_general | solution.py:52
  73.1 0.2 fusion.42
  73.3 0.1 copy.6
  73.4 0.6 fusion.32.gram_ref
  74.0 2.9 %shard_map.47 = f32[2,16,512]{2,1,0:T(8,128)} custom-call(f32[2,16,16]{2,1,0:T(8,128)} %fusion.32.gram_ref, f32[2,16,512]{2,1,0:T(8,128)} %copy-done.5), custom_call_target="tpu_custom_call" | custom-call | tf_op jit(solution)/shard_map/pallas_call | solution.py:42
  76.9 1.5 %fusion.43.rhs_ref = f32[2,16,512]{2,1,0:T(8,128)S(1)} fusion(f32[2,16,512]{2,1,0:T(8,128)} %shard_map.47, f32[2,512,512]{2,1,0:T(8,128)S(1)} %fusion.1), kind=kOutput, calls=%fused_computation.71 | convolution fusion | flops 50331648 | bytes 2228224 | tf_op jit(solution)/shard_map/bkv,bvw->bkw/dot_general | solution.py:52
  78.4 0.2 fusion.44
  78.6 0.1 copy.7
  78.6 0.6 fusion.31.gram_ref
  79.3 2.9 %shard_map.48 = f32[2,16,512]{2,1,0:T(8,128)} custom-call(f32[2,16,16]{2,1,0:T(8,128)} %fusion.31.gram_ref, f32[2,16,512]{2,1,0:T(8,128)} %copy-done.6), custom_call_target="tpu_custom_call" | custom-call | tf_op jit(solution)/shard_map/pallas_call | solution.py:42
  82.2 2.7 %fusion = f32[2,16,1024]{2,1,0:T(8,128)S(1)} fusion(f32[2,16,512]{2,1,0:T(8,128)} %shard_map.48, f32[1,512,1024]{2,1,0:T(8,128)} %copy-done.2, f32[1,512,1024]{2,1,0:T(8,128)} %copy-done.1), kind=kOutput, calls=%fused_computation.1 | convolution fusion | flops 34603008 | bytes 4390912 | tf_op jit(solution)/shard_map/bkv,bvf->bkf/dot_general | solution.py:57
  84.8 0.6 fusion.45
  85.5 0.2 fusion.46
  85.6 0.7 pad_maximum_fusion.4.rhs_ref
  86.3 0.1 copy.8
  86.4 0.6 fusion.30.gram_ref
  87.0 3.1 %shard_map.49 = f32[2,16,1536]{2,1,0:T(8,128)} custom-call(f32[2,16,16]{2,1,0:T(8,128)} %fusion.30.gram_ref, f32[2,16,1536]{2,1,0:T(8,128)} %pad_maximum_fusion.4.rhs_ref), custom_call_target="tpu_custom_call" | custom-call | tf_op jit(solution)/shard_map/pallas_call | solution.py:42
  90.1 3.1 %convert_select_fusion = bf16[2,512,1024]{2,1,0:T(8,128)(2,1)} fusion(pred[2]{0:T(512)(128)(4,1)S(1)} %broadcast_compare_fusion, f32[2,16,1536]{2,1,0:T(8,128)} %shard_map.49, pred[2,16]{1,0:T(4,128)(4,1)S(1)} %iota_compare_fusion), kind=kOutput, calls=%fused_computation.24 | convolution fusion | flops 34652160 | bytes 2196992 | tf_op jit(solution)/shard_map/bkv,bkf->bvf/dot_general | solution.py:64
  (32 shorter events, 0.1 us)
Async XLA Ops:
  0.0 65.5 %copy-start = (f32[16,1024]{1,0:T(8,128)S(1)}, f32[16,1024]{1,0:T(8,128)}, u32[]{:S(2)}) copy-start(f32[16,1024]{1,0:T(8,128)} %param.7) | copy-start | bytes 196612
  2.7 2.9 %collective-permute-start = (bf16[512,1024]{1,0:T(8,128)(2,1)}, bf16[512,1024]{1,0:T(8,128)(2,1)S(1)}, u32[]{:S(2)}, u32[]{:S(2)}) collective-permute-start(bf16[512,1024]{1,0:T(8,128)(2,1)} %get-tuple-element.18), channel_id=1, source_target_pairs={{0,64},{64,0},{128,192},{192,128},{1,65},{65,1},{129,193},{193,129... | collective-permute-start | bytes 3145736 | tf_op jit(solution)/shard_map/ppermute | solution.py:96
  2.7 4.4 %collective-permute-start.1 = (bf16[512,1024]{1,0:T(8,128)(2,1)S(1)}, bf16[512,1024]{1,0:T(8,128)(2,1)S(1)}, u32[]{:S(2)}, u32[]{:S(2)}) collective-permute-start(bf16[512,1024]{1,0:T(8,128)(2,1)S(1)} %get-tuple-element.17), channel_id=1, source_target_pairs={{0,64},{64,0},{128,192},{192,128},{1,65},{65,1},{129,193},{193,129... | collective-permute-start | bytes 3145736 | tf_op jit(solution)/shard_map/ppermute | solution.py:96
  10.6 16.3 %collective-permute-start.4 = (bf16[512,1024]{1,0:T(8,128)(2,1)}, bf16[512,1024]{1,0:T(8,128)(2,1)}, u32[]{:S(2)}, u32[]{:S(2)}) collective-permute-start(bf16[512,1024]{1,0:T(8,128)(2,1)} %get-tuple-element.9), channel_id=1, source_target_pairs={{0,1},{1,128},{2,3},{3,130},{4,5},{5,132},{6,7},{7,134},{8,9},{9,1... | collective-permute-start | bytes 3145736 | tf_op jit(solution)/shard_map/ppermute | solution.py:102
  12.0 10.1 %copy-start.12 = (s32[2]{0:T(128)S(1)}, s32[2]{0:T(128)}, u32[]{:S(2)}) copy-start(s32[2]{0:T(128)} %param.5) | copy-start | bytes 28
  12.1 19.8 %copy-start.13 = (s32[2]{0:T(128)S(1)}, s32[2]{0:T(128)}, u32[]{:S(2)}) copy-start(s32[2]{0:T(128)} %param.6) | copy-start | bytes 28
  12.1 26.1 %collective-permute-start.6 = (bf16[512,1024]{1,0:T(8,128)(2,1)S(1)}, bf16[512,1024]{1,0:T(8,128)(2,1)}, u32[]{:S(2)}, u32[]{:S(2)}) collective-permute-start(bf16[512,1024]{1,0:T(8,128)(2,1)S(1)} %get-tuple-element.10), channel_id=1, source_target_pairs={{0,1},{1,128},{2,3},{3,130},{4,5},{5,132},{6,7},{7,134},{8,9},{9,1... | collective-permute-start | bytes 3145736 | tf_op jit(solution)/shard_map/ppermute | solution.py:102
  16.2 22.2 %collective-permute-start.2 = (bf16[512,1024]{1,0:T(8,128)(2,1)}, bf16[512,1024]{1,0:T(8,128)(2,1)S(1)}, u32[]{:S(2)}, u32[]{:S(2)}) collective-permute-start(bf16[512,1024]{1,0:T(8,128)(2,1)} %get-tuple-element.13), channel_id=1, source_target_pairs={{0,64},{64,0},{128,192},{192,128},{1,65},{65,1},{129,193},{193,129... | collective-permute-start | bytes 3145736 | tf_op jit(solution)/shard_map/ppermute | solution.py:104
  16.4 22.0 %collective-permute-start.3 = (bf16[512,1024]{1,0:T(8,128)(2,1)S(1)}, bf16[512,1024]{1,0:T(8,128)(2,1)}, u32[]{:S(2)}, u32[]{:S(2)}) collective-permute-start(bf16[512,1024]{1,0:T(8,128)(2,1)S(1)} %get-tuple-element.14), channel_id=1, source_target_pairs={{0,64},{64,0},{128,192},{192,128},{1,65},{65,1},{129,193},{193,129... | collective-permute-start | bytes 3145736 | tf_op jit(solution)/shard_map/ppermute | solution.py:104
  26.9 22.5 %collective-permute-start.5 = (bf16[512,1024]{1,0:T(8,128)(2,1)}, bf16[512,1024]{1,0:T(8,128)(2,1)}, u32[]{:S(2)}, u32[]{:S(2)}) collective-permute-start(bf16[512,1024]{1,0:T(8,128)(2,1)} %collective-permute-done.4), channel_id=1, source_target_pairs={{0,1},{1,128},{2,3},{3,130},{4,5},{5,132},{6,7},{7,134},{8,9},{9,1... | collective-permute-start | bytes 3145736 | tf_op jit(solution)/shard_map/ppermute | solution.py:103
  31.9 9.3 %copy-start.9 = (bf16[512,512]{1,0:T(8,128)(2,1)S(1)}, bf16[512,512]{1,0:T(8,128)(2,1)}, u32[]{:S(2)}) copy-start(bf16[512,512]{1,0:T(8,128)(2,1)} %get-tuple-element.19) | copy-start | bytes 1572868
  31.9 9.3 %copy-start.10 = (bf16[512,512]{1,0:T(8,128)(2,1)S(1)}, bf16[512,512]{1,0:T(8,128)(2,1)}, u32[]{:S(2)}) copy-start(bf16[512,512]{1,0:T(8,128)(2,1)} %get-tuple-element.20) | copy-start | bytes 1572868
  31.9 9.3 %copy-start.11 = (bf16[512,512]{1,0:T(8,128)(2,1)S(1)}, bf16[512,512]{1,0:T(8,128)(2,1)}, u32[]{:S(2)}) copy-start(bf16[512,512]{1,0:T(8,128)(2,1)} %fusion.24) | copy-start | bytes 1572868
  38.1 22.4 %collective-permute-start.7 = (bf16[512,1024]{1,0:T(8,128)(2,1)}, bf16[512,1024]{1,0:T(8,128)(2,1)S(1)}, u32[]{:S(2)}, u32[]{:S(2)}) collective-permute-start(bf16[512,1024]{1,0:T(8,128)(2,1)} %collective-permute-done.6), channel_id=1, source_target_pairs={{0,1},{1,128},{2,3},{3,130},{4,5},{5,132},{6,7},{7,134},{8,9},{9,1... | collective-permute-start | bytes 3145736 | tf_op jit(solution)/shard_map/ppermute | solution.py:103
  51.9 13.6 %copy-start.1 = (f32[1,512,1024]{2,1,0:T(8,128)}, f32[1,512,1024]{2,1,0:T(8,128)S(1)}, u32[]{:S(2)}) copy-start(f32[1,512,1024]{2,1,0:T(8,128)S(1)} %fusion.6) | copy-start | bytes 6291460
  61.8 3.7 %copy-start.2 = (f32[1,512,1024]{2,1,0:T(8,128)}, f32[1,512,1024]{2,1,0:T(8,128)S(1)}, u32[]{:S(2)}) copy-start(f32[1,512,1024]{2,1,0:T(8,128)S(1)} %fusion.4) | copy-start | bytes 6291460
  67.8 0.9 copy-start.4
  71.6 1.5 %copy-start.7 = (f32[2,16,512]{2,1,0:T(8,128)S(1)}, f32[2,16,512]{2,1,0:T(8,128)}, u32[]{:S(2)}) copy-start(f32[2,16,512]{2,1,0:T(8,128)} %shard_map.46) | copy-start | bytes 196612
  73.1 0.9 copy-start.5
  76.9 1.5 %copy-start.8 = (f32[2,16,512]{2,1,0:T(8,128)S(1)}, f32[2,16,512]{2,1,0:T(8,128)}, u32[]{:S(2)}) copy-start(f32[2,16,512]{2,1,0:T(8,128)} %shard_map.47) | copy-start | bytes 196612
  78.4 0.9 copy-start.6
  82.2 2.7 %copy-start.3 = (f32[2,16,512]{2,1,0:T(8,128)S(1)}, f32[2,16,512]{2,1,0:T(8,128)}, u32[]{:S(2)}) copy-start(f32[2,16,512]{2,1,0:T(8,128)} %shard_map.48) | copy-start | bytes 196612
